TPU v7x, 256 devices: a whole 4x4x8 slice. The times are simulated.
256 devices in a mesh: shard: 64 (over y, z, core), cent: 4 (over x).
Axes of the slice: x: 4, y: 4, z: 8, core: 2. Of those that a mesh axis runs over, the one named last changes fastest.
Arguments:
- queries: bfloat16 [1024, 32, 128], P('shard'), may hold values from -6 to 6
- centroids: bfloat16 [196608, 128], P(('shard', 'cent')), may hold values from -0.5 to 0.5
- passages: bfloat16 [16384, 128, 128], P('shard', 'cent'), may hold values from -0.5 to 0.5
- lengths: int32 [16384], P('shard'), may hold values from 16 to 128, as said below
- passage_row: int32 [16384], replicated, may hold values from 0 to 16383, as said below
- candidates: int32 [1024, 16], P('shard'), may hold values from 0 to 16383, as said below
Outputs:
- token_best: float32 [1024, 32], P('shard')
- scores: float32 [1024, 16], P('shard')
Inputs may be any that keep to these rules, and one draw needn't show every extreme that they name: A permutation: passage g is stored at row passage_row[g]. The rows j < lengths[r] of stored passage r are real, the rest padding; the first stored passage of every index of shard has all 128. Among the 256 pairs of the queries of one index of shard, at most 12 have candidates stored at one owner (owner = passage_row[id] // 256); one owner takes exactly 12 pairs from every index of shard.
All inputs are finite; a program needn't handle non-finite values.
Results may differ from a plain program's by a relative error of at most 0.0003.
Values may be sent and summed in bfloat16 or wider, within the bound.
No kernel may reach another device: no remote copies, remote signals or barrier semaphores. Data moves between devices by JAX's collectives and lax.ppermute only.
A program may use at most 128 MiB of HBM per device.

v0:
```python
import jax
import jax.numpy as jnp
from jax import lax
from jax.sharding import PartitionSpec as P

masked_score = -1e30


def per_device(queries, centroids, passages, lengths, passage_row, candidates):
    query_count = queries.shape[0]
    query_tokens = queries.shape[1]
    feature_width = queries.shape[2]
    per_query = candidates.shape[1]
    passage_count = passages.shape[0]
    token_rows = passages.shape[1]
    shard_total = lax.axis_size("shard")
    capacity = max(2, 3 * query_count * per_query // shard_total)
    my_shard = lax.axis_index("shard")
    query_block = lax.all_gather(queries, "shard", axis=0, tiled=True)
    flattened = query_block.reshape(-1, feature_width)
    scored = jnp.einsum("rd,cd->rc", flattened, centroids, preferred_element_type=jnp.float32)
    local_best = jnp.max(scored, axis=1).reshape(query_block.shape[0], query_tokens)
    merged = lax.pmax(local_best, ("shard", "cent"))
    token_best = lax.dynamic_slice_in_dim(merged, my_shard * query_count, query_count, 0)
    pair_rows = jnp.take(passage_row, candidates.reshape(-1), axis=0)
    owners = pair_rows // passage_count
    slot_ids = pair_rows % passage_count
    onehot = (owners[:, None] == jnp.arange(shard_total, dtype=jnp.int32)[None, :]).astype(
        jnp.int32
    )
    ranking = jnp.sum((jnp.cumsum(onehot, axis=0) - onehot) * onehot, axis=1)
    places = owners * capacity + ranking
    pair_query = jnp.arange(query_count * per_query, dtype=jnp.int32) // per_query
    slot_table = (
        jnp.full((shard_total * capacity,), -1, jnp.int32)
        .at[places]
        .set(slot_ids)
        .reshape(shard_total, capacity)
    )
    token_index = lax.axis_index("cent") * token_rows + jnp.arange(token_rows, dtype=jnp.int32)
    flat_queries = queries.reshape(query_count, query_tokens * feature_width)
    token_table = jnp.zeros((shard_total * capacity, query_tokens * feature_width), jnp.bfloat16)
    token_table = token_table.at[places].set(jnp.take(flat_queries, pair_query, axis=0))
    token_table = token_table.reshape(shard_total, capacity, query_tokens * feature_width)
    slot_block = lax.all_to_all(slot_table, "shard", split_axis=0, concat_axis=0, tiled=True)
    safe_slots = jnp.maximum(slot_block, 0).reshape(-1)
    chosen = jnp.take(passages, safe_slots, axis=0)
    asked = lax.all_to_all(token_table, "shard", split_axis=0, concat_axis=0, tiled=True).reshape(
        -1, query_tokens, feature_width
    )
    scored = jnp.einsum("ntd,npd->ntp", asked, chosen, preferred_element_type=jnp.float32)
    valid_tokens = token_index[None, :] < jnp.take(lengths, safe_slots, axis=0)[:, None]
    scored = jnp.where(valid_tokens[:, None, :], scored, masked_score)
    partial_value = jnp.max(scored, axis=2).reshape(
        slot_block.shape[0], slot_block.shape[1], query_tokens
    )
    complete = lax.pmax(partial_value, "cent")
    pair_scores = jnp.sum(complete, axis=2) / query_tokens
    returned = lax.all_to_all(pair_scores, "shard", split_axis=0, concat_axis=0, tiled=True)
    scores = jnp.take(returned.reshape(-1), places, axis=0).reshape(query_count, per_query)
    return (token_best, scores)


def solution(mesh):
    in_specs = (
        P("shard", None, None),
        P(("shard", "cent"), None),
        P("shard", "cent", None),
        P("shard"),
        P(),
        P("shard", None),
    )
    out_specs = (P("shard", None), P("shard", None))
    return jax.shard_map(
        per_device, mesh=mesh, in_specs=in_specs, out_specs=out_specs, check_vma=False
    )
```

profile of v0, /device:TPU:1, one launch (start us, length us, event | category | flops | bytes accessed | tf_op | source)
XLA Modules:
  0.0 632.4 jit_solution(10304121452053333185)
XLA Ops:
  8.0 0.9 reshape.321
  10.5 2.1 gather_fusion
  13.6 1.4 scatter_custom_fusion
  15.7 13.2 %all-to-all-start = ((s32[64,1,12]{2,1,0:T(1,128)}), s32[64,1,12]{2,1,0:T(1,128)S(1)}, u32[]{:S(2)}, u32[]{:S(2)}) async-start(s32[64,1,12]{2,1,0:T(1,128)} %bitcast.7), calls=%async_computation | async-start | bytes 65536 | tf_op jit(solution)/shard_map/all_to_all | solution.py:45
  28.9 1.0 copy.15
  29.9 13.4 %scatter_custom_fusion.1 = bf16[768,4096]{1,0:T(8,128)(2,1)} fusion(s32[256]{0:T(256)S(1)} %bitcast.44, bf16[]{:T(256)} %constant.143.clone.1, pred[256]{0:T(512)(128)(4,1)S(1)} %compare_and_fusion, bf16[]{:T(256)} %constant.146.clone.1, bf16[16,4096]{1,0:T(8,128)(2,1)S(1)} %bitcast.38, s32[1024]{0:T(1024)S(1)} %pad_clamp_fusion.1), kind=kCustom, calls=%fused_computation.13 | custom fusion | flops 1048576 | bytes 6427140 | tf_op jit(solution)/shard_map/scatter | solution.py:43
  43.3 9.8 %reshape.326 = bf16[64,12,4096]{2,1,0:T(8,128)(2,1)} reshape(bf16[768,4096]{1,0:T(8,128)(2,1)} %scatter_custom_fusion.1) | data formatting | bytes 12582912 | tf_op jit(solution)/shard_map/reshape | solution.py:44
  53.1 10.6 %all-to-all-start.1 = ((bf16[64,12,4096]{2,1,0:T(8,128)(2,1)}), bf16[64,12,4096]{2,1,0:T(8,128)(2,1)}, u32[]{:S(2)}, u32[]{:S(2)}) async-start(bf16[64,12,4096]{2,1,0:T(8,128)(2,1)} %reshape.326), calls=%async_computation.1 | async-start | bytes 16777216 | tf_op jit(solution)/shard_map/all_to_all | solution.py:48
  64.3 5.0 gather_fusion.1
  69.3 4.4 gather_fusion.2
  73.9 175.6 %all-to-all-done.1 = bf16[64,12,4096]{2,1,0:T(8,128)(2,1)} async-done(((bf16[64,12,4096]{2,1,0:T(8,128)(2,1)}), bf16[64,12,4096]{2,1,0:T(8,128)(2,1)}, u32[]{:S(2)}, u32[]{:S(2)}) %all-to-all-start.1) | async-done | bytes 6291488 | tf_op jit(solution)/shard_map/all_to_all | solution.py:48
  249.5 12.2 %reshape.327 = bf16[768,32,128]{2,1,0:T(8,128)(2,1)} reshape(bf16[64,12,4096]{2,1,0:T(8,128)(2,1)} %all-to-all-done.1) | data formatting | bytes 12582912 | tf_op jit(solution)/shard_map/reshape | solution.py:48
  261.7 9.2 %select_reduce_fusion = f32[768,32]{1,0:T(8,128)S(1)} fusion(pred[768,32]{1,0:T(8,128)(4,1)S(1)} %broadcast_compare_fusion, bf16[768,32,128]{2,1,0:T(8,128)(2,1)} %reshape.327, bf16[768,32,128]{2,1,0:T(8,128)(2,1)} %gather_fusion.2, pred[768]{0:T(1024)(128)(4,1)S(1)} %le.92), kind=kOutput, calls=%fused_computation.8 | convolution fusion | flops 206020608 | bytes 12706560 | tf_op jit(solution)/shard_map/ntd,npd->ntp/dot_general | solution.py:51
  270.8 0.9 reshape.328
  272.3 42.1 %all-reduce.5.cloned.1.call-done = f32[64,12,32]{2,1,0:T(8,128)} async-done(((f32[64,12,32]{2,1,0:T(8,128)}), f32[64,12,32]{2,1,0:T(8,128)}) %all-reduce.5.cloned.1.call-update) | async-done | bytes 98320 | tf_op jit(solution)/shard_map/pmax | solution.py:57
  314.4 1.3 reduce_sum.25
  316.3 12.8 %all-to-all-start.2 = ((f32[64,1,12]{2,1,0:T(1,128)}), f32[64,1,12]{2,1,0:T(1,128)S(1)}, u32[]{:S(2)}, u32[]{:S(2)}) async-start(f32[64,1,12]{2,1,0:T(1,128)} %bitcast.9), calls=%async_computation.2 | async-start | bytes 65536 | tf_op jit(solution)/shard_map/all_to_all | solution.py:59
  329.6 8.9 %all-to-all-done.2 = f32[64,1,12]{2,1,0:T(1,128)S(1)} async-done(((f32[64,1,12]{2,1,0:T(1,128)}), f32[64,1,12]{2,1,0:T(1,128)S(1)}, u32[]{:S(2)}, u32[]{:S(2)}) %all-to-all-start.2) | async-done | bytes 3104 | tf_op jit(solution)/shard_map/all_to_all | solution.py:59
  339.9 1.4 gather_fusion.3
  341.3 14.3 %all-gather.2.cloned.1.call-done = bf16[1024,32,128]{2,1,0:T(8,128)(2,1)} async-done(((bf16[16,32,128]{2,1,0:T(8,128)(2,1)}), bf16[1024,32,128]{2,1,0:T(8,128)(2,1)}) %all-gather.2.cloned.1.call-update) | async-done | bytes 8388624 | tf_op jit(solution)/shard_map/all_gather | solution.py:19
  355.6 17.0 %convolution_reduce_fusion = f32[32768]{0:T(1024)S(1)} fusion(bf16[32768,128]{1,0:T(8,128)(2,1)} %bitcast.47, bf16[768,128]{1,0:T(8,128)(2,1)S(1)} %copy-done.3), kind=kOutput, calls=%fused_computation.7 | convolution fusion | flops 6467584000 | bytes 8716288 | tf_op jit(solution)/shard_map/rd,cd->rc/dot_general | solution.py:21
  372.7 1.0 reshape.320
  374.3 249.3 %all-reduce.3.cloned.1.call-done = f32[1024,32]{1,0:T(8,128)} async-done(((f32[1024,32]{1,0:T(8,128)}), f32[1024,32]{1,0:T(8,128)}) %all-reduce.3.cloned.1.call-update) | async-done | bytes 131088 | tf_op jit(solution)/shard_map/pmax | solution.py:23
  623.6 1.3 constant_dynamic-slice_fusion
  (50 shorter events, 7.7 us)
Async XLA Ops:
  8.0 61.3 %copy-start = (bf16[256,32,128]{2,1,0:T(8,128)(2,1)S(1)}, bf16[256,32,128]{2,1,0:T(8,128)(2,1)}, u32[]{:S(2)}) copy-start(bf16[256,32,128]{2,1,0:T(8,128)(2,1)} %param.8) | copy-start | bytes 6291460
  15.7 37.4 %all-to-all-start = ((s32[64,1,12]{2,1,0:T(1,128)}), s32[64,1,12]{2,1,0:T(1,128)S(1)}, u32[]{:S(2)}, u32[]{:S(2)}) async-start(s32[64,1,12]{2,1,0:T(1,128)} %bitcast.7), calls=%async_computation | async-start | bytes 65536 | tf_op jit(solution)/shard_map/all_to_all | solution.py:45
  53.1 11.2 %copy-start.1 = (s32[256]{0:T(256)S(1)}, s32[256]{0:T(256)}, u32[]{:S(2)}) copy-start(s32[256]{0:T(256)} %param.9) | copy-start | bytes 3076
  53.1 196.4 %all-to-all-start.1 = ((bf16[64,12,4096]{2,1,0:T(8,128)(2,1)}), bf16[64,12,4096]{2,1,0:T(8,128)(2,1)}, u32[]{:S(2)}, u32[]{:S(2)}) async-start(bf16[64,12,4096]{2,1,0:T(8,128)(2,1)} %reshape.326), calls=%async_computation.1 | async-start | bytes 16777216 | tf_op jit(solution)/shard_map/all_to_all | solution.py:48
  63.8 250.7 %all-reduce.5.cloned.1.call-start = ((), (), s32[]{:S(2)}) async-start(), calls=%async_computation.5 | async-start | bytes 1048576 | tf_op jit(solution)/shard_map/pmax | solution.py:57
  261.7 94.0 %copy-start.3 = (bf16[768,128]{1,0:T(8,128)(2,1)S(1)}, bf16[768,128]{1,0:T(8,128)(2,1)}, u32[]{:S(2)}) copy-start(bf16[768,128]{1,0:T(8,128)(2,1)} %param.7) | copy-start | bytes 589828
  271.8 83.9 %all-gather.2.cloned.1.call-start = ((), (), s32[]{:S(2)}) async-start(), calls=%async_computation.3 | async-start | bytes 8519680 | tf_op jit(solution)/shard_map/all_gather | solution.py:19
  316.3 22.2 %all-to-all-start.2 = ((f32[64,1,12]{2,1,0:T(1,128)}), f32[64,1,12]{2,1,0:T(1,128)S(1)}, u32[]{:S(2)}, u32[]{:S(2)}) async-start(f32[64,1,12]{2,1,0:T(1,128)} %bitcast.9), calls=%async_computation.2 | async-start | bytes 65536 | tf_op jit(solution)/shard_map/all_to_all | solution.py:59
  329.1 294.5 %all-reduce.3.cloned.1.call-start = ((), (), s32[]{:S(2)}) async-start(), calls=%async_computation.4 | async-start | bytes 1048576 | tf_op jit(solution)/shard_map/pmax | solution.py:23
  355.6 18.1 %copy-start.2 = (s32[16,16]{1,0:T(8,128)S(1)}, s32[16,16]{1,0:T(8,128)}, u32[]{:S(2)}) copy-start(s32[16,16]{1,0:T(8,128)} %param.11) | copy-start | bytes 3076
Sparse Core Ops, SparseCore 0:
  271.9 42.4 all-reduce.4
Sparse Core Ops, SparseCore 1:
  275.0 80.6 all-gather.1
  373.8 249.8 all-reduce.2
where the time goes:
time: 634 us; the launch traced here: 632 us
  waiting for transfers between devices  491 us (77%)
  local copies, waits for them, and re-layouts  44.8 us (7%)
  starting transfers between devices  37 us (6%)
  matrix products  26.2 us (4%)
  other arithmetic  17.9 us (3%)
  between operations  15.7 us (2%)
    pmax x1, waiting for transfers between devices, per_device(): merged = lax.pmax(local_best, ('shard', 'cent'))  249 us
    all_to_all x1, waiting for transfers between devices, per_device(): lax.all_to_all(token_table, 'shard', split_axis=0, concat_axis=0, tiled=T...  176 us
    pmax x1, waiting for transfers between devices, per_device(): complete = lax.pmax(partial_value, 'cent')  42.1 us
    dot_general x1, matrix products, per_device(): jnp.einsum('rd,cd->rc', flattened, centroids, preferred_element_type=jnp....  17 us
    all_gather x1, waiting for transfers between devices, per_device(): query_block = lax.all_gather(queries, 'shard', axis=0, tiled=True)  14.3 us
    scatter x1, other arithmetic, per_device(): token_table.at[places].set(jnp.take(flat_queries, pair_query, axis=0))  13.4 us
    all_to_all x1, starting transfers between devices, per_device(): lax.all_to_all(slot_table, 'shard', split_axis=0, concat_axis=0, tiled=True)  13.2 us
    all_to_all x1, starting transfers between devices, per_device(): lax.all_to_all(pair_scores, 'shard', split_axis=0, concat_axis=0, tiled=T...  12.8 us
  transfers between devices with their start and end apart: 6, of which 5 were waited for; matrix products, arithmetic and copies ran while one was open for 6% of the time, Pallas kernels for 0%

commit v1 on v0

v1 whole, which is shorter than its diff:
```python
import jax
import jax.numpy as jnp
from jax import lax
from jax.sharding import PartitionSpec as P

masked_score = -1e30


def per_device(queries, centroids, passages, lengths, passage_row, candidates):
    query_count = queries.shape[0]
    query_tokens = queries.shape[1]
    feature_width = queries.shape[2]
    per_query = candidates.shape[1]
    passage_count = passages.shape[0]
    token_rows = passages.shape[1]
    shard_total = lax.axis_size("shard")
    capacity = max(2, 3 * query_count * per_query // shard_total)
    pairs_here = query_count * per_query
    my_shard = lax.axis_index("shard")

    query_block = lax.all_gather(queries, "shard", axis=0, tiled=True)
    cand_block = lax.all_gather(candidates, "shard", axis=0, tiled=True)

    flattened = query_block.reshape(-1, feature_width)
    scored = jnp.einsum("rd,cd->rc", flattened, centroids, preferred_element_type=jnp.float32)
    local_best = jnp.max(scored, axis=1).reshape(shard_total, query_count, query_tokens)
    gathered_best = lax.all_to_all(local_best, "shard", split_axis=0, concat_axis=0, tiled=True)
    shard_best = jnp.max(gathered_best, axis=0)

    all_rows = jnp.take(passage_row, cand_block.reshape(-1), axis=0)
    is_mine = (all_rows // passage_count == my_shard).reshape(shard_total, pairs_here)
    mine_int = is_mine.astype(jnp.int32)
    rank = jnp.cumsum(mine_int, axis=1) - mine_int
    source_ids = jnp.arange(shard_total, dtype=jnp.int32)[:, None]
    places = jnp.where(is_mine, source_ids * capacity + rank, shard_total * capacity).reshape(-1)
    pair_query = jnp.arange(shard_total * pairs_here, dtype=jnp.int32) // per_query
    slot_table = (
        jnp.zeros((shard_total * capacity,), jnp.int32)
        .at[places]
        .set(all_rows % passage_count, mode="drop")
    )
    query_table = (
        jnp.zeros((shard_total * capacity,), jnp.int32).at[places].set(pair_query, mode="drop")
    )
    asked = jnp.take(query_block, query_table, axis=0)
    chosen = jnp.take(passages, slot_table, axis=0)
    pair_scored = jnp.einsum("ntd,npd->ntp", asked, chosen, preferred_element_type=jnp.float32)
    token_index = lax.axis_index("cent") * token_rows + jnp.arange(token_rows, dtype=jnp.int32)
    valid_tokens = token_index[None, :] < jnp.take(lengths, slot_table, axis=0)[:, None]
    pair_scored = jnp.where(valid_tokens[:, None, :], pair_scored, masked_score)
    partial_value = jnp.max(pair_scored, axis=2)

    merged = lax.pmax(
        jnp.concatenate([shard_best, partial_value], axis=0), "cent"
    )
    token_best = merged[:query_count]
    complete = merged[query_count:]
    pair_scores = (jnp.sum(complete, axis=1) / query_tokens).reshape(shard_total, capacity)
    returned = lax.all_to_all(pair_scores, "shard", split_axis=0, concat_axis=0, tiled=True)

    pair_rows = jnp.take(passage_row, candidates.reshape(-1), axis=0)
    owners = pair_rows // passage_count
    onehot = (owners[:, None] == jnp.arange(shard_total, dtype=jnp.int32)[None, :]).astype(
        jnp.int32
    )
    ranking = jnp.sum((jnp.cumsum(onehot, axis=0) - onehot) * onehot, axis=1)
    my_places = owners * capacity + ranking
    scores = jnp.take(returned.reshape(-1), my_places, axis=0).reshape(query_count, per_query)
    return (token_best, scores)


def solution(mesh):
    in_specs = (
        P("shard", None, None),
        P(("shard", "cent"), None),
        P("shard", "cent", None),
        P("shard"),
        P(),
        P("shard", None),
    )
    out_specs = (P("shard", None), P("shard", None))
    return jax.shard_map(
        per_device, mesh=mesh, in_specs=in_specs, out_specs=out_specs, check_vma=False
    )
```

time: 634 us -> 416 us (0.66)
  waiting for transfers between devices: 491 us -> 53.2 us
  local copies, waits for them, and re-layouts: 44.8 us -> 241 us
  blocking collectives: 0 us -> 55.1 us
  starting transfers between devices: 37 us -> 19.4 us
  other arithmetic: 17.9 us -> 6.63 us
    pmax x2 -> x1, waiting for transfers between devices: 291 us -> 44.7 us  [per_device(): lax.pmax(jnp.concatenate([shard_best, partial_value], axis=0), 'cent')]
    all_to_all x2 -> x1, waiting for transfers between devices: 176 us -> 0.01 us  [per_device(): lax.all_to_all(local_best, 'shard', split_axis=0, concat_axis=0, tiled=True)]
    scatter x1 -> x2, local copies, waits for them, and re-layouts: 1.41 us -> 121 us  [the longest x1 60.5 us: per_device(): slot_table = jnp.zeros((shard_total * capacity,), jnp.int32).at[places].s...]
    gather x4 -> x6, local copies, waits for them, and re-layouts: 10.9 us -> 110 us  [the longest x1 90.5 us: per_device(): all_rows = jnp.take(passage_row, cand_block.reshape(-1), axis=0)]
    all_gather x0 -> x1, blocking collectives: none -> 55.1 us  [per_device(): cand_block = lax.all_gather(candidates, 'shard', axis=0, tiled=True)]
    reshape x4, local copies, waits for them, and re-layouts: 23.8 us -> 0.81 us  [the longest x3 0.64 us: per_device(): all_rows = jnp.take(passage_row, cand_block.reshape(-1), axis=0)]
    all_to_all x2 -> x1, starting transfers between devices: 23.8 us -> 6.45 us  [per_device(): lax.all_to_all(local_best, 'shard', split_axis=0, concat_axis=0, tiled=True)]
    all_gather x1, waiting for transfers between devices: 14.3 us -> 0.02 us  [per_device(): query_block = lax.all_gather(queries, 'shard', axis=0, tiled=True)]
  transfers between devices with their start and end apart: 6 -> 4, of which waited for: 5 -> 2; matrix products, arithmetic and copies ran while one was open for 6% -> 60% of each run, Pallas kernels for 0% -> 0%
where the time goes in v1:
time: 416 us; the launch traced here: 415 us
  local copies, waits for them, and re-layouts  241 us (58%)
  blocking collectives  55.1 us (13%)
  waiting for transfers between devices  53.2 us (13%)
  matrix products  25.3 us (6%)
  starting transfers between devices  19.4 us (5%)
  between operations  14.5 us (3%)
  other arithmetic  6.63 us (2%)
    gather x1, local copies, waits for them, and re-layouts, per_device(): all_rows = jnp.take(passage_row, cand_block.reshape(-1), axis=0)  90.5 us
    scatter x1, local copies, waits for them, and re-layouts, per_device(): slot_table = jnp.zeros((shard_total * capacity,), jnp.int32).at[places].s...  60.5 us
    scatter x1, local copies, waits for them, and re-layouts, per_device(): jnp.zeros((shard_total * capacity,), jnp.int32).at[places]  60.3 us
    all_gather x1, blocking collectives, per_device(): cand_block = lax.all_gather(candidates, 'shard', axis=0, tiled=True)  55.1 us
    pmax x1, waiting for transfers between devices, per_device(): lax.pmax(jnp.concatenate([shard_best, partial_value], axis=0), 'cent')  44.7 us
    dot_general x1, matrix products, per_device(): jnp.einsum('rd,cd->rc', flattened, centroids, preferred_element_type=jnp....  17 us
    all_to_all x1, starting transfers between devices, per_device(): lax.all_to_all(pair_scores, 'shard', split_axis=0, concat_axis=0, tiled=T...  12.9 us
  transfers between devices with their start and end apart: 4, of which 2 were waited for; matrix products, arithmetic and copies ran while one was open for 60% of the time, Pallas kernels for 0%

profile of v1, /device:TPU:1, one launch (start us, length us, event | category | flops | bytes accessed | tf_op | source)
XLA Modules:
  0.0 415.2 jit_solution(12105765791642082866)
XLA Ops:
  7.9 0.8 reshape.445
  8.7 0.8 reshape.447
  9.5 0.8 reshape.446
  10.3 55.1 %all_gather.7 = s32[1024,16]{1,0:T(8,128)S(1)} all-gather(s32[16,16]{1,0:T(8,128)} %param.11), channel_id=1, replica_groups=mesh['shard'=64,'cent'=4] {'shard'}, dimensions={0}, use_global_device_ids=true | all-gather | bytes 66560 | tf_op jit(solution)/shard_map/all_gather | solution.py:22
  66.0 2.1 gather_fusion.4
  69.3 90.5 %gather_fusion = s32[16384]{0:T(1024)S(1)} fusion(s32[16384]{0:T(1024)S(1)} %copy-done.1, s32[16384]{0:T(1024)S(1)} %broadcast_clamp_fusion), kind=kCustom, calls=%fused_computation | custom fusion | bytes 196608 | tf_op jit(solution)/shard_map/jit(_take)/gather | solution.py:30
  161.5 60.3 %scatter_custom_fusion.1 = s32[768]{0:T(1024)S(1)} fusion(s32[16384]{0:T(1024)S(1)} %bitcast.49, s32[16384]{0:T(1024)S(1)} %add_select_fusion, s32[]{:T(128)} %constant.143.clone.1), kind=kCustom, calls=%fused_computation.97 | custom fusion | bytes 3076 | tf_op jit(solution)/shard_map/scatter | solution.py:43
  221.8 60.5 %scatter_custom_fusion = s32[768]{0:T(1024)S(1)} fusion(s32[16384]{0:T(1024)S(1)} %bitcast.50, s32[16384]{0:T(1024)S(1)} %add_select_fusion.1, s32[]{:T(128)} %constant.143.clone.1), kind=kCustom, calls=%fused_computation.99 | custom fusion | bytes 3076 | tf_op jit(solution)/shard_map/scatter | solution.py:40
  282.3 5.0 %gather_fusion.1 = s32[768]{0:T(1024)S(1)} fusion(s32[256]{0:T(256)S(1)} %copy-done.2, s32[1024]{0:T(1024)S(1)} %pad_clamp_fusion.3), kind=kCustom, calls=%fused_computation.1 | custom fusion | bytes 9216 | tf_op jit(solution)/shard_map/jit(_take)/gather | solution.py:49
  287.4 4.5 %gather_fusion.3 = bf16[768,32,128]{2,1,0:T(8,128)(2,1)} fusion(bf16[256,32,128]{2,1,0:T(8,128)(2,1)S(1)} %copy-done, s32[1024]{0:T(1024)S(1)} %pad_clamp_fusion.3), kind=kCustom, calls=%fused_computation.3 | custom fusion | bytes 12585984 | tf_op jit(solution)/shard_map/jit(_take)/gather | solution.py:46
  292.3 17.0 %convolution_reduce_fusion = f32[32768]{0:T(1024)S(1)} fusion(bf16[32768,128]{1,0:T(8,128)(2,1)} %bitcast.43, bf16[768,128]{1,0:T(8,128)(2,1)S(1)} %copy-done.5), kind=kOutput, calls=%fused_computation.8 | convolution fusion | flops 6467584000 | bytes 8716288 | tf_op jit(solution)/shard_map/rd,cd->rc/dot_general | solution.py:25
  309.5 0.9 reshape.532
  310.4 6.4 %all-to-all-start = ((f32[64,1,512]{2,1,0:T(1,128)}), f32[64,1,512]{2,1,0:T(1,128)S(1)}, u32[]{:S(2)}, u32[]{:S(2)}) async-start(f32[64,1,512]{2,1,0:T(1,128)} %reshape.532), calls=%async_computation | async-start | bytes 262144 | tf_op jit(solution)/shard_map/all_to_all | solution.py:27
  316.9 8.3 %gather_fusion.2 = bf16[768,32,128]{2,1,0:T(8,128)(2,1)} fusion(bf16[1024,32,128]{2,1,0:T(8,128)(2,1)} %all-gather.2.cloned.1.call-done, s32[1024]{0:T(1024)S(1)} %pad_clamp_fusion.2), kind=kCustom, calls=%fused_computation.2 | custom fusion | bytes 12585984 | tf_op jit(solution)/shard_map/jit(_take)/gather | solution.py:45
  325.2 8.3 %select_reduce_fusion = f32[768,32]{1,0:T(8,128)S(1)} fusion(pred[768,32]{1,0:T(8,128)(4,1)S(1)} %broadcast_compare_fusion, bf16[768,32,128]{2,1,0:T(8,128)(2,1)} %gather_fusion.3, pred[768]{0:T(1024)(128)(4,1)S(1)} %get-tuple-element.9, bf16[768,32,128]{2,1,0:T(8,128)(2,1)} %gather_fusion.2, pred[768]{0:T(1024)(128)(4,1)S(1)} %compare_and_fusion), kind=kOutput, calls=%fused_computation.9 | convolution fusion | flops 209166336 | bytes 12707328 | tf_op jit(solution)/shard_map/ntd,npd->ntp/dot_general | solution.py:47
  334.1 1.0 reduce.8
  335.4 0.7 pad_maximum_fusion
  336.2 44.7 %all-reduce.2.cloned.1.call-done = f32[784,32]{0,1:T(8,128)} async-done(((f32[784,32]{0,1:T(8,128)}), f32[784,32]{0,1:T(8,128)}) %all-reduce.2.cloned.1.call-update) | async-done | bytes 100368 | tf_op jit(solution)/shard_map/pmax | solution.py:53
  381.0 1.0 slice_reduce_fusion
  382.7 12.9 %all-to-all-start.1 = ((f32[64,1,12]{2,1,0:T(1,128)}), f32[64,1,12]{2,1,0:T(1,128)S(1)}, u32[]{:S(2)}, u32[]{:S(2)}) async-start(f32[64,1,12]{2,1,0:T(1,128)} %bitcast.9), calls=%async_computation.1 | async-start | bytes 65536 | tf_op jit(solution)/shard_map/all_to_all | solution.py:59
  395.7 0.7 slice.37
  397.1 7.7 %all-to-all-done.1 = f32[64,1,12]{2,1,0:T(1,128)S(1)} async-done(((f32[64,1,12]{2,1,0:T(1,128)}), f32[64,1,12]{2,1,0:T(1,128)S(1)}, u32[]{:S(2)}, u32[]{:S(2)}) %all-to-all-start.1) | async-done | bytes 3104 | tf_op jit(solution)/shard_map/all_to_all | solution.py:59
  405.4 0.7 reduce.7
  406.2 1.4 gather_fusion.5
  (72 shorter events, 8.6 us)
Async XLA Ops:
  7.2 280.2 %copy-start = (bf16[256,32,128]{2,1,0:T(8,128)(2,1)S(1)}, bf16[256,32,128]{2,1,0:T(8,128)(2,1)}, u32[]{:S(2)}) copy-start(bf16[256,32,128]{2,1,0:T(8,128)(2,1)} %param.8) | copy-start | bytes 6291460
  7.2 62.1 %copy-start.1 = (s32[16384]{0:T(1024)S(1)}, s32[16384]{0:T(1024)}, u32[]{:S(2)}) copy-start(s32[16384]{0:T(1024)} %param.10) | copy-start | bytes 196612
  7.2 285.1 %all-gather.2.cloned.1.call-start = ((), (), s32[]{:S(2)}) async-start(), calls=%async_computation.2 | async-start | bytes 8519680 | tf_op jit(solution)/shard_map/all_gather | solution.py:21
  69.0 90.8 %copy-start.4 = (s32[64,3]{0,1:T(4,128)}, s32[64,3]{0,1:T(4,128)S(1)}, u32[]{:S(2)}) copy-start(s32[64,3]{0,1:T(4,128)S(1)} %reduce-window.19) | copy-start | bytes 2308
  69.2 213.1 %copy-start.2 = (s32[256]{0:T(256)S(1)}, s32[256]{0:T(256)}, u32[]{:S(2)}) copy-start(s32[256]{0:T(256)} %param.9) | copy-start | bytes 3076
  287.3 4.6 %slice-start = ((s32[64,3]{0,1:T(4,128)}), s32[64,2]{0,1:T(2,128)S(1)}, s32[]{:S(2)}) async-start(s32[64,3]{0,1:T(4,128)} %copy-done.4), calls=%async_computation.4 | async-start | bytes 2048 | tf_op jit(solution)/shard_map/slice.5
  287.4 4.9 %copy-start.5 = (bf16[768,128]{1,0:T(8,128)(2,1)S(1)}, bf16[768,128]{1,0:T(8,128)(2,1)}, u32[]{:S(2)}) copy-start(bf16[768,128]{1,0:T(8,128)(2,1)} %param.7) | copy-start | bytes 589828
  310.4 23.2 %all-to-all-start = ((f32[64,1,512]{2,1,0:T(1,128)}), f32[64,1,512]{2,1,0:T(1,128)S(1)}, u32[]{:S(2)}, u32[]{:S(2)}) async-start(f32[64,1,512]{2,1,0:T(1,128)} %reshape.532), calls=%async_computation | async-start | bytes 262144 | tf_op jit(solution)/shard_map/all_to_all | solution.py:27
  316.8 64.1 %all-reduce.2.cloned.1.call-start = ((), (), s32[]{:S(2)}) async-start(), calls=%async_computation.3 | async-start | bytes 229376 | tf_op jit(solution)/shard_map/pmax | solution.py:53
  325.2 82.5 %copy-start.3 = (s32[16,16]{1,0:T(8,128)S(1)}, s32[16,16]{1,0:T(8,128)}, u32[]{:S(2)}) copy-start(s32[16,16]{1,0:T(8,128)} %param.11) | copy-start | bytes 3076
  382.7 22.2 %all-to-all-start.1 = ((f32[64,1,12]{2,1,0:T(1,128)}), f32[64,1,12]{2,1,0:T(1,128)S(1)}, u32[]{:S(2)}, u32[]{:S(2)}) async-start(f32[64,1,12]{2,1,0:T(1,128)} %bitcast.9), calls=%async_computation.1 | async-start | bytes 65536 | tf_op jit(solution)/shard_map/all_to_all | solution.py:59
Sparse Core Ops, SparseCore 0:
  10.8 87.3 all-gather.1
  336.3 44.5 all-reduce.1

commit v2 on v1

v2 whole, which is shorter than its diff:
```python
import jax
import jax.numpy as jnp
from jax import lax
from jax.sharding import PartitionSpec as P

masked_score = -1e30


def per_device(queries, centroids, passages, lengths, passage_row, candidates):
    query_count = queries.shape[0]
    query_tokens = queries.shape[1]
    feature_width = queries.shape[2]
    per_query = candidates.shape[1]
    passage_count = passages.shape[0]
    token_rows = passages.shape[1]
    shard_total = lax.axis_size("shard")
    capacity = max(2, 3 * query_count * per_query // shard_total)
    pairs_here = query_count * per_query
    my_shard = lax.axis_index("shard")

    pair_rows = jnp.take(passage_row, candidates.reshape(-1), axis=0)
    owners = pair_rows // passage_count
    onehot = (owners[:, None] == jnp.arange(shard_total, dtype=jnp.int32)[None, :]).astype(
        jnp.int32
    )
    ranking = jnp.sum((jnp.cumsum(onehot, axis=0) - onehot) * onehot, axis=1)
    my_places = owners * capacity + ranking
    pair_local = jnp.arange(pairs_here, dtype=jnp.int32) // per_query
    entries = jnp.stack([pair_rows % passage_count, pair_local], axis=1).astype(jnp.bfloat16)
    table = jnp.full((shard_total * capacity, 2), -1.0, jnp.bfloat16).at[my_places].set(entries)
    row_width = query_tokens * feature_width
    table_rows = -(-(shard_total * capacity * 2) // row_width)
    table = jnp.pad(table.reshape(-1), (0, table_rows * row_width - shard_total * capacity * 2))

    packed = jnp.concatenate(
        [queries.reshape(query_count, row_width), table.reshape(table_rows, row_width)], axis=0
    )
    packed_block = lax.all_gather(packed, "shard", axis=0, tiled=False)
    query_block = packed_block[:, :query_count].reshape(-1, query_tokens, feature_width)
    tables = packed_block[:, query_count:].reshape(shard_total, -1)[:, : shard_total * capacity * 2]
    tables = tables.reshape(shard_total, shard_total, capacity, 2)
    mine = lax.dynamic_index_in_dim(tables, my_shard, axis=1, keepdims=False).astype(jnp.int32)

    flattened = query_block.reshape(-1, feature_width)
    scored = jnp.einsum("rd,cd->rc", flattened, centroids, preferred_element_type=jnp.float32)
    local_best = jnp.max(scored, axis=1).reshape(shard_total, query_count, query_tokens)
    gathered_best = lax.all_to_all(local_best, "shard", split_axis=0, concat_axis=0, tiled=True)
    shard_best = jnp.max(gathered_best, axis=0)

    slot_table = jnp.maximum(mine[..., 0], 0).reshape(-1)
    query_table = (
        jnp.arange(shard_total, dtype=jnp.int32)[:, None] * query_count + jnp.maximum(mine[..., 1], 0)
    ).reshape(-1)
    asked = jnp.take(query_block, query_table, axis=0)
    chosen = jnp.take(passages, slot_table, axis=0)
    pair_scored = jnp.einsum("ntd,npd->ntp", asked, chosen, preferred_element_type=jnp.float32)
    token_index = lax.axis_index("cent") * token_rows + jnp.arange(token_rows, dtype=jnp.int32)
    valid_tokens = token_index[None, :] < jnp.take(lengths, slot_table, axis=0)[:, None]
    pair_scored = jnp.where(valid_tokens[:, None, :], pair_scored, masked_score)
    partial_value = jnp.max(pair_scored, axis=2)

    merged = jnp.concatenate([shard_best, partial_value], axis=0)
    cent_total = lax.axis_size("cent")
    step = 1
    while step < cent_total:
        partner = [(i, i ^ step) for i in range(cent_total)]
        merged = jnp.maximum(merged, lax.ppermute(merged, "cent", partner))
        step *= 2
    token_best = merged[:query_count]
    complete = merged[query_count:]
    pair_scores = (jnp.sum(complete, axis=1) / query_tokens).reshape(shard_total, capacity)
    returned = lax.all_to_all(pair_scores, "shard", split_axis=0, concat_axis=0, tiled=True)

    scores = jnp.take(returned.reshape(-1), my_places, axis=0).reshape(query_count, per_query)
    return (token_best, scores)


def solution(mesh):
    in_specs = (
        P("shard", None, None),
        P(("shard", "cent"), None),
        P("shard", "cent", None),
        P("shard"),
        P(),
        P("shard", None),
    )
    out_specs = (P("shard", None), P("shard", None))
    return jax.shard_map(
        per_device, mesh=mesh, in_specs=in_specs, out_specs=out_specs, check_vma=False
    )
```

time: 416 us -> 241 us (0.58)
  local copies, waits for them, and re-layouts: 241 us -> 66.4 us
  blocking collectives: 55.1 us -> 0 us
  waiting for transfers between devices: 53.2 us -> 107 us
    scatter x2 -> x1, local copies, waits for them, and re-layouts: 121 us -> 1.24 us  [per_device(): jnp.full((shard_total * capacity, 2), -1.0, jnp.bfloat16).at[my_places]]
    all_gather x1, waiting for transfers between devices: 0.02 us -> 93.5 us  [per_device(): packed_block = lax.all_gather(packed, 'shard', axis=0, tiled=False)]
    gather x1 -> x0, local copies, waits for them, and re-layouts: 90.5 us -> none  [per_device(): all_rows = jnp.take(passage_row, cand_block.reshape(-1), axis=0)]
    all_gather x1 -> x0, blocking collectives: 55.1 us -> none  [per_device(): cand_block = lax.all_gather(candidates, 'shard', axis=0, tiled=True)]
    pmax x1 -> x0, waiting for transfers between devices: 44.7 us -> none  [per_device(): lax.pmax(jnp.concatenate([shard_best, partial_value], axis=0), 'cent')]
    another operation x5 -> x3, local copies, waits for them, and re-layouts: 0.25 us -> 13.6 us  [the longest x1 13.5 us: per_device(): flattened = query_block.reshape(-1, feature_width)]
    slice x1 -> x5, local copies, waits for them, and re-layouts: 0.18 us -> 11.4 us  [the longest x1 7.7 us: per_device(): packed_block[:, :query_count].reshape(-1, query_tokens, feature_width)]
    unnamed x17 -> x14, local copies, waits for them, and re-layouts: 1.92 us -> 12.8 us
  transfers between devices with their start and end apart: 4 -> 5, of which waited for: 2 -> 4; matrix products, arithmetic and copies ran while one was open for 60% -> 7% of each run, Pallas kernels for 0% -> 0%
where the time goes in v2:
time: 241 us
  waiting for transfers between devices  107 us (44%)
  local copies, waits for them, and re-layouts  66.4 us (28%)
  matrix products  25.4 us (11%)
  starting transfers between devices  22.5 us (9%)
  between operations  14.4 us (6%)
  other arithmetic  4.51 us (2%)
    all_gather x1, waiting for transfers between devices, per_device(): packed_block = lax.all_gather(packed, 'shard', axis=0, tiled=False)  93.5 us
    dot_general x1, matrix products, per_device(): jnp.einsum('rd,cd->rc', flattened, centroids, preferred_element_type=jnp....  17.1 us
    another operation x1, local copies, waits for them, and re-layouts, per_device(): flattened = query_block.reshape(-1, feature_width)  13.5 us
    unnamed x14, local copies, waits for them, and re-layouts  12.8 us
    all_to_all x1, starting transfers between devices, per_device(): lax.all_to_all(pair_scores, 'shard', split_axis=0, concat_axis=0, tiled=T...  12.6 us
    all_to_all x1, waiting for transfers between devices, per_device(): lax.all_to_all(pair_scores, 'shard', split_axis=0, concat_axis=0, tiled=T...  8.46 us
    gather x1, local copies, waits for them, and re-layouts, per_device(): asked = jnp.take(query_block, query_table, axis=0)  8.3 us
    dot_general x1, matrix products, per_device(): jnp.einsum('ntd,npd->ntp', asked, chosen, preferred_element_type=jnp.floa...  8.29 us
  transfers between devices with their start and end apart: 5, of which 4 were waited for; matrix products, arithmetic and copies ran while one was open for 7% of the time, Pallas kernels for 0%

profile of v2, /device:TPU:1, one launch (start us, length us, event | category | flops | bytes accessed | tf_op | source)
XLA Modules:
  0.0 240.6 jit_solution(13284242471353563967)
XLA Ops:
  7.2 0.9 reshape.394
  9.7 2.1 gather_fusion
  13.0 1.2 scatter_custom_fusion
  14.5 1.0 copy.54
  16.5 93.5 %all-gather.4.cloned.1.call-done = bf16[64,17,4096]{2,1,0:T(8,128)(2,1)} async-done(((bf16[1,17,4096]{2,1,0:T(8,128)(2,1)}), bf16[64,17,4096]{2,1,0:T(8,128)(2,1)}) %all-gather.4.cloned.1.call-update) | async-done | bytes 8912912 | tf_op jit(solution)/shard_map/all_gather | solution.py:38
  110.1 3.3 %slice.48 = bf16[64,1,4096]{2,1,0:T(2,128)(2,1)S(1)} slice(bf16[64,17,4096]{2,1,0:T(8,128)(2,1)} %all-gather.4.cloned.1.call-done), slice={[0:64], [16:17], [0:4096]} | slice | bytes 1048576 | tf_op jit(solution)/shard_map/slice | solution.py:40
  115.1 7.7 %slice.47 = bf16[64,16,4096]{2,1,0:T(8,128)(2,1)} slice(bf16[64,17,4096]{2,1,0:T(8,128)(2,1)} %all-gather.4.cloned.1.call-done), slice={[0:64], [0:16], [0:4096]} | slice | bytes 16777216 | tf_op jit(solution)/shard_map/slice | solution.py:39
  122.8 13.5 %reshape_reshape.3 = bf16[32768,128]{1,0:T(8,128)(2,1)} reshape(bf16[64,16,4096]{2,1,0:T(8,128)(2,1)} %slice.47) | data formatting | bytes 16777216 | tf_op jit(solution)/shard_map/reshape;reshape | solution.py:44
  136.3 9.4 %copy.49 = bf16[128,8,32,128]{3,2,1,0:T(8,128)(2,1)} copy(bf16[128,8,32,128]{3,1,2,0:T(8,128)(2,1)} %bitcast.54) | data formatting | bytes 16777216
  145.7 5.0 %gather_fusion.1 = s32[768]{0:T(1024)S(1)} fusion(s32[256]{0:T(256)S(1)} %copy-done.1, s32[1024]{0:T(1024)S(1)} %pad_clamp_fusion.2), kind=kCustom, calls=%fused_computation.1 | custom fusion | bytes 9216 | tf_op jit(solution)/shard_map/jit(_take)/gather | solution.py:58
  150.7 4.5 %gather_fusion.3 = bf16[768,32,128]{2,1,0:T(8,128)(2,1)} fusion(bf16[256,32,128]{2,1,0:T(8,128)(2,1)S(1)} %copy-done, s32[1024]{0:T(1024)S(1)} %pad_clamp_fusion.2), kind=kCustom, calls=%fused_computation.3 | custom fusion | bytes 12585984 | tf_op jit(solution)/shard_map/jit(_take)/gather | solution.py:55
  155.2 17.1 %convolution_reduce_fusion = f32[32768]{0:T(1024)S(1)} fusion(bf16[32768,128]{1,0:T(8,128)(2,1)} %reshape_reshape.3, bf16[768,128]{1,0:T(8,128)(2,1)S(1)} %copy-done.3), kind=kOutput, calls=%fused_computation.6 | convolution fusion | flops 6467584000 | bytes 8716288 | tf_op jit(solution)/shard_map/rd,cd->rc/dot_general | solution.py:45
  172.5 0.9 reshape.473
  173.4 5.9 %all-to-all-start = ((f32[64,1,512]{2,1,0:T(1,128)}), f32[64,1,512]{2,1,0:T(1,128)S(1)}, u32[]{:S(2)}, u32[]{:S(2)}) async-start(f32[64,1,512]{2,1,0:T(1,128)} %reshape.473), calls=%async_computation | async-start | bytes 262144 | tf_op jit(solution)/shard_map/all_to_all | solution.py:47
  179.4 8.3 %gather_fusion.2 = bf16[768,32,128]{2,1,0:T(8,128)(2,1)} fusion(bf16[1024,32,128]{2,1,0:T(8,128)(2,1)} %bitcast.55, s32[1024]{0:T(1024)S(1)} %pad_clamp_fusion.1), kind=kCustom, calls=%fused_computation.2 | custom fusion | bytes 12585984 | tf_op jit(solution)/shard_map/jit(_take)/gather | solution.py:54
  187.8 8.3 %select_reduce_fusion = f32[768,32]{1,0:T(8,128)S(1)} fusion(pred[768,32]{1,0:T(8,128)(4,1)S(1)} %broadcast_compare_fusion, bf16[768,32,128]{2,1,0:T(8,128)(2,1)} %gather_fusion.3, pred[768]{0:T(1024)(128)(4,1)S(1)} %le.94, bf16[768,32,128]{2,1,0:T(8,128)(2,1)} %gather_fusion.2, pred[768]{0:T(1024)(128)(4,1)S(1)} %compare_and_fusion), kind=kOutput, calls=%fused_computation.7 | convolution fusion | flops 209166336 | bytes 12707328 | tf_op jit(solution)/shard_map/ntd,npd->ntp/dot_general | solution.py:56
  196.7 0.9 reduce.8
  198.1 1.3 collective-permute-start
  199.4 2.9 %collective-permute-done = f32[784,32]{0,1:T(8,128)S(1)} collective-permute-done((f32[784,32]{0,1:T(8,128)S(1)}, f32[784,32]{0,1:T(8,128)S(1)}, u32[]{:S(2)}, u32[]{:S(2)}) %collective-permute-start) | collective-permute-done | bytes 100384 | tf_op jit(solution)/shard_map/ppermute | solution.py:67
  202.4 2.8 %collective-permute-start.1 = (f32[784,32]{0,1:T(8,128)S(1)}, f32[784,32]{0,1:T(8,128)S(1)}, u32[]{:S(2)}, u32[]{:S(2)}) collective-permute-start(f32[784,32]{0,1:T(8,128)S(1)} %fusion.24), channel_id=1, source_target_pairs={{0,2},{1,3},{2,0},{3,1},{4,6},{5,7},{6,4},{7,5},{8,10},{9,11},{10,... | collective-permute-start | bytes 301064 | tf_op jit(solution)/shard_map/ppermute | solution.py:67
  205.2 2.4 %collective-permute-done.1 = f32[784,32]{0,1:T(8,128)S(1)} collective-permute-done((f32[784,32]{0,1:T(8,128)S(1)}, f32[784,32]{0,1:T(8,128)S(1)}, u32[]{:S(2)}, u32[]{:S(2)}) %collective-permute-start.1) | collective-permute-done | bytes 100384 | tf_op jit(solution)/shard_map/ppermute | solution.py:67
  208.4 12.6 %all-to-all-start.1 = ((f32[64,1,12]{2,1,0:T(1,128)}), f32[64,1,12]{2,1,0:T(1,128)S(1)}, u32[]{:S(2)}, u32[]{:S(2)}) async-start(f32[64,1,12]{2,1,0:T(1,128)} %bitcast.11), calls=%async_computation.1 | async-start | bytes 65536 | tf_op jit(solution)/shard_map/all_to_all | solution.py:72
  221.9 8.5 %all-to-all-done.1 = f32[64,1,12]{2,1,0:T(1,128)S(1)} async-done(((f32[64,1,12]{2,1,0:T(1,128)}), f32[64,1,12]{2,1,0:T(1,128)S(1)}, u32[]{:S(2)}, u32[]{:S(2)}) %all-to-all-start.1) | async-done | bytes 3104 | tf_op jit(solution)/shard_map/all_to_all | solution.py:72
  231.7 1.4 gather_fusion.4
  (77 shorter events, 10.9 us)
Async XLA Ops:
  7.2 143.5 %copy-start = (bf16[256,32,128]{2,1,0:T(8,128)(2,1)S(1)}, bf16[256,32,128]{2,1,0:T(8,128)(2,1)}, u32[]{:S(2)}) copy-start(bf16[256,32,128]{2,1,0:T(8,128)(2,1)} %param.8) | copy-start | bytes 6291460
  7.2 102.9 %all-gather.4.cloned.1.call-start = ((), (), s32[]{:S(2)}) async-start(), calls=%async_computation.2 | async-start | bytes 12779520 | tf_op jit(solution)/shard_map/all_gather | solution.py:38
  136.3 9.5 %copy-start.1 = (s32[256]{0:T(256)S(1)}, s32[256]{0:T(256)}, u32[]{:S(2)}) copy-start(s32[256]{0:T(256)} %param.9) | copy-start | bytes 3076
  150.7 4.5 %copy-start.3 = (bf16[768,128]{1,0:T(8,128)(2,1)S(1)}, bf16[768,128]{1,0:T(8,128)(2,1)}, u32[]{:S(2)}) copy-start(bf16[768,128]{1,0:T(8,128)(2,1)} %param.7) | copy-start | bytes 589828
  173.4 22.8 %all-to-all-start = ((f32[64,1,512]{2,1,0:T(1,128)}), f32[64,1,512]{2,1,0:T(1,128)S(1)}, u32[]{:S(2)}, u32[]{:S(2)}) async-start(f32[64,1,512]{2,1,0:T(1,128)} %reshape.473), calls=%async_computation | async-start | bytes 262144 | tf_op jit(solution)/shard_map/all_to_all | solution.py:47
  187.7 45.4 %copy-start.2 = (s32[16,16]{1,0:T(8,128)S(1)}, s32[16,16]{1,0:T(8,128)}, u32[]{:S(2)}) copy-start(s32[16,16]{1,0:T(8,128)} %param.11) | copy-start | bytes 3076
  198.1 4.2 %collective-permute-start = (f32[784,32]{0,1:T(8,128)S(1)}, f32[784,32]{0,1:T(8,128)S(1)}, u32[]{:S(2)}, u32[]{:S(2)}) collective-permute-start(f32[784,32]{0,1:T(8,128)S(1)} %pad_maximum_fusion), channel_id=1, source_target_pairs={{0,1},{1,0},{2,3},{3,2},{4,5},{5,4},{6,7},{7,6},{8,9},{9,8},{10,11... | collective-permute-start | bytes 301064 | tf_op jit(solution)/shard_map/ppermute | solution.py:67
  202.4 5.2 %collective-permute-start.1 = (f32[784,32]{0,1:T(8,128)S(1)}, f32[784,32]{0,1:T(8,128)S(1)}, u32[]{:S(2)}, u32[]{:S(2)}) collective-permute-start(f32[784,32]{0,1:T(8,128)S(1)} %fusion.24), channel_id=1, source_target_pairs={{0,2},{1,3},{2,0},{3,1},{4,6},{5,7},{6,4},{7,5},{8,10},{9,11},{10,... | collective-permute-start | bytes 301064 | tf_op jit(solution)/shard_map/ppermute | solution.py:67
  208.4 21.9 %all-to-all-start.1 = ((f32[64,1,12]{2,1,0:T(1,128)}), f32[64,1,12]{2,1,0:T(1,128)S(1)}, u32[]{:S(2)}, u32[]{:S(2)}) async-start(f32[64,1,12]{2,1,0:T(1,128)} %bitcast.11), calls=%async_computation.1 | async-start | bytes 65536 | tf_op jit(solution)/shard_map/all_to_all | solution.py:72
Sparse Core Ops, SparseCore 0:
  16.3 93.7 all-gather.3

commit v3 on v2

v3 whole, which is shorter than its diff:
```python
import jax
import jax.numpy as jnp
from jax import lax
from jax.sharding import Mesh, PartitionSpec as P

masked_score = -1e30


def per_device(queries, centroids, passages, lengths, passage_row, candidates):
    query_count = queries.shape[0]
    query_tokens = queries.shape[1]
    feature_width = queries.shape[2]
    per_query = candidates.shape[1]
    passage_count = passages.shape[0]
    token_rows = passages.shape[1]
    shard_total = lax.axis_size(("chip", "core"))
    capacity = max(2, 3 * query_count * per_query // shard_total)
    pairs_here = query_count * per_query
    my_shard = lax.axis_index(("chip", "core"))

    pair_rows = jnp.take(passage_row, candidates.reshape(-1), axis=0)
    owners = pair_rows // passage_count
    onehot = (owners[:, None] == jnp.arange(shard_total, dtype=jnp.int32)[None, :]).astype(
        jnp.int32
    )
    ranking = jnp.sum((jnp.cumsum(onehot, axis=0) - onehot) * onehot, axis=1)
    my_places = owners * capacity + ranking
    pair_local = jnp.arange(pairs_here, dtype=jnp.int32) // per_query
    entries = jnp.stack([pair_rows % passage_count, pair_local], axis=1).astype(jnp.bfloat16)
    table = jnp.full((shard_total * capacity, 2), -1.0, jnp.bfloat16).at[my_places].set(entries)
    table = table.reshape(-1)

    tables = lax.all_gather(table, ("chip", "core"), axis=0, tiled=False)
    tables = tables[:, : shard_total * capacity * 2].reshape(shard_total, shard_total, capacity, 2)
    mine = lax.dynamic_index_in_dim(tables, my_shard, axis=1, keepdims=False).astype(jnp.int32)
    core_total = lax.axis_size("core")
    my_core = lax.axis_index("core")
    same_core = lax.all_gather(queries, "chip", axis=0, tiled=False)
    other_core = lax.ppermute(same_core, "core", [(i, (i + 1) % core_total) for i in range(core_total)])
    first, second = (
        jnp.where(my_core == 0, same_core, other_core),
        jnp.where(my_core == 0, other_core, same_core),
    )
    query_block = jnp.stack([first, second], axis=1).reshape(-1, query_tokens, feature_width)

    def block_best(block):
        scored = jnp.einsum("rd,cd->rc", block.reshape(-1, feature_width), centroids,
                            preferred_element_type=jnp.float32)
        return jnp.max(scored, axis=1).reshape(-1, query_count, query_tokens)

    best_same = block_best(same_core)
    best_other = block_best(other_core)
    local_best = jnp.stack(
        [jnp.where(my_core == 0, best_same, best_other), jnp.where(my_core == 0, best_other, best_same)],
        axis=1,
    ).reshape(shard_total, query_count, query_tokens)
    gathered_best = lax.all_to_all(local_best, ("chip", "core"), split_axis=0, concat_axis=0, tiled=True)
    shard_best = jnp.max(gathered_best, axis=0)

    slot_table = jnp.maximum(mine[..., 0], 0).reshape(-1)
    query_table = (
        jnp.arange(shard_total, dtype=jnp.int32)[:, None] * query_count + jnp.maximum(mine[..., 1], 0)
    ).reshape(-1)
    asked = jnp.take(query_block, query_table, axis=0)
    chosen = jnp.take(passages, slot_table, axis=0)
    pair_scored = jnp.einsum("ntd,npd->ntp", asked, chosen, preferred_element_type=jnp.float32)
    token_index = lax.axis_index("cent") * token_rows + jnp.arange(token_rows, dtype=jnp.int32)
    valid_tokens = token_index[None, :] < jnp.take(lengths, slot_table, axis=0)[:, None]
    pair_scored = jnp.where(valid_tokens[:, None, :], pair_scored, masked_score)
    partial_value = jnp.max(pair_scored, axis=2)

    merged = jnp.concatenate([shard_best, partial_value], axis=0)
    cent_total = lax.axis_size("cent")
    step = 1
    while step < cent_total:
        partner = [(i, i ^ step) for i in range(cent_total)]
        merged = jnp.maximum(merged, lax.ppermute(merged, "cent", partner))
        step *= 2
    token_best = merged[:query_count]
    complete = merged[query_count:]
    pair_scores = (jnp.sum(complete, axis=1) / query_tokens).reshape(shard_total, capacity)
    returned = lax.all_to_all(pair_scores, ("chip", "core"), split_axis=0, concat_axis=0, tiled=True)

    scores = jnp.take(returned.reshape(-1), my_places, axis=0).reshape(query_count, per_query)
    return (token_best, scores)


def solution(mesh):
    shard_size, cent_size = mesh.devices.shape
    split_mesh = Mesh(mesh.devices.reshape(shard_size // 2, 2, cent_size), ("chip", "core", "cent"))
    shard = ("chip", "core")
    in_specs = (
        P(shard, None, None),
        P((*shard, "cent"), None),
        P(shard, "cent", None),
        P(shard),
        P(),
        P(shard, None),
    )
    out_specs = (P(shard, None), P(shard, None))
    return jax.shard_map(
        per_device, mesh=split_mesh, in_specs=in_specs, out_specs=out_specs, check_vma=False
    )
```

time: 241 us -> 261 us (1.083)
  blocking collectives: 0 us -> 47.7 us
  local copies, waits for them, and re-layouts: 66.4 us -> 31.2 us
  other arithmetic: 4.51 us -> 15.1 us
  waiting for transfers between devices: 107 us -> 99.4 us
  starting transfers between devices: 22.5 us -> 26 us
    all_gather x0 -> x1, blocking collectives: none -> 47.7 us  [per_device(): tables = lax.all_gather(table, ('chip', 'core'), axis=0, tiled=False)]
    another operation x2, local copies, waits for them, and re-layouts: 13.5 us -> 0.06 us  [the longest x1 0.05 us: per_device(): jnp.stack([jnp.where(my_core == 0, best_same, best_other), jnp.where(my_c...]
    another operation x3 -> x6, other arithmetic: 0.66 us -> 12 us  [the longest x2 11.3 us: per_device(): jnp.stack([first, second], axis=1).reshape(-1, query_tokens, feature_width)]
    slice x5 -> x1, local copies, waits for them, and re-layouts: 11.4 us -> 0.18 us  [the longest x1 7.7 us: per_device(): packed_block[:, :query_count].reshape(-1, query_tokens, feature_width)]
    unnamed x14 -> x12, local copies, waits for them, and re-layouts: 12.8 us -> 2.02 us
    all_gather x1, waiting for transfers between devices: 93.5 us -> 84.7 us  [per_device(): same_core = lax.all_gather(queries, 'chip', axis=0, tiled=False)]
    ppermute x0 -> x1, starting transfers between devices: none -> 4.21 us  [per_device(): lax.ppermute(same_core, 'core', [(i, (i + 1) % core_total) for i in range...]
    dot_general x1 -> x2, matrix products: 17.1 us -> 18.3 us  [block_best(): jnp.einsum('rd,cd->rc', block.reshape(-1, feature_width), centroids, pref...]
  transfers between devices with their start and end apart: 5 -> 6, of which waited for: 4 -> 4; matrix products, arithmetic and copies ran while one was open for 7% -> 22% of each run, Pallas kernels for 0% -> 0%
where the time goes in v3:
time: 261 us; the launch traced here: 260 us
  waiting for transfers between devices  99.4 us (38%)
  blocking collectives  47.7 us (18%)
  local copies, waits for them, and re-layouts  31.2 us (12%)
  matrix products  26.6 us (10%)
  starting transfers between devices  26 us (10%)
  other arithmetic  15.1 us (6%)
  between operations  14.4 us (6%)
    all_gather x1, waiting for transfers between devices, per_device(): same_core = lax.all_gather(queries, 'chip', axis=0, tiled=False)  84.7 us
    all_gather x1, blocking collectives, per_device(): tables = lax.all_gather(table, ('chip', 'core'), axis=0, tiled=False)  47.7 us
    dot_general x2, matrix products, block_best(): jnp.einsum('rd,cd->rc', block.reshape(-1, feature_width), centroids, pref...  18.3 us
    all_to_all x1, starting transfers between devices, per_device(): lax.all_to_all(pair_scores, ('chip', 'core'), split_axis=0, concat_axis=0...  12.4 us
    another operation x2, other arithmetic, per_device(): jnp.stack([first, second], axis=1).reshape(-1, query_tokens, feature_width)  11.3 us
    all_to_all x1, waiting for transfers between devices, per_device(): lax.all_to_all(pair_scores, ('chip', 'core'), split_axis=0, concat_axis=0...  8.46 us
    dot_general x1, matrix products, per_device(): jnp.einsum('ntd,npd->ntp', asked, chosen, preferred_element_type=jnp.floa...  8.31 us
    gather x1, local copies, waits for them, and re-layouts, per_device(): asked = jnp.take(query_block, query_table, axis=0)  8.29 us
  transfers between devices with their start and end apart: 6, of which 4 were waited for; matrix products, arithmetic and copies ran while one was open for 22% of the time, Pallas kernels for 0%

profile of v3, /device:TPU:1, one launch (start us, length us, event | category | flops | bytes accessed | tf_op | source)
XLA Modules:
  0.0 260.4 jit_solution(3005330066560406726)
XLA Ops:
  7.9 84.7 %all-gather.4.cloned.1.call-done = bf16[512,32,128]{2,1,0:T(8,128)(2,1)} async-done(((bf16[16,32,128]{2,1,0:T(8,128)(2,1)}), bf16[512,32,128]{2,1,0:T(8,128)(2,1)}) %all-gather.4.cloned.1.call-update) | async-done | bytes 4194320 | tf_op jit(solution)/shard_map/all_gather | solution.py:38
  92.7 4.2 %collective-permute-start = (bf16[32,16,32,128]{3,2,1,0:T(8,128)(2,1)}, bf16[32,16,32,128]{3,2,1,0:T(8,128)(2,1)}, u32[]{:S(2)}, u32[]{:S(2)}) collective-permute-start(bf16[32,16,32,128]{3,2,1,0:T(8,128)(2,1)} %bitcast.57), channel_id=1, source_target_pairs={{0,4},{4,0},{1,5},{5,1},{2,6},{6,2},{3,7},{7,3},{8,12},{12,8},{9,1... | collective-permute-start | bytes 12582920 | tf_op jit(solution)/shard_map/ppermute | solution.py:39
  97.6 0.8 reshape.431
  99.5 2.1 gather_fusion
  102.8 1.2 scatter_custom_fusion
  104.3 47.7 %all-gather.1 = bf16[64,1,1536]{2,1,0:T(2,128)(2,1)S(1)} all-gather(bf16[1,1,1536]{2,1,0:T(2,128)(2,1)S(1)} %reshape.490), channel_id=1, replica_groups=mesh['chip'=32,'core'=2,'cent'=4] {'chip','core'}, dimensions={0}, use_global_device_ids=true | all-gather | bytes 199680 | tf_op jit(solution)/shard_map/all_gather | solution.py:33
  153.4 5.0 %gather_fusion.1 = s32[768]{0:T(1024)S(1)} fusion(s32[256]{0:T(256)S(1)} %copy-done.1, s32[1024]{0:T(1024)S(1)} %pad_clamp_fusion.2), kind=kCustom, calls=%fused_computation.1 | custom fusion | bytes 9216 | tf_op jit(solution)/shard_map/jit(_take)/gather | solution.py:68
  158.4 4.5 %gather_fusion.3 = bf16[768,32,128]{2,1,0:T(8,128)(2,1)} fusion(bf16[256,32,128]{2,1,0:T(8,128)(2,1)S(1)} %copy-done, s32[1024]{0:T(1024)S(1)} %pad_clamp_fusion.2), kind=kCustom, calls=%fused_computation.3 | custom fusion | bytes 12585984 | tf_op jit(solution)/shard_map/jit(_take)/gather | solution.py:65
  163.1 9.1 %convolution_reduce_fusion.1 = f32[16384]{0:T(1024)S(1)} fusion(bf16[16384,128]{1,0:T(8,128)(2,1)} %bitcast.58, bf16[768,128]{1,0:T(8,128)(2,1)S(1)} %copy-done.3), kind=kOutput, calls=%fused_computation.9 | convolution fusion | flops 3233792000 | bytes 4456448 | tf_op jit(solution)/shard_map/rd,cd->rc/dot_general | solution.py:47
  172.3 9.1 %convolution_reduce_fusion = f32[16384]{0:T(1024)S(1)} fusion(bf16[16384,128]{1,0:T(8,128)(2,1)} %bitcast.2, bf16[768,128]{1,0:T(8,128)(2,1)S(1)} %copy-done.3), kind=kOutput, calls=%fused_computation.8 | convolution fusion | flops 3233792000 | bytes 4456448 | tf_op jit(solution)/shard_map/rd,cd->rc/dot_general | solution.py:47
  181.8 0.9 reshape.507
  182.7 5.3 %all-to-all-start = ((f32[64,1,512]{2,1,0:T(1,128)}), f32[64,1,512]{2,1,0:T(1,128)S(1)}, u32[]{:S(2)}, u32[]{:S(2)}) async-start(f32[64,1,512]{2,1,0:T(1,128)} %reshape.507), calls=%async_computation | async-start | bytes 262144 | tf_op jit(solution)/shard_map/all_to_all | solution.py:57
  188.0 5.1 %select_bitcast_fusion.1 = (bf16[32,1,16,32,128]{4,3,2,1,0:T(8,128)(2,1)S(1)}, bf16[32,1,16,32,128]{4,3,2,1,0:T(8,128)(2,1)}) fusion(bf16[32,16,32,128]{3,2,1,0:T(8,128)(2,1)} %bitcast.59, bf16[32,16,32,128]{3,2,1,0:T(8,128)(2,1)} %collective-permute-done, pred[]{:T(512)S(6)} %eq.29), kind=kLoop, calls=%fused_computation.16 | loop fusion | flops 4194304 | bytes 16777216 | tf_op jit(solution)/shard_map/stack | solution.py:44
  193.1 6.2 %pad_maximum_fusion = bf16[32,2,16,32,128]{4,3,2,1,0:T(8,128)(2,1)} fusion(bf16[32,1,16,32,128]{4,3,2,1,0:T(8,128)(2,1)} %get-tuple-element.13, bf16[32,1,16,32,128]{4,3,2,1,0:T(8,128)(2,1)S(1)} %get-tuple-element.12), kind=kLoop, calls=%fused_computation.7 | loop fusion | flops 4194304 | bytes 16777216 | tf_op jit(solution)/shard_map/stack | solution.py:44
  199.3 8.3 %gather_fusion.2 = bf16[768,32,128]{2,1,0:T(8,128)(2,1)} fusion(bf16[1024,32,128]{2,1,0:T(8,128)(2,1)} %bitcast.56, s32[1024]{0:T(1024)S(1)} %pad_clamp_fusion.1), kind=kCustom, calls=%fused_computation.2 | custom fusion | bytes 12585984 | tf_op jit(solution)/shard_map/jit(_take)/gather | solution.py:64
  207.6 8.3 %select_reduce_fusion = f32[768,32]{1,0:T(8,128)S(1)} fusion(pred[768,32]{1,0:T(8,128)(4,1)S(1)} %broadcast_compare_fusion, bf16[768,32,128]{2,1,0:T(8,128)(2,1)} %gather_fusion.3, pred[768]{0:T(1024)(128)(4,1)S(1)} %le.94, bf16[768,32,128]{2,1,0:T(8,128)(2,1)} %gather_fusion.2, pred[768]{0:T(1024)(128)(4,1)S(1)} %compare_and_fusion), kind=kOutput, calls=%fused_computation.6 | convolution fusion | flops 209166336 | bytes 12707328 | tf_op jit(solution)/shard_map/ntd,npd->ntp/dot_general | solution.py:66
  216.6 0.9 reduce.8
  218.0 1.3 collective-permute-start.1
  219.2 3.1 %collective-permute-done.1 = f32[784,32]{0,1:T(8,128)S(1)} collective-permute-done((f32[784,32]{0,1:T(8,128)S(1)}, f32[784,32]{0,1:T(8,128)S(1)}, u32[]{:S(2)}, u32[]{:S(2)}) %collective-permute-start.1) | collective-permute-done | bytes 100384 | tf_op jit(solution)/shard_map/ppermute | solution.py:77
  222.4 2.8 %collective-permute-start.2 = (f32[784,32]{0,1:T(8,128)S(1)}, f32[784,32]{0,1:T(8,128)S(1)}, u32[]{:S(2)}, u32[]{:S(2)}) collective-permute-start(f32[784,32]{0,1:T(8,128)S(1)} %fusion.24), channel_id=1, source_target_pairs={{0,2},{1,3},{2,0},{3,1},{4,6},{5,7},{6,4},{7,5},{8,10},{9,11},{10,... | collective-permute-start | bytes 301064 | tf_op jit(solution)/shard_map/ppermute | solution.py:77
  225.2 2.4 collective-permute-done.2
  228.5 12.4 %all-to-all-start.1 = ((f32[64,1,12]{2,1,0:T(1,128)}), f32[64,1,12]{2,1,0:T(1,128)S(1)}, u32[]{:S(2)}, u32[]{:S(2)}) async-start(f32[64,1,12]{2,1,0:T(1,128)} %bitcast.17), calls=%async_computation.1 | async-start | bytes 65536 | tf_op jit(solution)/shard_map/all_to_all | solution.py:82
  241.7 8.5 %all-to-all-done.1 = f32[64,1,12]{2,1,0:T(1,128)S(1)} async-done(((f32[64,1,12]{2,1,0:T(1,128)}), f32[64,1,12]{2,1,0:T(1,128)S(1)}, u32[]{:S(2)}, u32[]{:S(2)}) %all-to-all-start.1) | async-done | bytes 3104 | tf_op jit(solution)/shard_map/all_to_all | solution.py:82
  251.5 1.4 gather_fusion.4
  (77 shorter events, 10.6 us)
Async XLA Ops:
  7.2 151.2 %copy-start = (bf16[256,32,128]{2,1,0:T(8,128)(2,1)S(1)}, bf16[256,32,128]{2,1,0:T(8,128)(2,1)}, u32[]{:S(2)}) copy-start(bf16[256,32,128]{2,1,0:T(8,128)(2,1)} %param.8) | copy-start | bytes 6291460
  7.2 146.2 %copy-start.1 = (s32[256]{0:T(256)S(1)}, s32[256]{0:T(256)}, u32[]{:S(2)}) copy-start(s32[256]{0:T(256)} %param.9) | copy-start | bytes 3076
  7.2 85.5 %all-gather.4.cloned.1.call-start = ((), (), s32[]{:S(2)}) async-start(), calls=%async_computation.2 | async-start | bytes 4325376 | tf_op jit(solution)/shard_map/all_gather | solution.py:38
  92.7 79.6 %collective-permute-start = (bf16[32,16,32,128]{3,2,1,0:T(8,128)(2,1)}, bf16[32,16,32,128]{3,2,1,0:T(8,128)(2,1)}, u32[]{:S(2)}, u32[]{:S(2)}) collective-permute-start(bf16[32,16,32,128]{3,2,1,0:T(8,128)(2,1)} %bitcast.57), channel_id=1, source_target_pairs={{0,4},{4,0},{1,5},{5,1},{2,6},{6,2},{3,7},{7,3},{8,12},{12,8},{9,1... | collective-permute-start | bytes 12582920 | tf_op jit(solution)/shard_map/ppermute | solution.py:39
  158.4 4.8 %copy-start.3 = (bf16[768,128]{1,0:T(8,128)(2,1)S(1)}, bf16[768,128]{1,0:T(8,128)(2,1)}, u32[]{:S(2)}) copy-start(bf16[768,128]{1,0:T(8,128)(2,1)} %param.7) | copy-start | bytes 589828
  182.7 33.4 %all-to-all-start = ((f32[64,1,512]{2,1,0:T(1,128)}), f32[64,1,512]{2,1,0:T(1,128)S(1)}, u32[]{:S(2)}, u32[]{:S(2)}) async-start(f32[64,1,512]{2,1,0:T(1,128)} %reshape.507), calls=%async_computation | async-start | bytes 262144 | tf_op jit(solution)/shard_map/all_to_all | solution.py:57
  207.6 45.4 %copy-start.2 = (s32[16,16]{1,0:T(8,128)S(1)}, s32[16,16]{1,0:T(8,128)}, u32[]{:S(2)}) copy-start(s32[16,16]{1,0:T(8,128)} %param.11) | copy-start | bytes 3076
  218.0 4.3 %collective-permute-start.1 = (f32[784,32]{0,1:T(8,128)S(1)}, f32[784,32]{0,1:T(8,128)S(1)}, u32[]{:S(2)}, u32[]{:S(2)}) collective-permute-start(f32[784,32]{0,1:T(8,128)S(1)} %pad_maximum_fusion.2), channel_id=1, source_target_pairs={{0,1},{1,0},{2,3},{3,2},{4,5},{5,4},{6,7},{7,6},{8,9},{9,8},{10,11... | collective-permute-start | bytes 301064 | tf_op jit(solution)/shard_map/ppermute | solution.py:77
  222.4 5.2 %collective-permute-start.2 = (f32[784,32]{0,1:T(8,128)S(1)}, f32[784,32]{0,1:T(8,128)S(1)}, u32[]{:S(2)}, u32[]{:S(2)}) collective-permute-start(f32[784,32]{0,1:T(8,128)S(1)} %fusion.24), channel_id=1, source_target_pairs={{0,2},{1,3},{2,0},{3,1},{4,6},{5,7},{6,4},{7,5},{8,10},{9,11},{10,... | collective-permute-start | bytes 301064 | tf_op jit(solution)/shard_map/ppermute | solution.py:77
  228.5 21.7 %all-to-all-start.1 = ((f32[64,1,12]{2,1,0:T(1,128)}), f32[64,1,12]{2,1,0:T(1,128)S(1)}, u32[]{:S(2)}, u32[]{:S(2)}) async-start(f32[64,1,12]{2,1,0:T(1,128)} %bitcast.17), calls=%async_computation.1 | async-start | bytes 65536 | tf_op jit(solution)/shard_map/all_to_all | solution.py:82
Sparse Core Ops, SparseCore 0:
  10.6 82.0 all-gather.3

commit v4 on v2

--- a/solution.py
+++ b/solution.py
@@ -26,20 +26,18 @@
     ranking = jnp.sum((jnp.cumsum(onehot, axis=0) - onehot) * onehot, axis=1)
     my_places = owners * capacity + ranking
     pair_local = jnp.arange(pairs_here, dtype=jnp.int32) // per_query
-    entries = jnp.stack([pair_rows % passage_count, pair_local], axis=1).astype(jnp.bfloat16)
-    table = jnp.full((shard_total * capacity, 2), -1.0, jnp.bfloat16).at[my_places].set(entries)
-    row_width = query_tokens * feature_width
-    table_rows = -(-(shard_total * capacity * 2) // row_width)
-    table = jnp.pad(table.reshape(-1), (0, table_rows * row_width - shard_total * capacity * 2))
+    entries = jnp.stack([pair_rows % passage_count, my_shard * query_count + pair_local], axis=1)
+    table = (
+        jnp.full((shard_total * capacity, 2), -1, jnp.int32)
+        .at[my_places]
+        .set(entries)
+        .reshape(shard_total, capacity * 2)
+    )
 
-    packed = jnp.concatenate(
-        [queries.reshape(query_count, row_width), table.reshape(table_rows, row_width)], axis=0
+    query_block = lax.all_gather(queries, "shard", axis=0, tiled=True)
+    mine = lax.all_to_all(table, "shard", split_axis=0, concat_axis=0, tiled=True).reshape(
+        shard_total, capacity, 2
     )
-    packed_block = lax.all_gather(packed, "shard", axis=0, tiled=False)
-    query_block = packed_block[:, :query_count].reshape(-1, query_tokens, feature_width)
-    tables = packed_block[:, query_count:].reshape(shard_total, -1)[:, : shard_total * capacity * 2]
-    tables = tables.reshape(shard_total, shard_total, capacity, 2)
-    mine = lax.dynamic_index_in_dim(tables, my_shard, axis=1, keepdims=False).astype(jnp.int32)
 
     flattened = query_block.reshape(-1, feature_width)
     scored = jnp.einsum("rd,cd->rc", flattened, centroids, preferred_element_type=jnp.float32)
@@ -48,9 +46,7 @@
     shard_best = jnp.max(gathered_best, axis=0)
 
     slot_table = jnp.maximum(mine[..., 0], 0).reshape(-1)
-    query_table = (
-        jnp.arange(shard_total, dtype=jnp.int32)[:, None] * query_count + jnp.maximum(mine[..., 1], 0)
-    ).reshape(-1)
+    query_table = jnp.maximum(mine[..., 1], 0).reshape(-1)
     asked = jnp.take(query_block, query_table, axis=0)
     chosen = jnp.take(passages, slot_table, axis=0)
     pair_scored = jnp.einsum("ntd,npd->ntp", asked, chosen, preferred_element_type=jnp.float32)

time: 241 us -> 184 us (0.76)
  local copies, waits for them, and re-layouts: 66.4 us -> 30.8 us
  waiting for transfers between devices: 107 us -> 73.3 us
  starting transfers between devices: 22.5 us -> 35.6 us
    all_gather x1, waiting for transfers between devices: 93.5 us -> 49.5 us  [per_device(): query_block = lax.all_gather(queries, 'shard', axis=0, tiled=True)]
    another operation x3 -> x2, local copies, waits for them, and re-layouts: 13.6 us -> 0.14 us  [the longest x1 0.13 us: per_device(): jnp.stack([pair_rows % passage_count, my_shard * query_count + pair_local...]
    all_to_all x0 -> x1, starting transfers between devices: none -> 13.1 us  [per_device(): lax.all_to_all(table, 'shard', split_axis=0, concat_axis=0, tiled=True)]
    slice x5 -> x1, local copies, waits for them, and re-layouts: 11.4 us -> 0.18 us  [the longest x1 7.7 us: per_device(): packed_block[:, :query_count].reshape(-1, query_tokens, feature_width)]
    unnamed x14 -> x9, local copies, waits for them, and re-layouts: 12.8 us -> 1.76 us
    all_to_all x0 -> x1, waiting for transfers between devices: none -> 9.3 us  [per_device(): lax.all_to_all(table, 'shard', split_axis=0, concat_axis=0, tiled=True)]
  transfers between devices with their start and end apart: 5 -> 6, of which waited for: 4 -> 5; matrix products, arithmetic and copies ran while one was open for 7% -> 19% of each run, Pallas kernels for 0% -> 0%
where the time goes in v4:
time: 184 us; the launch traced here: 183 us
  waiting for transfers between devices  73.3 us (40%)
  starting transfers between devices  35.6 us (19%)
  local copies, waits for them, and re-layouts  30.8 us (17%)
  matrix products  25.3 us (14%)
  between operations  14.3 us (8%)
  other arithmetic  3.76 us (2%)
    all_gather x1, waiting for transfers between devices, per_device(): query_block = lax.all_gather(queries, 'shard', axis=0, tiled=True)  49.5 us
    dot_general x1, matrix products, per_device(): jnp.einsum('rd,cd->rc', flattened, centroids, preferred_element_type=jnp....  17 us
    all_to_all x1, starting transfers between devices, per_device(): lax.all_to_all(table, 'shard', split_axis=0, concat_axis=0, tiled=True)  13.1 us
    all_to_all x1, starting transfers between devices, per_device(): lax.all_to_all(pair_scores, 'shard', split_axis=0, concat_axis=0, tiled=T...  12.6 us
    all_to_all x1, waiting for transfers between devices, per_device(): lax.all_to_all(table, 'shard', split_axis=0, concat_axis=0, tiled=True)  9.3 us
    all_to_all x1, waiting for transfers between devices, per_device(): lax.all_to_all(pair_scores, 'shard', split_axis=0, concat_axis=0, tiled=T...  8.46 us
    gather x1, local copies, waits for them, and re-layouts, per_device(): asked = jnp.take(query_block, query_table, axis=0)  8.3 us
    dot_general x1, matrix products, per_device(): jnp.einsum('ntd,npd->ntp', asked, chosen, preferred_element_type=jnp.floa...  8.3 us
  transfers between devices with their start and end apart: 6, of which 5 were waited for; matrix products, arithmetic and copies ran while one was open for 19% of the time, Pallas kernels for 0%

profile of v4, /device:TPU:1, one launch (start us, length us, event | category | flops | bytes accessed | tf_op | source)
XLA Modules:
  0.0 183.1 jit_solution(7115414526718233200)
XLA Ops:
  7.9 0.8 reshape.364
  8.7 0.8 reshape.365
  9.5 0.8 reshape.366
  10.3 2.1 %gather_fusion = s32[256]{0:T(256)S(1)} fusion(s32[16384]{0:T(1024)} %param.10, s32[1024]{0:T(1024)S(1)} %pad_clamp_fusion.3), kind=kCustom, calls=%fused_computation | custom fusion | bytes 3072 | tf_op jit(solution)/shard_map/jit(_take)/gather | solution.py:21
  13.5 1.2 scatter_custom_fusion
  14.8 0.8 all_to_all.14
  15.6 13.1 %all-to-all-start.1 = ((s32[64,1,24]{2,1,0:T(1,128)}), s32[64,1,24]{2,1,0:T(1,128)S(1)}, u32[]{:S(2)}, u32[]{:S(2)}) async-start(s32[64,1,24]{2,1,0:T(1,128)} %bitcast.7), calls=%async_computation.1 | async-start | bytes 65536 | tf_op jit(solution)/shard_map/all_to_all | solution.py:38
  28.7 9.3 %all-to-all-done.1 = s32[64,1,24]{2,1,0:T(1,128)S(1)} async-done(((s32[64,1,24]{2,1,0:T(1,128)}), s32[64,1,24]{2,1,0:T(1,128)S(1)}, u32[]{:S(2)}, u32[]{:S(2)}) %all-to-all-start.1) | async-done | bytes 6176 | tf_op jit(solution)/shard_map/all_to_all | solution.py:38
  39.0 4.8 %gather_fusion.1 = s32[768]{0:T(1024)S(1)} fusion(s32[256]{0:T(256)} %param.9, s32[1024]{0:T(1024)S(1)} %pad_clamp_fusion.2), kind=kCustom, calls=%fused_computation.1 | custom fusion | bytes 9216 | tf_op jit(solution)/shard_map/jit(_take)/gather | solution.py:54
  43.9 4.5 %gather_fusion.3 = bf16[768,32,128]{2,1,0:T(8,128)(2,1)} fusion(bf16[256,32,128]{2,1,0:T(8,128)(2,1)S(1)} %copy-done, s32[1024]{0:T(1024)S(1)} %pad_clamp_fusion.2), kind=kCustom, calls=%fused_computation.3 | custom fusion | bytes 12585984 | tf_op jit(solution)/shard_map/jit(_take)/gather | solution.py:51
  48.6 49.5 %all-gather.2.cloned.1.call-done = bf16[1024,32,128]{2,1,0:T(8,128)(2,1)} async-done(((bf16[16,32,128]{2,1,0:T(8,128)(2,1)}), bf16[1024,32,128]{2,1,0:T(8,128)(2,1)}) %all-gather.2.cloned.1.call-update) | async-done | bytes 8388624 | tf_op jit(solution)/shard_map/all_gather | solution.py:37
  98.1 17.0 %convolution_reduce_fusion = f32[32768]{0:T(1024)S(1)} fusion(bf16[32768,128]{1,0:T(8,128)(2,1)} %bitcast.42, bf16[768,128]{1,0:T(8,128)(2,1)S(1)} %copy-done.2), kind=kOutput, calls=%fused_computation.6 | convolution fusion | flops 6467584000 | bytes 8716288 | tf_op jit(solution)/shard_map/rd,cd->rc/dot_general | solution.py:43
  115.3 0.9 reshape.433
  116.2 5.7 %all-to-all-start = ((f32[64,1,512]{2,1,0:T(1,128)}), f32[64,1,512]{2,1,0:T(1,128)S(1)}, u32[]{:S(2)}, u32[]{:S(2)}) async-start(f32[64,1,512]{2,1,0:T(1,128)} %reshape.433), calls=%async_computation | async-start | bytes 262144 | tf_op jit(solution)/shard_map/all_to_all | solution.py:45
  122.0 8.3 %gather_fusion.2 = bf16[768,32,128]{2,1,0:T(8,128)(2,1)} fusion(bf16[1024,32,128]{2,1,0:T(8,128)(2,1)} %all-gather.2.cloned.1.call-done, s32[1024]{0:T(1024)S(1)} %pad_clamp_fusion.1), kind=kCustom, calls=%fused_computation.2 | custom fusion | bytes 12585984 | tf_op jit(solution)/shard_map/jit(_take)/gather | solution.py:50
  130.2 8.3 %select_reduce_fusion = f32[768,32]{1,0:T(8,128)S(1)} fusion(pred[768,32]{1,0:T(8,128)(4,1)S(1)} %broadcast_compare_fusion, bf16[768,32,128]{2,1,0:T(8,128)(2,1)} %gather_fusion.3, pred[768]{0:T(1024)(128)(4,1)S(1)} %le.97, bf16[768,32,128]{2,1,0:T(8,128)(2,1)} %gather_fusion.2, pred[768]{0:T(1024)(128)(4,1)S(1)} %le.100), kind=kOutput, calls=%fused_computation.7 | convolution fusion | flops 209166336 | bytes 12707328 | tf_op jit(solution)/shard_map/ntd,npd->ntp/dot_general | solution.py:52
  139.2 0.9 reduce.6
  140.6 1.3 collective-permute-start
  141.9 2.9 %collective-permute-done = f32[784,32]{0,1:T(8,128)S(1)} collective-permute-done((f32[784,32]{0,1:T(8,128)S(1)}, f32[784,32]{0,1:T(8,128)S(1)}, u32[]{:S(2)}, u32[]{:S(2)}) %collective-permute-start) | collective-permute-done | bytes 100384 | tf_op jit(solution)/shard_map/ppermute | solution.py:63
  144.9 2.8 %collective-permute-start.1 = (f32[784,32]{0,1:T(8,128)S(1)}, f32[784,32]{0,1:T(8,128)S(1)}, u32[]{:S(2)}, u32[]{:S(2)}) collective-permute-start(f32[784,32]{0,1:T(8,128)S(1)} %fusion.22), channel_id=1, source_target_pairs={{0,2},{1,3},{2,0},{3,1},{4,6},{5,7},{6,4},{7,5},{8,10},{9,11},{10,... | collective-permute-start | bytes 301064 | tf_op jit(solution)/shard_map/ppermute | solution.py:63
  147.7 2.4 %collective-permute-done.1 = f32[784,32]{0,1:T(8,128)S(1)} collective-permute-done((f32[784,32]{0,1:T(8,128)S(1)}, f32[784,32]{0,1:T(8,128)S(1)}, u32[]{:S(2)}, u32[]{:S(2)}) %collective-permute-start.1) | collective-permute-done | bytes 100384 | tf_op jit(solution)/shard_map/ppermute | solution.py:63
  150.9 12.6 %all-to-all-start.2 = ((f32[64,1,12]{2,1,0:T(1,128)}), f32[64,1,12]{2,1,0:T(1,128)S(1)}, u32[]{:S(2)}, u32[]{:S(2)}) async-start(f32[64,1,12]{2,1,0:T(1,128)} %bitcast.9), calls=%async_computation.2 | async-start | bytes 65536 | tf_op jit(solution)/shard_map/all_to_all | solution.py:68
  164.4 8.5 %all-to-all-done.2 = f32[64,1,12]{2,1,0:T(1,128)S(1)} async-done(((f32[64,1,12]{2,1,0:T(1,128)}), f32[64,1,12]{2,1,0:T(1,128)S(1)}, u32[]{:S(2)}, u32[]{:S(2)}) %all-to-all-start.2) | async-done | bytes 3104 | tf_op jit(solution)/shard_map/all_to_all | solution.py:68
  174.2 1.4 gather_fusion.4
  (61 shorter events, 8.1 us)
Async XLA Ops:
  7.2 36.7 %copy-start = (bf16[256,32,128]{2,1,0:T(8,128)(2,1)S(1)}, bf16[256,32,128]{2,1,0:T(8,128)(2,1)}, u32[]{:S(2)}) copy-start(bf16[256,32,128]{2,1,0:T(8,128)(2,1)} %param.8) | copy-start | bytes 6291460
  7.2 90.9 %all-gather.2.cloned.1.call-start = ((), (), s32[]{:S(2)}) async-start(), calls=%async_computation.3 | async-start | bytes 8519680 | tf_op jit(solution)/shard_map/all_gather | solution.py:37
  15.6 22.5 %all-to-all-start.1 = ((s32[64,1,24]{2,1,0:T(1,128)}), s32[64,1,24]{2,1,0:T(1,128)S(1)}, u32[]{:S(2)}, u32[]{:S(2)}) async-start(s32[64,1,24]{2,1,0:T(1,128)} %bitcast.7), calls=%async_computation.1 | async-start | bytes 65536 | tf_op jit(solution)/shard_map/all_to_all | solution.py:38
  43.9 54.2 %copy-start.2 = (bf16[768,128]{1,0:T(8,128)(2,1)S(1)}, bf16[768,128]{1,0:T(8,128)(2,1)}, u32[]{:S(2)}) copy-start(bf16[768,128]{1,0:T(8,128)(2,1)} %param.7) | copy-start | bytes 589828
  116.2 22.5 %all-to-all-start = ((f32[64,1,512]{2,1,0:T(1,128)}), f32[64,1,512]{2,1,0:T(1,128)S(1)}, u32[]{:S(2)}, u32[]{:S(2)}) async-start(f32[64,1,512]{2,1,0:T(1,128)} %reshape.433), calls=%async_computation | async-start | bytes 262144 | tf_op jit(solution)/shard_map/all_to_all | solution.py:45
  130.2 45.4 %copy-start.1 = (s32[16,16]{1,0:T(8,128)S(1)}, s32[16,16]{1,0:T(8,128)}, u32[]{:S(2)}) copy-start(s32[16,16]{1,0:T(8,128)} %param.11) | copy-start | bytes 3076
  140.6 4.2 %collective-permute-start = (f32[784,32]{0,1:T(8,128)S(1)}, f32[784,32]{0,1:T(8,128)S(1)}, u32[]{:S(2)}, u32[]{:S(2)}) collective-permute-start(f32[784,32]{0,1:T(8,128)S(1)} %pad_maximum_fusion), channel_id=1, source_target_pairs={{0,1},{1,0},{2,3},{3,2},{4,5},{5,4},{6,7},{7,6},{8,9},{9,8},{10,11... | collective-permute-start | bytes 301064 | tf_op jit(solution)/shard_map/ppermute | solution.py:63
  144.9 5.2 %collective-permute-start.1 = (f32[784,32]{0,1:T(8,128)S(1)}, f32[784,32]{0,1:T(8,128)S(1)}, u32[]{:S(2)}, u32[]{:S(2)}) collective-permute-start(f32[784,32]{0,1:T(8,128)S(1)} %fusion.22), channel_id=1, source_target_pairs={{0,2},{1,3},{2,0},{3,1},{4,6},{5,7},{6,4},{7,5},{8,10},{9,11},{10,... | collective-permute-start | bytes 301064 | tf_op jit(solution)/shard_map/ppermute | solution.py:63
  150.9 21.9 %all-to-all-start.2 = ((f32[64,1,12]{2,1,0:T(1,128)}), f32[64,1,12]{2,1,0:T(1,128)S(1)}, u32[]{:S(2)}, u32[]{:S(2)}) async-start(f32[64,1,12]{2,1,0:T(1,128)} %bitcast.9), calls=%async_computation.2 | async-start | bytes 65536 | tf_op jit(solution)/shard_map/all_to_all | solution.py:68
Sparse Core Ops, SparseCore 0:
  10.8 87.2 all-gather.1

commit v5 on v4

--- a/solution.py
+++ b/solution.py
@@ -1,9 +1,12 @@
 import jax
 import jax.numpy as jnp
 from jax import lax
-from jax.sharding import PartitionSpec as P
+from jax.sharding import Mesh, PartitionSpec as P
 
 masked_score = -1e30
+
+
+shard = ("y", "rest")
 
 
 def per_device(queries, centroids, passages, lengths, passage_row, candidates):
@@ -13,10 +16,10 @@
     per_query = candidates.shape[1]
     passage_count = passages.shape[0]
     token_rows = passages.shape[1]
-    shard_total = lax.axis_size("shard")
+    shard_total = lax.axis_size(shard)
     capacity = max(2, 3 * query_count * per_query // shard_total)
     pairs_here = query_count * per_query
-    my_shard = lax.axis_index("shard")
+    my_shard = lax.axis_index(shard)
 
     pair_rows = jnp.take(passage_row, candidates.reshape(-1), axis=0)
     owners = pair_rows // passage_count
@@ -34,19 +37,32 @@
         .reshape(shard_total, capacity * 2)
     )
 
-    query_block = lax.all_gather(queries, "shard", axis=0, tiled=True)
-    mine = lax.all_to_all(table, "shard", split_axis=0, concat_axis=0, tiled=True).reshape(
+    query_block = lax.all_gather(
+        lax.all_gather(queries, "y", axis=0, tiled=True), "rest", axis=0, tiled=True
+    )
+    y_total = lax.axis_size("y")
+    rest_total = lax.axis_size("rest")
+    mine = lax.all_to_all(table, shard, split_axis=0, concat_axis=0, tiled=True).reshape(
         shard_total, capacity, 2
     )
 
     flattened = query_block.reshape(-1, feature_width)
     scored = jnp.einsum("rd,cd->rc", flattened, centroids, preferred_element_type=jnp.float32)
-    local_best = jnp.max(scored, axis=1).reshape(shard_total, query_count, query_tokens)
-    gathered_best = lax.all_to_all(local_best, "shard", split_axis=0, concat_axis=0, tiled=True)
+    local_best = (
+        jnp.max(scored, axis=1)
+        .reshape(rest_total, y_total, query_count, query_tokens)
+        .transpose(1, 0, 2, 3)
+        .reshape(shard_total, query_count, query_tokens)
+    )
+    gathered_best = lax.all_to_all(local_best, shard, split_axis=0, concat_axis=0, tiled=True)
     shard_best = jnp.max(gathered_best, axis=0)
 
     slot_table = jnp.maximum(mine[..., 0], 0).reshape(-1)
-    query_table = jnp.maximum(mine[..., 1], 0).reshape(-1)
+    global_query = jnp.maximum(mine[..., 1], 0).reshape(-1)
+    source_shard = global_query // query_count
+    query_table = (
+        (source_shard % rest_total) * y_total + source_shard // rest_total
+    ) * query_count + global_query % query_count
     asked = jnp.take(query_block, query_table, axis=0)
     chosen = jnp.take(passages, slot_table, axis=0)
     pair_scored = jnp.einsum("ntd,npd->ntp", asked, chosen, preferred_element_type=jnp.float32)
@@ -65,22 +81,27 @@
     token_best = merged[:query_count]
     complete = merged[query_count:]
     pair_scores = (jnp.sum(complete, axis=1) / query_tokens).reshape(shard_total, capacity)
-    returned = lax.all_to_all(pair_scores, "shard", split_axis=0, concat_axis=0, tiled=True)
+    returned = lax.all_to_all(pair_scores, shard, split_axis=0, concat_axis=0, tiled=True)
 
     scores = jnp.take(returned.reshape(-1), my_places, axis=0).reshape(query_count, per_query)
     return (token_best, scores)
 
 
 def solution(mesh):
+    shard_size, cent_size = mesh.devices.shape
+    y_size = len({d.coords[1] for d in mesh.devices.flat})
+    split_mesh = Mesh(
+        mesh.devices.reshape(y_size, shard_size // y_size, cent_size), ("y", "rest", "cent")
+    )
     in_specs = (
-        P("shard", None, None),
-        P(("shard", "cent"), None),
-        P("shard", "cent", None),
-        P("shard"),
+        P(shard, None, None),
+        P((*shard, "cent"), None),
+        P(shard, "cent", None),
+        P(shard),
         P(),
-        P("shard", None),
+        P(shard, None),
     )
-    out_specs = (P("shard", None), P("shard", None))
+    out_specs = (P(shard, None), P(shard, None))
     return jax.shard_map(
-        per_device, mesh=mesh, in_specs=in_specs, out_specs=out_specs, check_vma=False
+        per_device, mesh=split_mesh, in_specs=in_specs, out_specs=out_specs, check_vma=False
     )

time: 184 us -> 169 us (0.918)
  waiting for transfers between devices: 73.3 us -> 42.5 us
  blocking collectives: 0 us -> 13.4 us
  starting transfers between devices: 35.6 us -> 37.7 us
    all_gather x1, waiting for transfers between devices: 49.5 us -> 19.1 us  [per_device(): lax.all_gather(lax.all_gather(queries, 'y', axis=0, tiled=True), 'rest',...]
    all_gather x0 -> x1, blocking collectives: none -> 13.4 us  [per_device(): lax.all_gather(queries, 'y', axis=0, tiled=True)]
    all_to_all x3, starting transfers between devices: 31.4 us -> 33.6 us  [the longest x1 13.5 us: per_device(): lax.all_to_all(table, shard, split_axis=0, concat_axis=0, tiled=True)]
  transfers between devices with their start and end apart: 6 -> 6, of which waited for: 5 -> 5; matrix products, arithmetic and copies ran while one was open for 19% -> 21% of each run, Pallas kernels for 0% -> 0%
where the time goes in v5:
time: 169 us
  waiting for transfers between devices  42.5 us (25%)
  starting transfers between devices  37.7 us (22%)
  local copies, waits for them, and re-layouts  31.6 us (19%)
  matrix products  25.5 us (15%)
  between operations  14.4 us (9%)
  blocking collectives  13.4 us (8%)
  other arithmetic  3.86 us (2%)
    all_gather x1, waiting for transfers between devices, per_device(): lax.all_gather(lax.all_gather(queries, 'y', axis=0, tiled=True), 'rest',...  19.1 us
    dot_general x1, matrix products, per_device(): jnp.einsum('rd,cd->rc', flattened, centroids, preferred_element_type=jnp....  17.2 us
    all_to_all x1, starting transfers between devices, per_device(): lax.all_to_all(table, shard, split_axis=0, concat_axis=0, tiled=True)  13.5 us
    all_gather x1, blocking collectives, per_device(): lax.all_gather(queries, 'y', axis=0, tiled=True)  13.4 us
    all_to_all x1, starting transfers between devices, per_device(): lax.all_to_all(pair_scores, shard, split_axis=0, concat_axis=0, tiled=True)  12.6 us
    all_to_all x1, waiting for transfers between devices, per_device(): lax.all_to_all(table, shard, split_axis=0, concat_axis=0, tiled=True)  9.58 us
    all_to_all x1, waiting for transfers between devices, per_device(): lax.all_to_all(pair_scores, shard, split_axis=0, concat_axis=0, tiled=True)  8.46 us
    gather x1, local copies, waits for them, and re-layouts, per_device(): asked = jnp.take(query_block, query_table, axis=0)  8.3 us
  transfers between devices with their start and end apart: 6, of which 5 were waited for; matrix products, arithmetic and copies ran while one was open for 21% of the time, Pallas kernels for 0%

profile of v5, /device:TPU:1, one launch (start us, length us, event | category | flops | bytes accessed | tf_op | source)
XLA Modules:
  0.0 168.9 jit_solution(1618512273172525122)
XLA Ops:
  7.2 13.4 %all_gather.6 = bf16[64,32,128]{2,1,0:T(8,128)(2,1)} all-gather(bf16[16,32,128]{2,1,0:T(8,128)(2,1)} %param.6), channel_id=1, replica_groups=mesh['y'=4,'rest'=16,'cent'=4] {'y'}, dimensions={0}, use_global_device_ids=true | all-gather | bytes 655360 | tf_op jit(solution)/shard_map/all_gather | solution.py:41
  20.6 0.8 reshape.503
  21.4 0.8 reshape.504
  22.2 0.8 reshape.505
  23.0 2.1 %gather_fusion = s32[256]{0:T(256)S(1)} fusion(s32[16384]{0:T(1024)} %param.10, s32[1024]{0:T(1024)S(1)} %pad_clamp_fusion.3), kind=kCustom, calls=%fused_computation | custom fusion | bytes 3072 | tf_op jit(solution)/shard_map/jit(_take)/gather | solution.py:24
  26.3 1.2 scatter_custom_fusion
  28.3 13.5 %all-to-all-start.1 = ((s32[64,1,24]{2,1,0:T(1,128)}), s32[64,1,24]{2,1,0:T(1,128)S(1)}, u32[]{:S(2)}, u32[]{:S(2)}) async-start(s32[64,1,24]{2,1,0:T(1,128)} %bitcast.9), calls=%async_computation.1 | async-start | bytes 65536 | tf_op jit(solution)/shard_map/all_to_all | solution.py:45
  41.8 9.6 %all-to-all-done.1 = s32[64,1,24]{2,1,0:T(1,128)S(1)} async-done(((s32[64,1,24]{2,1,0:T(1,128)}), s32[64,1,24]{2,1,0:T(1,128)S(1)}, u32[]{:S(2)}, u32[]{:S(2)}) %all-to-all-start.1) | async-done | bytes 6176 | tf_op jit(solution)/shard_map/all_to_all | solution.py:45
  52.9 5.0 %gather_fusion.1 = s32[768]{0:T(1024)S(1)} fusion(s32[256]{0:T(256)S(1)} %copy-done.1, s32[1024]{0:T(1024)S(1)} %pad_clamp_fusion.2), kind=kCustom, calls=%fused_computation.1 | custom fusion | bytes 9216 | tf_op jit(solution)/shard_map/jit(_take)/gather | solution.py:70
  57.9 4.5 %gather_fusion.3 = bf16[768,32,128]{2,1,0:T(8,128)(2,1)} fusion(bf16[256,32,128]{2,1,0:T(8,128)(2,1)S(1)} %copy-done, s32[1024]{0:T(1024)S(1)} %pad_clamp_fusion.2), kind=kCustom, calls=%fused_computation.3 | custom fusion | bytes 12585984 | tf_op jit(solution)/shard_map/jit(_take)/gather | solution.py:67
  62.7 19.1 %all-gather.2.cloned.1.call-done = bf16[1024,32,128]{2,1,0:T(8,128)(2,1)} async-done(((bf16[64,32,128]{2,1,0:T(8,128)(2,1)}), bf16[1024,32,128]{2,1,0:T(8,128)(2,1)}) %all-gather.2.cloned.1.call-update) | async-done | bytes 8388624 | tf_op jit(solution)/shard_map/all_gather | solution.py:40
  81.8 17.2 %convolution_reduce_fusion = f32[32768]{0:T(1024)S(1)} fusion(bf16[32768,128]{1,0:T(8,128)(2,1)} %bitcast.52, bf16[768,128]{1,0:T(8,128)(2,1)S(1)} %copy-done.3), kind=kOutput, calls=%fused_computation.6 | convolution fusion | flops 6467584000 | bytes 8716288 | tf_op jit(solution)/shard_map/rd,cd->rc/dot_general | solution.py:50
  99.3 0.9 reshape.572
  100.1 7.6 %all-to-all-start = ((f32[64,1,512]{2,1,0:T(1,128)}), f32[64,1,512]{2,1,0:T(1,128)S(1)}, u32[]{:S(2)}, u32[]{:S(2)}) async-start(f32[64,1,512]{2,1,0:T(1,128)} %reshape.572), calls=%async_computation | async-start | bytes 262144 | tf_op jit(solution)/shard_map/all_to_all | solution.py:57
  107.7 8.3 %gather_fusion.2 = bf16[768,32,128]{2,1,0:T(8,128)(2,1)} fusion(bf16[1024,32,128]{2,1,0:T(8,128)(2,1)} %all-gather.2.cloned.1.call-done, s32[1024]{0:T(1024)S(1)} %pad_clamp_fusion.1), kind=kCustom, calls=%fused_computation.2 | custom fusion | bytes 12585984 | tf_op jit(solution)/shard_map/jit(_take)/gather | solution.py:66
  116.0 8.3 %select_reduce_fusion = f32[768,32]{1,0:T(8,128)S(1)} fusion(pred[768,32]{1,0:T(8,128)(4,1)S(1)} %broadcast_compare_fusion, bf16[768,32,128]{2,1,0:T(8,128)(2,1)} %gather_fusion.3, pred[768]{0:T(1024)(128)(4,1)S(1)} %le.94, bf16[768,32,128]{2,1,0:T(8,128)(2,1)} %gather_fusion.2, pred[768]{0:T(1024)(128)(4,1)S(1)} %compare_and_fusion), kind=kOutput, calls=%fused_computation.7 | convolution fusion | flops 209166336 | bytes 12707328 | tf_op jit(solution)/shard_map/ntd,npd->ntp/dot_general | solution.py:68
  125.0 1.0 reduce.8
  126.4 1.3 collective-permute-start
  127.6 2.9 %collective-permute-done = f32[784,32]{0,1:T(8,128)S(1)} collective-permute-done((f32[784,32]{0,1:T(8,128)S(1)}, f32[784,32]{0,1:T(8,128)S(1)}, u32[]{:S(2)}, u32[]{:S(2)}) %collective-permute-start) | collective-permute-done | bytes 100384 | tf_op jit(solution)/shard_map/ppermute | solution.py:79
  130.6 2.8 %collective-permute-start.1 = (f32[784,32]{0,1:T(8,128)S(1)}, f32[784,32]{0,1:T(8,128)S(1)}, u32[]{:S(2)}, u32[]{:S(2)}) collective-permute-start(f32[784,32]{0,1:T(8,128)S(1)} %fusion.34), channel_id=1, source_target_pairs={{0,2},{1,3},{2,0},{3,1},{4,6},{5,7},{6,4},{7,5},{8,10},{9,11},{10,... | collective-permute-start | bytes 301064 | tf_op jit(solution)/shard_map/ppermute | solution.py:79
  133.4 2.4 %collective-permute-done.1 = f32[784,32]{0,1:T(8,128)S(1)} collective-permute-done((f32[784,32]{0,1:T(8,128)S(1)}, f32[784,32]{0,1:T(8,128)S(1)}, u32[]{:S(2)}, u32[]{:S(2)}) %collective-permute-start.1) | collective-permute-done | bytes 100384 | tf_op jit(solution)/shard_map/ppermute | solution.py:79
  136.7 12.6 %all-to-all-start.2 = ((f32[64,1,12]{2,1,0:T(1,128)}), f32[64,1,12]{2,1,0:T(1,128)S(1)}, u32[]{:S(2)}, u32[]{:S(2)}) async-start(f32[64,1,12]{2,1,0:T(1,128)} %bitcast.11), calls=%async_computation.2 | async-start | bytes 65536 | tf_op jit(solution)/shard_map/all_to_all | solution.py:84
  150.1 8.5 %all-to-all-done.2 = f32[64,1,12]{2,1,0:T(1,128)S(1)} async-done(((f32[64,1,12]{2,1,0:T(1,128)}), f32[64,1,12]{2,1,0:T(1,128)S(1)}, u32[]{:S(2)}, u32[]{:S(2)}) %all-to-all-start.2) | async-done | bytes 3104 | tf_op jit(solution)/shard_map/all_to_all | solution.py:84
  159.9 1.4 gather_fusion.4
  (72 shorter events, 8.8 us)
Async XLA Ops:
  7.2 50.8 %copy-start = (bf16[256,32,128]{2,1,0:T(8,128)(2,1)S(1)}, bf16[256,32,128]{2,1,0:T(8,128)(2,1)}, u32[]{:S(2)}) copy-start(bf16[256,32,128]{2,1,0:T(8,128)(2,1)} %param.8) | copy-start | bytes 6291460
  7.2 45.7 %copy-start.1 = (s32[256]{0:T(256)S(1)}, s32[256]{0:T(256)}, u32[]{:S(2)}) copy-start(s32[256]{0:T(256)} %param.9) | copy-start | bytes 3076
  7.2 74.6 %all-gather.2.cloned.1.call-start = ((), (), s32[]{:S(2)}) async-start(), calls=%async_computation.3 | async-start | bytes 8912896 | tf_op jit(solution)/shard_map/all_gather | solution.py:40
  28.3 23.1 %all-to-all-start.1 = ((s32[64,1,24]{2,1,0:T(1,128)}), s32[64,1,24]{2,1,0:T(1,128)S(1)}, u32[]{:S(2)}, u32[]{:S(2)}) async-start(s32[64,1,24]{2,1,0:T(1,128)} %bitcast.9), calls=%async_computation.1 | async-start | bytes 65536 | tf_op jit(solution)/shard_map/all_to_all | solution.py:45
  57.9 23.9 %copy-start.3 = (bf16[768,128]{1,0:T(8,128)(2,1)S(1)}, bf16[768,128]{1,0:T(8,128)(2,1)}, u32[]{:S(2)}) copy-start(bf16[768,128]{1,0:T(8,128)(2,1)} %param.7) | copy-start | bytes 589828
  100.1 24.3 %all-to-all-start = ((f32[64,1,512]{2,1,0:T(1,128)}), f32[64,1,512]{2,1,0:T(1,128)S(1)}, u32[]{:S(2)}, u32[]{:S(2)}) async-start(f32[64,1,512]{2,1,0:T(1,128)} %reshape.572), calls=%async_computation | async-start | bytes 262144 | tf_op jit(solution)/shard_map/all_to_all | solution.py:57
  116.0 45.4 %copy-start.2 = (s32[16,16]{1,0:T(8,128)S(1)}, s32[16,16]{1,0:T(8,128)}, u32[]{:S(2)}) copy-start(s32[16,16]{1,0:T(8,128)} %param.11) | copy-start | bytes 3076
  126.4 4.2 %collective-permute-start = (f32[784,32]{0,1:T(8,128)S(1)}, f32[784,32]{0,1:T(8,128)S(1)}, u32[]{:S(2)}, u32[]{:S(2)}) collective-permute-start(f32[784,32]{0,1:T(8,128)S(1)} %pad_maximum_fusion), channel_id=1, source_target_pairs={{0,1},{1,0},{2,3},{3,2},{4,5},{5,4},{6,7},{7,6},{8,9},{9,8},{10,11... | collective-permute-start | bytes 301064 | tf_op jit(solution)/shard_map/ppermute | solution.py:79
  130.6 5.2 %collective-permute-start.1 = (f32[784,32]{0,1:T(8,128)S(1)}, f32[784,32]{0,1:T(8,128)S(1)}, u32[]{:S(2)}, u32[]{:S(2)}) collective-permute-start(f32[784,32]{0,1:T(8,128)S(1)} %fusion.34), channel_id=1, source_target_pairs={{0,2},{1,3},{2,0},{3,1},{4,6},{5,7},{6,4},{7,5},{8,10},{9,11},{10,... | collective-permute-start | bytes 301064 | tf_op jit(solution)/shard_map/ppermute | solution.py:79
  136.7 21.9 %all-to-all-start.2 = ((f32[64,1,12]{2,1,0:T(1,128)}), f32[64,1,12]{2,1,0:T(1,128)S(1)}, u32[]{:S(2)}, u32[]{:S(2)}) async-start(f32[64,1,12]{2,1,0:T(1,128)} %bitcast.11), calls=%async_computation.2 | async-start | bytes 65536 | tf_op jit(solution)/shard_map/all_to_all | solution.py:84
Sparse Core Ops, SparseCore 0:
  20.7 61.0 all-gather.1

commit v6 on v5

--- a/solution.py
+++ b/solution.py
@@ -73,11 +73,12 @@
 
     merged = jnp.concatenate([shard_best, partial_value], axis=0)
     cent_total = lax.axis_size("cent")
-    step = 1
-    while step < cent_total:
-        partner = [(i, i ^ step) for i in range(cent_total)]
-        merged = jnp.maximum(merged, lax.ppermute(merged, "cent", partner))
-        step *= 2
+    arrived = [
+        lax.ppermute(merged, "cent", [(i, (i + shift) % cent_total) for i in range(cent_total)])
+        for shift in range(1, cent_total)
+    ]
+    for other in arrived:
+        merged = jnp.maximum(merged, other)
     token_best = merged[:query_count]
     complete = merged[query_count:]
     pair_scores = (jnp.sum(complete, axis=1) / query_tokens).reshape(shard_total, capacity)

time: 169 us -> 168 us (level)
    ppermute x2 -> x3, waiting for transfers between devices: 5.34 us -> 4.27 us  [per_device(): lax.ppermute(merged, 'cent', [(i, (i + shift) % cent_total) for i in rang...]
    ppermute x2 -> x3, starting transfers between devices: 4.06 us -> 4.25 us  [per_device(): lax.ppermute(merged, 'cent', [(i, (i + shift) % cent_total) for i in rang...]
  transfers between devices with their start and end apart: 6 -> 7, of which waited for: 5 -> 6; matrix products, arithmetic and copies ran while one was open for 21% -> 21% of each run, Pallas kernels for 0% -> 0%
where the time goes in v6:
time: 168 us; the launch traced here: 167 us
  waiting for transfers between devices  41.4 us (25%)
  starting transfers between devices  37.3 us (22%)
  local copies, waits for them, and re-layouts  31.6 us (19%)
  matrix products  25.5 us (15%)
  between operations  14.4 us (9%)
  blocking collectives  13.4 us (8%)
  other arithmetic  3.85 us (2%)
    all_gather x1, waiting for transfers between devices, per_device(): lax.all_gather(lax.all_gather(queries, 'y', axis=0, tiled=True), 'rest',...  19.1 us
    dot_general x1, matrix products, per_device(): jnp.einsum('rd,cd->rc', flattened, centroids, preferred_element_type=jnp....  17.2 us
    all_to_all x1, starting transfers between devices, per_device(): lax.all_to_all(table, shard, split_axis=0, concat_axis=0, tiled=True)  13.5 us
    all_gather x1, blocking collectives, per_device(): lax.all_gather(queries, 'y', axis=0, tiled=True)  13.4 us
    all_to_all x1, starting transfers between devices, per_device(): lax.all_to_all(pair_scores, shard, split_axis=0, concat_axis=0, tiled=True)  12 us
    all_to_all x1, waiting for transfers between devices, per_device(): lax.all_to_all(table, shard, split_axis=0, concat_axis=0, tiled=True)  9.58 us
    all_to_all x1, waiting for transfers between devices, per_device(): lax.all_to_all(pair_scores, shard, split_axis=0, concat_axis=0, tiled=True)  8.46 us
    gather x1, local copies, waits for them, and re-layouts, per_device(): asked = jnp.take(query_block, query_table, axis=0)  8.3 us
  transfers between devices with their start and end apart: 7, of which 6 were waited for; matrix products, arithmetic and copies ran while one was open for 21% of the time, Pallas kernels for 0%

profile of v6, /device:TPU:1, one launch (start us, length us, event | category | flops | bytes accessed | tf_op | source)
XLA Modules:
  0.0 167.4 jit_solution(509737769823410722)
XLA Ops:
  7.2 13.4 %all_gather.6 = bf16[64,32,128]{2,1,0:T(8,128)(2,1)} all-gather(bf16[16,32,128]{2,1,0:T(8,128)(2,1)} %param.6), channel_id=1, replica_groups=mesh['y'=4,'rest'=16,'cent'=4] {'y'}, dimensions={0}, use_global_device_ids=true | all-gather | bytes 655360 | tf_op jit(solution)/shard_map/all_gather | solution.py:41
  20.6 0.8 reshape.503
  21.4 0.8 reshape.504
  22.2 0.8 reshape.505
  23.0 2.1 %gather_fusion = s32[256]{0:T(256)S(1)} fusion(s32[16384]{0:T(1024)} %param.10, s32[1024]{0:T(1024)S(1)} %pad_clamp_fusion.3), kind=kCustom, calls=%fused_computation | custom fusion | bytes 3072 | tf_op jit(solution)/shard_map/jit(_take)/gather | solution.py:24
  26.3 1.2 scatter_custom_fusion
  28.3 13.5 %all-to-all-start.1 = ((s32[64,1,24]{2,1,0:T(1,128)}), s32[64,1,24]{2,1,0:T(1,128)S(1)}, u32[]{:S(2)}, u32[]{:S(2)}) async-start(s32[64,1,24]{2,1,0:T(1,128)} %bitcast.9), calls=%async_computation.1 | async-start | bytes 65536 | tf_op jit(solution)/shard_map/all_to_all | solution.py:45
  41.8 9.6 %all-to-all-done.1 = s32[64,1,24]{2,1,0:T(1,128)S(1)} async-done(((s32[64,1,24]{2,1,0:T(1,128)}), s32[64,1,24]{2,1,0:T(1,128)S(1)}, u32[]{:S(2)}, u32[]{:S(2)}) %all-to-all-start.1) | async-done | bytes 6176 | tf_op jit(solution)/shard_map/all_to_all | solution.py:45
  52.9 5.0 %gather_fusion.1 = s32[768]{0:T(1024)S(1)} fusion(s32[256]{0:T(256)S(1)} %copy-done.1, s32[1024]{0:T(1024)S(1)} %pad_clamp_fusion.2), kind=kCustom, calls=%fused_computation.1 | custom fusion | bytes 9216 | tf_op jit(solution)/shard_map/jit(_take)/gather | solution.py:70
  57.9 4.5 %gather_fusion.3 = bf16[768,32,128]{2,1,0:T(8,128)(2,1)} fusion(bf16[256,32,128]{2,1,0:T(8,128)(2,1)S(1)} %copy-done, s32[1024]{0:T(1024)S(1)} %pad_clamp_fusion.2), kind=kCustom, calls=%fused_computation.3 | custom fusion | bytes 12585984 | tf_op jit(solution)/shard_map/jit(_take)/gather | solution.py:67
  62.7 19.1 %all-gather.2.cloned.1.call-done = bf16[1024,32,128]{2,1,0:T(8,128)(2,1)} async-done(((bf16[64,32,128]{2,1,0:T(8,128)(2,1)}), bf16[1024,32,128]{2,1,0:T(8,128)(2,1)}) %all-gather.2.cloned.1.call-update) | async-done | bytes 8388624 | tf_op jit(solution)/shard_map/all_gather | solution.py:40
  81.8 17.2 %convolution_reduce_fusion = f32[32768]{0:T(1024)S(1)} fusion(bf16[32768,128]{1,0:T(8,128)(2,1)} %bitcast.52, bf16[768,128]{1,0:T(8,128)(2,1)S(1)} %copy-done.3), kind=kOutput, calls=%fused_computation.6 | convolution fusion | flops 6467584000 | bytes 8716288 | tf_op jit(solution)/shard_map/rd,cd->rc/dot_general | solution.py:50
  99.3 0.9 reshape.572
  100.1 7.6 %all-to-all-start = ((f32[64,1,512]{2,1,0:T(1,128)}), f32[64,1,512]{2,1,0:T(1,128)S(1)}, u32[]{:S(2)}, u32[]{:S(2)}) async-start(f32[64,1,512]{2,1,0:T(1,128)} %reshape.572), calls=%async_computation | async-start | bytes 262144 | tf_op jit(solution)/shard_map/all_to_all | solution.py:57
  107.7 8.3 %gather_fusion.2 = bf16[768,32,128]{2,1,0:T(8,128)(2,1)} fusion(bf16[1024,32,128]{2,1,0:T(8,128)(2,1)} %all-gather.2.cloned.1.call-done, s32[1024]{0:T(1024)S(1)} %pad_clamp_fusion.1), kind=kCustom, calls=%fused_computation.2 | custom fusion | bytes 12585984 | tf_op jit(solution)/shard_map/jit(_take)/gather | solution.py:66
  116.0 8.3 %select_reduce_fusion = f32[768,32]{1,0:T(8,128)S(1)} fusion(pred[768,32]{1,0:T(8,128)(4,1)S(1)} %broadcast_compare_fusion, bf16[768,32,128]{2,1,0:T(8,128)(2,1)} %gather_fusion.3, pred[768]{0:T(1024)(128)(4,1)S(1)} %le.94, bf16[768,32,128]{2,1,0:T(8,128)(2,1)} %gather_fusion.2, pred[768]{0:T(1024)(128)(4,1)S(1)} %compare_and_fusion), kind=kOutput, calls=%fused_computation.7 | convolution fusion | flops 209166336 | bytes 12707328 | tf_op jit(solution)/shard_map/ntd,npd->ntp/dot_general | solution.py:68
  125.0 1.0 reduce.8
  126.4 2.8 %collective-permute-start.1 = (f32[784,32]{0,1:T(8,128)S(1)}, f32[784,32]{0,1:T(8,128)S(1)}, u32[]{:S(2)}, u32[]{:S(2)}) collective-permute-start(f32[784,32]{0,1:T(8,128)S(1)} %pad_maximum_fusion), channel_id=1, source_target_pairs={{0,2},{1,3},{2,0},{3,1},{4,6},{5,7},{6,4},{7,5},{8,10},{9,11},{10,... | collective-permute-start | bytes 301064 | tf_op jit(solution)/shard_map/ppermute | solution.py:77
  129.1 0.9 collective-permute-start.2
  130.6 1.4 collective-permute-done.1
  132.0 2.5 %collective-permute-done.2 = f32[784,32]{0,1:T(8,128)S(1)} collective-permute-done((f32[784,32]{0,1:T(8,128)S(1)}, f32[784,32]{0,1:T(8,128)S(1)}, u32[]{:S(2)}, u32[]{:S(2)}) %collective-permute-start.2) | collective-permute-done | bytes 100384 | tf_op jit(solution)/shard_map/ppermute | solution.py:77
  135.8 12.0 %all-to-all-start.2 = ((f32[64,1,12]{2,1,0:T(1,128)}), f32[64,1,12]{2,1,0:T(1,128)S(1)}, u32[]{:S(2)}, u32[]{:S(2)}) async-start(f32[64,1,12]{2,1,0:T(1,128)} %bitcast.11), calls=%async_computation.2 | async-start | bytes 65536 | tf_op jit(solution)/shard_map/all_to_all | solution.py:85
  148.7 8.5 %all-to-all-done.2 = f32[64,1,12]{2,1,0:T(1,128)S(1)} async-done(((f32[64,1,12]{2,1,0:T(1,128)}), f32[64,1,12]{2,1,0:T(1,128)S(1)}, u32[]{:S(2)}, u32[]{:S(2)}) %all-to-all-start.2) | async-done | bytes 3104 | tf_op jit(solution)/shard_map/all_to_all | solution.py:85
  158.5 1.4 gather_fusion.4
  (73 shorter events, 9.8 us)
Async XLA Ops:
  7.2 50.8 %copy-start = (bf16[256,32,128]{2,1,0:T(8,128)(2,1)S(1)}, bf16[256,32,128]{2,1,0:T(8,128)(2,1)}, u32[]{:S(2)}) copy-start(bf16[256,32,128]{2,1,0:T(8,128)(2,1)} %param.8) | copy-start | bytes 6291460
  7.2 45.7 %copy-start.1 = (s32[256]{0:T(256)S(1)}, s32[256]{0:T(256)}, u32[]{:S(2)}) copy-start(s32[256]{0:T(256)} %param.9) | copy-start | bytes 3076
  7.2 74.6 %all-gather.2.cloned.1.call-start = ((), (), s32[]{:S(2)}) async-start(), calls=%async_computation.3 | async-start | bytes 8912896 | tf_op jit(solution)/shard_map/all_gather | solution.py:40
  28.3 23.1 %all-to-all-start.1 = ((s32[64,1,24]{2,1,0:T(1,128)}), s32[64,1,24]{2,1,0:T(1,128)S(1)}, u32[]{:S(2)}, u32[]{:S(2)}) async-start(s32[64,1,24]{2,1,0:T(1,128)} %bitcast.9), calls=%async_computation.1 | async-start | bytes 65536 | tf_op jit(solution)/shard_map/all_to_all | solution.py:45
  57.9 23.9 %copy-start.3 = (bf16[768,128]{1,0:T(8,128)(2,1)S(1)}, bf16[768,128]{1,0:T(8,128)(2,1)}, u32[]{:S(2)}) copy-start(bf16[768,128]{1,0:T(8,128)(2,1)} %param.7) | copy-start | bytes 589828
  100.1 24.3 %all-to-all-start = ((f32[64,1,512]{2,1,0:T(1,128)}), f32[64,1,512]{2,1,0:T(1,128)S(1)}, u32[]{:S(2)}, u32[]{:S(2)}) async-start(f32[64,1,512]{2,1,0:T(1,128)} %reshape.572), calls=%async_computation | async-start | bytes 262144 | tf_op jit(solution)/shard_map/all_to_all | solution.py:57
  116.0 43.9 %copy-start.2 = (s32[16,16]{1,0:T(8,128)S(1)}, s32[16,16]{1,0:T(8,128)}, u32[]{:S(2)}) copy-start(s32[16,16]{1,0:T(8,128)} %param.11) | copy-start | bytes 3076
  126.4 5.7 %collective-permute-start.1 = (f32[784,32]{0,1:T(8,128)S(1)}, f32[784,32]{0,1:T(8,128)S(1)}, u32[]{:S(2)}, u32[]{:S(2)}) collective-permute-start(f32[784,32]{0,1:T(8,128)S(1)} %pad_maximum_fusion), channel_id=1, source_target_pairs={{0,2},{1,3},{2,0},{3,1},{4,6},{5,7},{6,4},{7,5},{8,10},{9,11},{10,... | collective-permute-start | bytes 301064 | tf_op jit(solution)/shard_map/ppermute | solution.py:77
  129.1 5.4 %collective-permute-start.2 = (f32[784,32]{0,1:T(8,128)S(1)}, f32[784,32]{0,1:T(8,128)S(1)}, u32[]{:S(2)}, u32[]{:S(2)}) collective-permute-start(f32[784,32]{0,1:T(8,128)S(1)} %pad_maximum_fusion), channel_id=1, source_target_pairs={{0,3},{1,0},{2,1},{3,2},{4,7},{5,4},{6,5},{7,6},{8,11},{9,8},{10,9... | collective-permute-start | bytes 301064 | tf_op jit(solution)/shard_map/ppermute | solution.py:77
  130.0 4.9 %collective-permute-start = (f32[784,32]{0,1:T(8,128)S(1)}, f32[784,32]{0,1:T(8,128)S(1)}, u32[]{:S(2)}, u32[]{:S(2)}) collective-permute-start(f32[784,32]{0,1:T(8,128)S(1)} %pad_maximum_fusion), channel_id=1, source_target_pairs={{0,1},{1,2},{2,3},{3,0},{4,5},{5,6},{6,7},{7,4},{8,9},{9,10},{10,1... | collective-permute-start | bytes 301064 | tf_op jit(solution)/shard_map/ppermute | solution.py:77
  135.8 21.4 %all-to-all-start.2 = ((f32[64,1,12]{2,1,0:T(1,128)}), f32[64,1,12]{2,1,0:T(1,128)S(1)}, u32[]{:S(2)}, u32[]{:S(2)}) async-start(f32[64,1,12]{2,1,0:T(1,128)} %bitcast.11), calls=%async_computation.2 | async-start | bytes 65536 | tf_op jit(solution)/shard_map/all_to_all | solution.py:85
Sparse Core Ops, SparseCore 0:
  20.7 61.0 all-gather.1

commit v7 on v6

--- a/solution.py
+++ b/solution.py
@@ -37,39 +37,53 @@
         .reshape(shard_total, capacity * 2)
     )
 
-    query_block = lax.all_gather(
-        lax.all_gather(queries, "y", axis=0, tiled=True), "rest", axis=0, tiled=True
-    )
-    y_total = lax.axis_size("y")
-    rest_total = lax.axis_size("rest")
     mine = lax.all_to_all(table, shard, split_axis=0, concat_axis=0, tiled=True).reshape(
         shard_total, capacity, 2
     )
+    slot_table = jnp.maximum(mine[..., 0], 0).reshape(-1)
+    global_query = jnp.maximum(mine[..., 1], 0).reshape(-1)
+    chosen = jnp.take(passages, slot_table, axis=0)
+    token_index = lax.axis_index("cent") * token_rows + jnp.arange(token_rows, dtype=jnp.int32)
+    valid_tokens = token_index[None, :] < jnp.take(lengths, slot_table, axis=0)[:, None]
 
-    flattened = query_block.reshape(-1, feature_width)
-    scored = jnp.einsum("rd,cd->rc", flattened, centroids, preferred_element_type=jnp.float32)
+    y_total = lax.axis_size("y")
+    rest_total = lax.axis_size("rest")
+    part_total = 2 if y_total % 2 == 0 else 1
+    y_part = y_total // part_total
+    along_y = lax.all_gather(queries, "y", axis=0, tiled=True)
+    part_best = []
+    part_value = []
+    pairs_per_part = shard_total * capacity // part_total
+    for part in range(part_total):
+        block = lax.all_gather(
+            along_y[part * y_part * query_count:(part + 1) * y_part * query_count],
+            "rest", axis=0, tiled=True,
+        )
+        scored = jnp.einsum("rd,cd->rc", block.reshape(-1, feature_width), centroids,
+                            preferred_element_type=jnp.float32)
+        part_best.append(
+            jnp.max(scored, axis=1).reshape(rest_total, y_part, query_count, query_tokens)
+        )
+        rows = slice(part * pairs_per_part, (part + 1) * pairs_per_part)
+        query_here = global_query[rows]
+        source_shard = query_here // query_count
+        query_table = (
+            (source_shard % rest_total) * y_part + source_shard // rest_total - part * y_part
+        ) * query_count + query_here % query_count
+        asked = jnp.take(block, query_table, axis=0)
+        pair_scored = jnp.einsum("ntd,npd->ntp", asked, chosen[rows],
+                                 preferred_element_type=jnp.float32)
+        pair_scored = jnp.where(valid_tokens[rows][:, None, :], pair_scored, masked_score)
+        part_value.append(jnp.max(pair_scored, axis=2))
+
     local_best = (
-        jnp.max(scored, axis=1)
-        .reshape(rest_total, y_total, query_count, query_tokens)
-        .transpose(1, 0, 2, 3)
+        jnp.stack(part_best, axis=0)
+        .transpose(0, 2, 1, 3, 4)
         .reshape(shard_total, query_count, query_tokens)
     )
     gathered_best = lax.all_to_all(local_best, shard, split_axis=0, concat_axis=0, tiled=True)
     shard_best = jnp.max(gathered_best, axis=0)
-
-    slot_table = jnp.maximum(mine[..., 0], 0).reshape(-1)
-    global_query = jnp.maximum(mine[..., 1], 0).reshape(-1)
-    source_shard = global_query // query_count
-    query_table = (
-        (source_shard % rest_total) * y_total + source_shard // rest_total
-    ) * query_count + global_query % query_count
-    asked = jnp.take(query_block, query_table, axis=0)
-    chosen = jnp.take(passages, slot_table, axis=0)
-    pair_scored = jnp.einsum("ntd,npd->ntp", asked, chosen, preferred_element_type=jnp.float32)
-    token_index = lax.axis_index("cent") * token_rows + jnp.arange(token_rows, dtype=jnp.int32)
-    valid_tokens = token_index[None, :] < jnp.take(lengths, slot_table, axis=0)[:, None]
-    pair_scored = jnp.where(valid_tokens[:, None, :], pair_scored, masked_score)
-    partial_value = jnp.max(pair_scored, axis=2)
+    partial_value = jnp.concatenate(part_value, axis=0)
 
     merged = jnp.concatenate([shard_best, partial_value], axis=0)
     cent_total = lax.axis_size("cent")

time: 168 us -> 193 us (1.15)
  waiting for transfers between devices: 41.4 us -> 53.3 us
  other arithmetic: 3.85 us -> 11.7 us
  matrix products: 25.5 us -> 28.4 us
  local copies, waits for them, and re-layouts: 31.6 us -> 33.6 us
    all_gather x1 -> x2, waiting for transfers between devices: 19.1 us -> 30.5 us  [per_device(): lax.all_gather(along_y[part * y_part * query_count:(part + 1) * y_part *...]
    select_n x1, other arithmetic: 0.05 us -> 7.83 us  [per_device(): chosen = jnp.take(passages, slot_table, axis=0)]
    dot_general x2 -> x4, matrix products: 25.5 us -> 28.4 us  [the longest x2 18.2 us: per_device(): jnp.einsum('rd,cd->rc', block.reshape(-1, feature_width), centroids, pref...]
    gather x1 -> x2, local copies, waits for them, and re-layouts: 8.3 us -> 9.83 us  [per_device(): asked = jnp.take(block, query_table, axis=0)]
  transfers between devices with their start and end apart: 7 -> 8, of which waited for: 6 -> 6; matrix products, arithmetic and copies ran while one was open for 21% -> 29% of each run, Pallas kernels for 0% -> 0%
where the time goes in v7:
time: 193 us; the launch traced here: 192 us
  waiting for transfers between devices  53.3 us (28%)
  starting transfers between devices  37.7 us (20%)
  local copies, waits for them, and re-layouts  33.6 us (17%)
  matrix products  28.4 us (15%)
  between operations  14.4 us (7%)
  blocking collectives  12.9 us (7%)
  other arithmetic  11.7 us (6%)
    all_gather x2, waiting for transfers between devices, per_device(): lax.all_gather(along_y[part * y_part * query_count:(part + 1) * y_part *...  30.5 us
    dot_general x2, matrix products, per_device(): jnp.einsum('rd,cd->rc', block.reshape(-1, feature_width), centroids, pref...  18.2 us
    all_to_all x1, starting transfers between devices, per_device(): lax.all_to_all(table, shard, split_axis=0, concat_axis=0, tiled=True)  13.8 us
    all_gather x1, blocking collectives, per_device(): along_y = lax.all_gather(queries, 'y', axis=0, tiled=True)  12.9 us
    all_to_all x1, starting transfers between devices, per_device(): lax.all_to_all(pair_scores, shard, split_axis=0, concat_axis=0, tiled=True)  12 us
    dot_general x2, matrix products, per_device(): jnp.einsum('ntd,npd->ntp', asked, chosen[rows], preferred_element_type=jn...  10.2 us
    gather x2, local copies, waits for them, and re-layouts, per_device(): asked = jnp.take(block, query_table, axis=0)  9.83 us
    all_to_all x1, waiting for transfers between devices, per_device(): lax.all_to_all(table, shard, split_axis=0, concat_axis=0, tiled=True)  9.37 us
  transfers between devices with their start and end apart: 8, of which 6 were waited for; matrix products, arithmetic and copies ran while one was open for 29% of the time, Pallas kernels for 0%

profile of v7, /device:TPU:1, one launch (start us, length us, event | category | flops | bytes accessed | tf_op | source)
XLA Modules:
  0.0 192.1 jit_solution(10943913004906813701)
XLA Ops:
  7.2 12.9 %all_gather.9 = bf16[64,32,128]{2,1,0:T(8,128)(2,1)S(1)} all-gather(bf16[16,32,128]{2,1,0:T(8,128)(2,1)} %param.8), channel_id=1, replica_groups=mesh['y'=4,'rest'=16,'cent'=4] {'y'}, dimensions={0}, use_global_device_ids=true | all-gather | bytes 655360 | tf_op jit(solution)/shard_map/all_gather | solution.py:53
  24.2 2.1 %gather_fusion = s32[256]{0:T(256)S(1)} fusion(s32[16384]{0:T(1024)} %param.12, s32[1024]{0:T(1024)S(1)} %pad_clamp_fusion.4), kind=kCustom, calls=%fused_computation.2 | custom fusion | bytes 3072 | tf_op jit(solution)/shard_map/jit(_take)/gather | solution.py:24
  27.4 1.2 scatter_custom_fusion
  29.5 13.8 %all-to-all-start.1 = ((s32[64,1,24]{2,1,0:T(1,128)}), s32[64,1,24]{2,1,0:T(1,128)S(1)}, u32[]{:S(2)}, u32[]{:S(2)}) async-start(s32[64,1,24]{2,1,0:T(1,128)} %bitcast.10), calls=%async_computation.1 | async-start | bytes 65536 | tf_op jit(solution)/shard_map/all_to_all | solution.py:40
  43.3 9.4 %all-to-all-done.1 = s32[64,1,24]{2,1,0:T(1,128)S(1)} async-done(((s32[64,1,24]{2,1,0:T(1,128)}), s32[64,1,24]{2,1,0:T(1,128)S(1)}, u32[]{:S(2)}, u32[]{:S(2)}) %all-to-all-start.1) | async-done | bytes 6176 | tf_op jit(solution)/shard_map/all_to_all | solution.py:40
  53.7 5.0 %gather_fusion.1 = s32[768]{0:T(1024)S(1)} fusion(s32[256]{0:T(256)S(1)} %copy-done.1, s32[1024]{0:T(1024)S(1)} %pad_clamp_fusion.3), kind=kCustom, calls=%fused_computation.3 | custom fusion | bytes 9216 | tf_op jit(solution)/shard_map/jit(_take)/gather | solution.py:47
  58.7 4.4 %gather_fusion.2 = bf16[768,32,128]{2,1,0:T(8,128)(2,1)} fusion(bf16[256,32,128]{2,1,0:T(8,128)(2,1)S(1)} %copy-done, s32[1024]{0:T(1024)S(1)} %pad_clamp_fusion.3), kind=kCustom, calls=%fused_computation.4 | custom fusion | bytes 12585984 | tf_op jit(solution)/shard_map/jit(_take)/gather | solution.py:45
  63.4 7.8 %broadcast_select_fusion = bf16[768,32,128]{2,1,0:T(8,128)(2,1)} fusion(bf16[768,32,128]{2,1,0:T(8,128)(2,1)} %gather_fusion.2, pred[768]{0:T(1024)(128)(4,1)S(1)} %le.90), kind=kLoop, calls=%fused_computation.11 | loop fusion | flops 3145728 | bytes 12583680 | tf_op jit(solution)/shard_map/jit(_take)/select_n | solution.py:45
  71.3 9.1 %convolution_reduce_fusion = f32[16384]{0:T(1024)S(1)} fusion(bf16[16384,128]{1,0:T(8,128)(2,1)} %bitcast.48, bf16[768,128]{1,0:T(8,128)(2,1)S(1)} %copy-done.3), kind=kOutput, calls=%fused_computation.7 | convolution fusion | flops 3233792000 | bytes 4456448 | tf_op jit(solution)/shard_map/rd,cd->rc/dot_general | solution.py:62
  80.4 30.5 %all-gather.3.cloned.1.call-done = bf16[512,32,128]{2,1,0:T(8,128)(2,1)} async-done(((bf16[32,32,128]{2,1,0:T(8,128)(2,1)}), bf16[512,32,128]{2,1,0:T(8,128)(2,1)}) %all-gather.3.cloned.1.call-update) | async-done | bytes 4194320 | tf_op jit(solution)/shard_map/all_gather | solution.py:58
  110.9 9.1 %convolution_reduce_fusion.1 = f32[16384]{0:T(1024)S(1)} fusion(bf16[16384,128]{1,0:T(8,128)(2,1)} %bitcast.49, bf16[768,128]{1,0:T(8,128)(2,1)S(1)} %copy-done.3), kind=kOutput, calls=%fused_computation.8 | convolution fusion | flops 3233792000 | bytes 4456448 | tf_op jit(solution)/shard_map/rd,cd->rc/dot_general | solution.py:62
  120.4 0.9 reshape.419
  121.3 7.6 %all-to-all-start = ((f32[64,1,512]{2,1,0:T(1,128)}), f32[64,1,512]{2,1,0:T(1,128)S(1)}, u32[]{:S(2)}, u32[]{:S(2)}) async-start(f32[64,1,512]{2,1,0:T(1,128)} %reshape.419), calls=%async_computation | async-start | bytes 262144 | tf_op jit(solution)/shard_map/all_to_all | solution.py:84
  128.8 4.9 %gather_fusion.5 = bf16[384,32,128]{2,1,0:T(8,128)(2,1)} fusion(bf16[512,32,128]{2,1,0:T(8,128)(2,1)} %all-gather.5.cloned.1.call-done, s32[1024]{0:T(1024)S(1)} %pad_clamp_fusion.1), kind=kCustom, calls=%fused_computation.1.clone | custom fusion | bytes 6292992 | tf_op jit(solution)/shard_map/jit(_take)/gather | solution.py:73
  133.7 5.1 %select_reduce_fusion = f32[384,32]{1,0:T(8,128)S(1)} fusion(pred[384,32]{1,0:T(8,128)(4,1)S(1)} %get-tuple-element.16, bf16[768,32,128]{2,1,0:T(8,128)(2,1)} %broadcast_select_fusion, bf16[384,32,128]{2,1,0:T(8,128)(2,1)} %gather_fusion.5, pred[384]{0:T(512)(128)(4,1)S(1)} %get-tuple-element.9), kind=kOutput, calls=%fused_computation.9 | convolution fusion | flops 103010304 | bytes 6353280 | tf_op jit(solution)/shard_map/ntd,npd->ntp/dot_general | solution.py:74
  138.8 5.0 %gather_fusion.4 = bf16[384,32,128]{2,1,0:T(8,128)(2,1)} fusion(bf16[512,32,128]{2,1,0:T(8,128)(2,1)} %all-gather.3.cloned.1.call-done, s32[1024]{0:T(1024)S(1)} %pad_clamp_fusion.2), kind=kCustom, calls=%fused_computation.clone | custom fusion | bytes 6292992 | tf_op jit(solution)/shard_map/jit(_take)/gather | solution.py:73
  143.8 5.1 %select_reduce_fusion.1 = f32[384,32]{1,0:T(8,128)S(1)} fusion(pred[384,32]{1,0:T(8,128)(4,1)S(1)} %get-tuple-element.15, bf16[768,32,128]{2,1,0:T(8,128)(2,1)} %broadcast_select_fusion, bf16[384,32,128]{2,1,0:T(8,128)(2,1)} %gather_fusion.4, pred[384]{0:T(512)(128)(4,1)S(1)} %get-tuple-element.7), kind=kOutput, calls=%fused_computation.10 | convolution fusion | flops 103010304 | bytes 6353280 | tf_op jit(solution)/shard_map/ntd,npd->ntp/dot_general | solution.py:74
  149.7 0.9 reduce.6
  151.0 2.8 %collective-permute-start.1 = (f32[784,32]{0,1:T(8,128)S(1)}, f32[784,32]{0,1:T(8,128)S(1)}, u32[]{:S(2)}, u32[]{:S(2)}) collective-permute-start(f32[784,32]{0,1:T(8,128)S(1)} %pad_maximum_fusion), channel_id=1, source_target_pairs={{0,2},{1,3},{2,0},{3,1},{4,6},{5,7},{6,4},{7,5},{8,10},{9,11},{10,... | collective-permute-start | bytes 301064 | tf_op jit(solution)/shard_map/ppermute | solution.py:91
  155.3 1.4 collective-permute-done.1
  156.7 2.5 %collective-permute-done.2 = f32[784,32]{0,1:T(8,128)S(1)} collective-permute-done((f32[784,32]{0,1:T(8,128)S(1)}, f32[784,32]{0,1:T(8,128)S(1)}, u32[]{:S(2)}, u32[]{:S(2)}) %collective-permute-start.2) | collective-permute-done | bytes 100384 | tf_op jit(solution)/shard_map/ppermute | solution.py:91
  160.5 12.0 %all-to-all-start.2 = ((f32[64,1,12]{2,1,0:T(1,128)}), f32[64,1,12]{2,1,0:T(1,128)S(1)}, u32[]{:S(2)}, u32[]{:S(2)}) async-start(f32[64,1,12]{2,1,0:T(1,128)} %bitcast.12), calls=%async_computation.2 | async-start | bytes 65536 | tf_op jit(solution)/shard_map/all_to_all | solution.py:99
  173.4 8.5 %all-to-all-done.2 = f32[64,1,12]{2,1,0:T(1,128)S(1)} async-done(((f32[64,1,12]{2,1,0:T(1,128)}), f32[64,1,12]{2,1,0:T(1,128)S(1)}, u32[]{:S(2)}, u32[]{:S(2)}) %all-to-all-start.2) | async-done | bytes 3104 | tf_op jit(solution)/shard_map/all_to_all | solution.py:99
  183.2 1.4 gather_fusion.3
  (82 shorter events, 14.3 us)
Async XLA Ops:
  7.2 51.5 %copy-start = (bf16[256,32,128]{2,1,0:T(8,128)(2,1)S(1)}, bf16[256,32,128]{2,1,0:T(8,128)(2,1)}, u32[]{:S(2)}) copy-start(bf16[256,32,128]{2,1,0:T(8,128)(2,1)} %param.10) | copy-start | bytes 6291460
  7.2 46.5 %copy-start.1 = (s32[256]{0:T(256)S(1)}, s32[256]{0:T(256)}, u32[]{:S(2)}) copy-start(s32[256]{0:T(256)} %param.11) | copy-start | bytes 3076
  7.2 64.1 %all-gather.5.cloned.1.call-start = ((), (), s32[]{:S(2)}) async-start(), calls=%async_computation.4 | async-start | bytes 4456448 | tf_op jit(solution)/shard_map/all_gather | solution.py:58
  21.0 89.9 %all-gather.3.cloned.1.call-start = ((), (), s32[]{:S(2)}) async-start(), calls=%async_computation.3 | async-start | bytes 4456448 | tf_op jit(solution)/shard_map/all_gather | solution.py:58
  29.5 23.2 %all-to-all-start.1 = ((s32[64,1,24]{2,1,0:T(1,128)}), s32[64,1,24]{2,1,0:T(1,128)S(1)}, u32[]{:S(2)}, u32[]{:S(2)}) async-start(s32[64,1,24]{2,1,0:T(1,128)} %bitcast.10), calls=%async_computation.1 | async-start | bytes 65536 | tf_op jit(solution)/shard_map/all_to_all | solution.py:40
  63.4 7.8 %copy-start.3 = (bf16[768,128]{1,0:T(8,128)(2,1)S(1)}, bf16[768,128]{1,0:T(8,128)(2,1)}, u32[]{:S(2)}) copy-start(bf16[768,128]{1,0:T(8,128)(2,1)} %param.9) | copy-start | bytes 589828
  121.3 27.9 %all-to-all-start = ((f32[64,1,512]{2,1,0:T(1,128)}), f32[64,1,512]{2,1,0:T(1,128)S(1)}, u32[]{:S(2)}, u32[]{:S(2)}) async-start(f32[64,1,512]{2,1,0:T(1,128)} %reshape.419), calls=%async_computation | async-start | bytes 262144 | tf_op jit(solution)/shard_map/all_to_all | solution.py:84
  148.9 35.7 %copy-start.2 = (s32[16,16]{1,0:T(8,128)S(1)}, s32[16,16]{1,0:T(8,128)}, u32[]{:S(2)}) copy-start(s32[16,16]{1,0:T(8,128)} %param.13) | copy-start | bytes 3076
  151.0 5.6 %collective-permute-start.1 = (f32[784,32]{0,1:T(8,128)S(1)}, f32[784,32]{0,1:T(8,128)S(1)}, u32[]{:S(2)}, u32[]{:S(2)}) collective-permute-start(f32[784,32]{0,1:T(8,128)S(1)} %pad_maximum_fusion), channel_id=1, source_target_pairs={{0,2},{1,3},{2,0},{3,1},{4,6},{5,7},{6,4},{7,5},{8,10},{9,11},{10,... | collective-permute-start | bytes 301064 | tf_op jit(solution)/shard_map/ppermute | solution.py:91
  153.8 5.3 %collective-permute-start.2 = (f32[784,32]{0,1:T(8,128)S(1)}, f32[784,32]{0,1:T(8,128)S(1)}, u32[]{:S(2)}, u32[]{:S(2)}) collective-permute-start(f32[784,32]{0,1:T(8,128)S(1)} %pad_maximum_fusion), channel_id=1, source_target_pairs={{0,3},{1,0},{2,1},{3,2},{4,7},{5,4},{6,5},{7,6},{8,11},{9,8},{10,9... | collective-permute-start | bytes 301064 | tf_op jit(solution)/shard_map/ppermute | solution.py:91
  154.7 4.9 %collective-permute-start = (f32[784,32]{0,1:T(8,128)S(1)}, f32[784,32]{0,1:T(8,128)S(1)}, u32[]{:S(2)}, u32[]{:S(2)}) collective-permute-start(f32[784,32]{0,1:T(8,128)S(1)} %pad_maximum_fusion), channel_id=1, source_target_pairs={{0,1},{1,2},{2,3},{3,0},{4,5},{5,6},{6,7},{7,4},{8,9},{9,10},{10,1... | collective-permute-start | bytes 301064 | tf_op jit(solution)/shard_map/ppermute | solution.py:91
  160.5 21.4 %all-to-all-start.2 = ((f32[64,1,12]{2,1,0:T(1,128)}), f32[64,1,12]{2,1,0:T(1,128)S(1)}, u32[]{:S(2)}, u32[]{:S(2)}) async-start(f32[64,1,12]{2,1,0:T(1,128)} %bitcast.12), calls=%async_computation.2 | async-start | bytes 65536 | tf_op jit(solution)/shard_map/all_to_all | solution.py:99
Sparse Core Ops, SparseCore 0:
  21.2 47.0 all-gather.4
  70.1 40.7 all-gather.2

commit v8 on v6

--- a/solution.py
+++ b/solution.py
@@ -37,20 +37,26 @@
         .reshape(shard_total, capacity * 2)
     )
 
-    query_block = lax.all_gather(
-        lax.all_gather(queries, "y", axis=0, tiled=True), "rest", axis=0, tiled=True
-    )
     y_total = lax.axis_size("y")
     rest_total = lax.axis_size("rest")
+    my_y = lax.axis_index("y")
+    along_y = [queries] + [
+        lax.ppermute(queries, "y", [(i, (i + shift) % y_total) for i in range(y_total)])
+        for shift in range(1, y_total)
+    ]
+    query_block = lax.all_gather(
+        jnp.concatenate(along_y, axis=0), "rest", axis=0, tiled=True
+    )
     mine = lax.all_to_all(table, shard, split_axis=0, concat_axis=0, tiled=True).reshape(
         shard_total, capacity, 2
     )
 
     flattened = query_block.reshape(-1, feature_width)
     scored = jnp.einsum("rd,cd->rc", flattened, centroids, preferred_element_type=jnp.float32)
+    by_shift = jnp.max(scored, axis=1).reshape(rest_total, y_total, query_count, query_tokens)
+    shift_of_y = (my_y - jnp.arange(y_total, dtype=jnp.int32)) % y_total
     local_best = (
-        jnp.max(scored, axis=1)
-        .reshape(rest_total, y_total, query_count, query_tokens)
+        jnp.take(by_shift, shift_of_y, axis=1)
         .transpose(1, 0, 2, 3)
         .reshape(shard_total, query_count, query_tokens)
     )
@@ -61,7 +67,7 @@
     global_query = jnp.maximum(mine[..., 1], 0).reshape(-1)
     source_shard = global_query // query_count
     query_table = (
-        (source_shard % rest_total) * y_total + source_shard // rest_total
+        (source_shard % rest_total) * y_total + (my_y - source_shard // rest_total) % y_total
     ) * query_count + global_query % query_count
     asked = jnp.take(query_block, query_table, axis=0)
     chosen = jnp.take(passages, slot_table, axis=0)

time: 168 us -> 167 us (level)
  blocking collectives: 13.4 us -> 0 us
  starting transfers between devices: 37.3 us -> 42.2 us
  waiting for transfers between devices: 41.4 us -> 46.2 us
  other arithmetic: 3.85 us -> 5.79 us
    all_gather x1 -> x0, blocking collectives: 13.4 us -> none  [per_device(): lax.all_gather(queries, 'y', axis=0, tiled=True)]
    ppermute x0 -> x3, starting transfers between devices: none -> 6.5 us  [per_device(): lax.ppermute(queries, 'y', [(i, (i + shift) % y_total) for i in range(y_t...]
    ppermute x0 -> x3, waiting for transfers between devices: none -> 4.88 us  [per_device(): lax.ppermute(queries, 'y', [(i, (i + shift) % y_total) for i in range(y_t...]
    concatenate x0 -> x1, other arithmetic: none -> 1.79 us  [per_device(): jnp.concatenate(along_y, axis=0)]
  transfers between devices with their start and end apart: 7 -> 10, of which waited for: 6 -> 7; matrix products, arithmetic and copies ran while one was open for 21% -> 21% of each run, Pallas kernels for 0% -> 0%
where the time goes in v8:
time: 167 us; the launch traced here: 166 us
  waiting for transfers between devices  46.2 us (28%)
  starting transfers between devices  42.2 us (25%)
  local copies, waits for them, and re-layouts  32.1 us (19%)
  matrix products  25.5 us (15%)
  between operations  14.4 us (9%)
  other arithmetic  5.79 us (3%)
    all_gather x1, waiting for transfers between devices, per_device(): lax.all_gather(jnp.concatenate(along_y, axis=0), 'rest', axis=0, tiled=True)  19.1 us
    dot_general x1, matrix products, per_device(): jnp.einsum('rd,cd->rc', flattened, centroids, preferred_element_type=jnp....  17.2 us
    all_to_all x1, starting transfers between devices, per_device(): lax.all_to_all(pair_scores, shard, split_axis=0, concat_axis=0, tiled=True)  12 us
    all_to_all x1, starting transfers between devices, per_device(): lax.all_to_all(table, shard, split_axis=0, concat_axis=0, tiled=True)  11.9 us
    all_to_all x1, waiting for transfers between devices, per_device(): lax.all_to_all(table, shard, split_axis=0, concat_axis=0, tiled=True)  9.53 us
    all_to_all x1, waiting for transfers between devices, per_device(): lax.all_to_all(pair_scores, shard, split_axis=0, concat_axis=0, tiled=True)  8.46 us
    dot_general x1, matrix products, per_device(): jnp.einsum('ntd,npd->ntp', asked, chosen, preferred_element_type=jnp.floa...  8.3 us
    gather x1, local copies, waits for them, and re-layouts, per_device(): asked = jnp.take(query_block, query_table, axis=0)  8.3 us
  transfers between devices with their start and end apart: 10, of which 7 were waited for; matrix products, arithmetic and copies ran while one was open for 21% of the time, Pallas kernels for 0%

profile of v8, /device:TPU:1, one launch (start us, length us, event | category | flops | bytes accessed | tf_op | source)
XLA Modules:
  0.0 166.3 jit_solution(6402702467048940356)
XLA Ops:
  7.2 3.8 %collective-permute-start.1 = (bf16[16,32,128]{2,1,0:T(8,128)(2,1)}, bf16[16,32,128]{2,1,0:T(8,128)(2,1)S(1)}, u32[]{:S(2)}, u32[]{:S(2)}) collective-permute-start(bf16[16,32,128]{2,1,0:T(8,128)(2,1)} %param.6), channel_id=1, source_target_pairs={{0,128},{64,192},{128,0},{192,64},{1,129},{65,193},{129,1},{193,65... | collective-permute-start | bytes 393224 | tf_op jit(solution)/shard_map/ppermute | solution.py:44
  11.5 2.3 %collective-permute-start.2 = (bf16[16,32,128]{2,1,0:T(8,128)(2,1)}, bf16[16,32,128]{2,1,0:T(8,128)(2,1)S(1)}, u32[]{:S(2)}, u32[]{:S(2)}) collective-permute-start(bf16[16,32,128]{2,1,0:T(8,128)(2,1)} %param.6), channel_id=1, source_target_pairs={{0,192},{64,0},{128,64},{192,128},{1,193},{65,1},{129,65},{193,129... | collective-permute-start | bytes 393224 | tf_op jit(solution)/shard_map/ppermute | solution.py:44
  13.7 4.9 %collective-permute-done = bf16[16,32,128]{2,1,0:T(8,128)(2,1)S(1)} collective-permute-done((bf16[16,32,128]{2,1,0:T(8,128)(2,1)}, bf16[16,32,128]{2,1,0:T(8,128)(2,1)S(1)}, u32[]{:S(2)}, u32[]{:S(2)}) %collective-permute-start) | collective-permute-done | bytes 131104 | tf_op jit(solution)/shard_map/ppermute | solution.py:44
  18.6 1.8 %pad_maximum_fusion = bf16[64,32,128]{2,1,0:T(8,128)(2,1)} fusion(bf16[16,32,128]{2,1,0:T(8,128)(2,1)S(1)} %collective-permute-done.2, bf16[16,32,128]{2,1,0:T(8,128)(2,1)S(1)} %collective-permute-done.1, bf16[16,32,128]{2,1,0:T(8,128)(2,1)S(1)} %collective-permute-done, bf16[16,32,128]{2,1,0:T(8,128)(2,1)} %param.6), kind=kLoop, calls=%fused_computation.15 | loop fusion | flops 786432 | bytes 1048576 | tf_op jit(solution)/shard_map/concatenate | solution.py:48
  22.8 2.1 %gather_fusion.1 = s32[256]{0:T(256)S(1)} fusion(s32[16384]{0:T(1024)} %param.10, s32[1024]{0:T(1024)S(1)} %pad_clamp_fusion.3), kind=kCustom, calls=%fused_computation.1 | custom fusion | bytes 3072 | tf_op jit(solution)/shard_map/jit(_take)/gather | solution.py:24
  26.1 1.2 scatter_custom_fusion
  28.1 11.9 %all-to-all-start.1 = ((s32[64,1,24]{2,1,0:T(1,128)}), s32[64,1,24]{2,1,0:T(1,128)S(1)}, u32[]{:S(2)}, u32[]{:S(2)}) async-start(s32[64,1,24]{2,1,0:T(1,128)} %bitcast.9), calls=%async_computation.1 | async-start | bytes 65536 | tf_op jit(solution)/shard_map/all_to_all | solution.py:50
  40.0 9.5 %all-to-all-done.1 = s32[64,1,24]{2,1,0:T(1,128)S(1)} async-done(((s32[64,1,24]{2,1,0:T(1,128)}), s32[64,1,24]{2,1,0:T(1,128)S(1)}, u32[]{:S(2)}, u32[]{:S(2)}) %all-to-all-start.1) | async-done | bytes 6176 | tf_op jit(solution)/shard_map/all_to_all | solution.py:50
  51.1 5.0 %gather_fusion.2 = s32[768]{0:T(1024)S(1)} fusion(s32[256]{0:T(256)S(1)} %copy-done.1, s32[1024]{0:T(1024)S(1)} %pad_clamp_fusion.2), kind=kCustom, calls=%fused_computation.2 | custom fusion | bytes 9216 | tf_op jit(solution)/shard_map/jit(_take)/gather | solution.py:76
  56.2 4.5 %gather_fusion.4 = bf16[768,32,128]{2,1,0:T(8,128)(2,1)} fusion(bf16[256,32,128]{2,1,0:T(8,128)(2,1)S(1)} %copy-done, s32[1024]{0:T(1024)S(1)} %pad_clamp_fusion.2), kind=kCustom, calls=%fused_computation.4 | custom fusion | bytes 12585984 | tf_op jit(solution)/shard_map/jit(_take)/gather | solution.py:73
  61.0 19.1 %all-gather.2.cloned.1.call-done = bf16[1024,32,128]{2,1,0:T(8,128)(2,1)} async-done(((bf16[64,32,128]{2,1,0:T(8,128)(2,1)}), bf16[1024,32,128]{2,1,0:T(8,128)(2,1)}) %all-gather.2.cloned.1.call-update) | async-done | bytes 8388624 | tf_op jit(solution)/shard_map/all_gather | solution.py:47
  80.1 17.2 %convolution_reduce_fusion = f32[32768]{0:T(1024)S(1)} fusion(bf16[32768,128]{1,0:T(8,128)(2,1)} %bitcast.53, bf16[768,128]{1,0:T(8,128)(2,1)S(1)} %copy-done.3), kind=kOutput, calls=%fused_computation.7 | convolution fusion | flops 6467584000 | bytes 8716288 | tf_op jit(solution)/shard_map/rd,cd->rc/dot_general | solution.py:55
  98.1 0.9 reshape.670
  99.0 7.6 %all-to-all-start = ((f32[64,1,512]{2,1,0:T(1,128)}), f32[64,1,512]{2,1,0:T(1,128)S(1)}, u32[]{:S(2)}, u32[]{:S(2)}) async-start(f32[64,1,512]{2,1,0:T(1,128)} %reshape.670), calls=%async_computation | async-start | bytes 262144 | tf_op jit(solution)/shard_map/all_to_all | solution.py:63
  106.6 8.3 %gather_fusion.3 = bf16[768,32,128]{2,1,0:T(8,128)(2,1)} fusion(bf16[1024,32,128]{2,1,0:T(8,128)(2,1)} %all-gather.2.cloned.1.call-done, s32[1024]{0:T(1024)S(1)} %pad_clamp_fusion.1), kind=kCustom, calls=%fused_computation.3 | custom fusion | bytes 12585984 | tf_op jit(solution)/shard_map/jit(_take)/gather | solution.py:72
  114.9 8.3 %select_reduce_fusion = f32[768,32]{1,0:T(8,128)S(1)} fusion(pred[768,32]{1,0:T(8,128)(4,1)S(1)} %broadcast_compare_fusion, bf16[768,32,128]{2,1,0:T(8,128)(2,1)} %gather_fusion.4, pred[768]{0:T(1024)(128)(4,1)S(1)} %le.102, bf16[768,32,128]{2,1,0:T(8,128)(2,1)} %gather_fusion.3, pred[768]{0:T(1024)(128)(4,1)S(1)} %compare_and_fusion), kind=kOutput, calls=%fused_computation.8 | convolution fusion | flops 209166336 | bytes 12707328 | tf_op jit(solution)/shard_map/ntd,npd->ntp/dot_general | solution.py:74
  123.8 1.0 reduce.8
  125.2 2.8 %collective-permute-start.4 = (f32[784,32]{0,1:T(8,128)S(1)}, f32[784,32]{0,1:T(8,128)S(1)}, u32[]{:S(2)}, u32[]{:S(2)}) collective-permute-start(f32[784,32]{0,1:T(8,128)S(1)} %pad_maximum_fusion.1), channel_id=1, source_target_pairs={{0,2},{1,3},{2,0},{3,1},{4,6},{5,7},{6,4},{7,5},{8,10},{9,11},{10,... | collective-permute-start | bytes 301064 | tf_op jit(solution)/shard_map/ppermute | solution.py:83
  128.0 0.9 collective-permute-start.5
  129.5 1.6 collective-permute-done.4
  131.1 2.5 %collective-permute-done.5 = f32[784,32]{0,1:T(8,128)S(1)} collective-permute-done((f32[784,32]{0,1:T(8,128)S(1)}, f32[784,32]{0,1:T(8,128)S(1)}, u32[]{:S(2)}, u32[]{:S(2)}) %collective-permute-start.5) | collective-permute-done | bytes 100384 | tf_op jit(solution)/shard_map/ppermute | solution.py:83
  134.7 12.0 %all-to-all-start.2 = ((f32[64,1,12]{2,1,0:T(1,128)}), f32[64,1,12]{2,1,0:T(1,128)S(1)}, u32[]{:S(2)}, u32[]{:S(2)}) async-start(f32[64,1,12]{2,1,0:T(1,128)} %bitcast.11), calls=%async_computation.2 | async-start | bytes 65536 | tf_op jit(solution)/shard_map/all_to_all | solution.py:91
  147.6 8.5 %all-to-all-done.2 = f32[64,1,12]{2,1,0:T(1,128)S(1)} async-done(((f32[64,1,12]{2,1,0:T(1,128)}), f32[64,1,12]{2,1,0:T(1,128)S(1)}, u32[]{:S(2)}, u32[]{:S(2)}) %all-to-all-start.2) | async-done | bytes 3104 | tf_op jit(solution)/shard_map/all_to_all | solution.py:91
  157.4 1.4 gather_fusion.5
  (83 shorter events, 13.0 us)
Async XLA Ops:
  7.2 49.0 %copy-start = (bf16[256,32,128]{2,1,0:T(8,128)(2,1)S(1)}, bf16[256,32,128]{2,1,0:T(8,128)(2,1)}, u32[]{:S(2)}) copy-start(bf16[256,32,128]{2,1,0:T(8,128)(2,1)} %param.8) | copy-start | bytes 6291460
  7.2 43.9 %copy-start.1 = (s32[256]{0:T(256)S(1)}, s32[256]{0:T(256)}, u32[]{:S(2)}) copy-start(s32[256]{0:T(256)} %param.9) | copy-start | bytes 3076
  7.2 72.9 %all-gather.2.cloned.1.call-start = ((), (), s32[]{:S(2)}) async-start(), calls=%async_computation.3 | async-start | bytes 8912896 | tf_op jit(solution)/shard_map/all_gather | solution.py:47
  7.2 6.5 %collective-permute-start.1 = (bf16[16,32,128]{2,1,0:T(8,128)(2,1)}, bf16[16,32,128]{2,1,0:T(8,128)(2,1)S(1)}, u32[]{:S(2)}, u32[]{:S(2)}) collective-permute-start(bf16[16,32,128]{2,1,0:T(8,128)(2,1)} %param.6), channel_id=1, source_target_pairs={{0,128},{64,192},{128,0},{192,64},{1,129},{65,193},{129,1},{193,65... | collective-permute-start | bytes 393224 | tf_op jit(solution)/shard_map/ppermute | solution.py:44
  11.1 7.6 %collective-permute-start = (bf16[16,32,128]{2,1,0:T(8,128)(2,1)}, bf16[16,32,128]{2,1,0:T(8,128)(2,1)S(1)}, u32[]{:S(2)}, u32[]{:S(2)}) collective-permute-start(bf16[16,32,128]{2,1,0:T(8,128)(2,1)} %param.6), channel_id=1, source_target_pairs={{0,64},{64,128},{128,192},{192,0},{1,65},{65,129},{129,193},{193,1... | collective-permute-start | bytes 393224 | tf_op jit(solution)/shard_map/ppermute | solution.py:44
  11.5 7.2 %collective-permute-start.2 = (bf16[16,32,128]{2,1,0:T(8,128)(2,1)}, bf16[16,32,128]{2,1,0:T(8,128)(2,1)S(1)}, u32[]{:S(2)}, u32[]{:S(2)}) collective-permute-start(bf16[16,32,128]{2,1,0:T(8,128)(2,1)} %param.6), channel_id=1, source_target_pairs={{0,192},{64,0},{128,64},{192,128},{1,193},{65,1},{129,65},{193,129... | collective-permute-start | bytes 393224 | tf_op jit(solution)/shard_map/ppermute | solution.py:44
  28.1 21.5 %all-to-all-start.1 = ((s32[64,1,24]{2,1,0:T(1,128)}), s32[64,1,24]{2,1,0:T(1,128)S(1)}, u32[]{:S(2)}, u32[]{:S(2)}) async-start(s32[64,1,24]{2,1,0:T(1,128)} %bitcast.9), calls=%async_computation.1 | async-start | bytes 65536 | tf_op jit(solution)/shard_map/all_to_all | solution.py:50
  56.1 23.9 %copy-start.3 = (bf16[768,128]{1,0:T(8,128)(2,1)S(1)}, bf16[768,128]{1,0:T(8,128)(2,1)}, u32[]{:S(2)}) copy-start(bf16[768,128]{1,0:T(8,128)(2,1)} %param.7) | copy-start | bytes 589828
  99.0 24.3 %all-to-all-start = ((f32[64,1,512]{2,1,0:T(1,128)}), f32[64,1,512]{2,1,0:T(1,128)S(1)}, u32[]{:S(2)}, u32[]{:S(2)}) async-start(f32[64,1,512]{2,1,0:T(1,128)} %reshape.670), calls=%async_computation | async-start | bytes 262144 | tf_op jit(solution)/shard_map/all_to_all | solution.py:63
  114.9 44.0 %copy-start.2 = (s32[16,16]{1,0:T(8,128)S(1)}, s32[16,16]{1,0:T(8,128)}, u32[]{:S(2)}) copy-start(s32[16,16]{1,0:T(8,128)} %param.11) | copy-start | bytes 3076
  125.2 5.8 %collective-permute-start.4 = (f32[784,32]{0,1:T(8,128)S(1)}, f32[784,32]{0,1:T(8,128)S(1)}, u32[]{:S(2)}, u32[]{:S(2)}) collective-permute-start(f32[784,32]{0,1:T(8,128)S(1)} %pad_maximum_fusion.1), channel_id=1, source_target_pairs={{0,2},{1,3},{2,0},{3,1},{4,6},{5,7},{6,4},{7,5},{8,10},{9,11},{10,... | collective-permute-start | bytes 301064 | tf_op jit(solution)/shard_map/ppermute | solution.py:83
  128.0 5.5 %collective-permute-start.5 = (f32[784,32]{0,1:T(8,128)S(1)}, f32[784,32]{0,1:T(8,128)S(1)}, u32[]{:S(2)}, u32[]{:S(2)}) collective-permute-start(f32[784,32]{0,1:T(8,128)S(1)} %pad_maximum_fusion.1), channel_id=1, source_target_pairs={{0,3},{1,0},{2,1},{3,2},{4,7},{5,4},{6,5},{7,6},{8,11},{9,8},{10,9... | collective-permute-start | bytes 301064 | tf_op jit(solution)/shard_map/ppermute | solution.py:83
  128.9 4.9 %collective-permute-start.3 = (f32[784,32]{0,1:T(8,128)S(1)}, f32[784,32]{0,1:T(8,128)S(1)}, u32[]{:S(2)}, u32[]{:S(2)}) collective-permute-start(f32[784,32]{0,1:T(8,128)S(1)} %pad_maximum_fusion.1), channel_id=1, source_target_pairs={{0,1},{1,2},{2,3},{3,0},{4,5},{5,6},{6,7},{7,4},{8,9},{9,10},{10,1... | collective-permute-start | bytes 301064 | tf_op jit(solution)/shard_map/ppermute | solution.py:83
  134.7 21.4 %all-to-all-start.2 = ((f32[64,1,12]{2,1,0:T(1,128)}), f32[64,1,12]{2,1,0:T(1,128)S(1)}, u32[]{:S(2)}, u32[]{:S(2)}) async-start(f32[64,1,12]{2,1,0:T(1,128)} %bitcast.11), calls=%async_computation.2 | async-start | bytes 65536 | tf_op jit(solution)/shard_map/all_to_all | solution.py:91
Sparse Core Ops, SparseCore 0:
  20.5 59.4 all-gather.1

commit v9 on v8

--- a/solution.py
+++ b/solution.py
@@ -60,8 +60,6 @@
         .transpose(1, 0, 2, 3)
         .reshape(shard_total, query_count, query_tokens)
     )
-    gathered_best = lax.all_to_all(local_best, shard, split_axis=0, concat_axis=0, tiled=True)
-    shard_best = jnp.max(gathered_best, axis=0)
 
     slot_table = jnp.maximum(mine[..., 0], 0).reshape(-1)
     global_query = jnp.maximum(mine[..., 1], 0).reshape(-1)
@@ -77,7 +75,7 @@
     pair_scored = jnp.where(valid_tokens[:, None, :], pair_scored, masked_score)
     partial_value = jnp.max(pair_scored, axis=2)
 
-    merged = jnp.concatenate([shard_best, partial_value], axis=0)
+    merged = jnp.concatenate([local_best.reshape(-1, query_tokens), partial_value], axis=0)
     cent_total = lax.axis_size("cent")
     arrived = [
         lax.ppermute(merged, "cent", [(i, (i + shift) % cent_total) for i in range(cent_total)])
@@ -85,10 +83,17 @@
     ]
     for other in arrived:
         merged = jnp.maximum(merged, other)
-    token_best = merged[:query_count]
-    complete = merged[query_count:]
+    token_rows_out = shard_total * query_count
+    best_all = merged[:token_rows_out].reshape(shard_total, query_count * query_tokens)
+    complete = merged[token_rows_out:]
     pair_scores = (jnp.sum(complete, axis=1) / query_tokens).reshape(shard_total, capacity)
-    returned = lax.all_to_all(pair_scores, shard, split_axis=0, concat_axis=0, tiled=True)
+
+    outgoing = jnp.concatenate([best_all, pair_scores], axis=1)
+    incoming = lax.all_to_all(outgoing, shard, split_axis=0, concat_axis=0, tiled=True)
+    token_best = jnp.max(incoming[:, : query_count * query_tokens], axis=0).reshape(
+        query_count, query_tokens
+    )
+    returned = incoming[:, query_count * query_tokens:]
 
     scores = jnp.take(returned.reshape(-1), my_places, axis=0).reshape(query_count, per_query)
     return (token_best, scores)

time: 167 us -> 159 us (0.952)
  starting transfers between devices: 42.2 us -> 30.6 us
  waiting for transfers between devices: 46.2 us -> 53.6 us
  other arithmetic: 5.79 us -> 3.89 us
    all_to_all x2 -> x1, starting transfers between devices: 19.6 us -> 7.93 us  [per_device(): lax.all_to_all(outgoing, shard, split_axis=0, concat_axis=0, tiled=True)]
    ppermute x3, waiting for transfers between devices: 4.27 us -> 9.68 us  [per_device(): lax.ppermute(merged, 'cent', [(i, (i + shift) % cent_total) for i in rang...]
    all_to_all x2 -> x1, waiting for transfers between devices: 8.46 us -> 10.4 us  [per_device(): lax.all_to_all(outgoing, shard, split_axis=0, concat_axis=0, tiled=True)]
    unnamed x11 -> x9, local copies, waits for them, and re-layouts: 1.76 us -> 0.04 us
  transfers between devices with their start and end apart: 10 -> 9, of which waited for: 7 -> 7; matrix products, arithmetic and copies ran while one was open for 21% -> 12% of each run, Pallas kernels for 0% -> 0%
where the time goes in v9:
time: 159 us
  waiting for transfers between devices  53.6 us (34%)
  local copies, waits for them, and re-layouts  30.8 us (19%)
  starting transfers between devices  30.6 us (19%)
  matrix products  25.5 us (16%)
  between operations  14.4 us (9%)
  other arithmetic  3.89 us (2%)
    all_gather x1, waiting for transfers between devices, per_device(): lax.all_gather(jnp.concatenate(along_y, axis=0), 'rest', axis=0, tiled=True)  19.1 us
    dot_general x1, matrix products, per_device(): jnp.einsum('rd,cd->rc', flattened, centroids, preferred_element_type=jnp....  17.2 us
    all_to_all x1, starting transfers between devices, per_device(): lax.all_to_all(table, shard, split_axis=0, concat_axis=0, tiled=True)  11.9 us
    all_to_all x1, waiting for transfers between devices, per_device(): lax.all_to_all(outgoing, shard, split_axis=0, concat_axis=0, tiled=True)  10.4 us
    ppermute x3, waiting for transfers between devices, per_device(): lax.ppermute(merged, 'cent', [(i, (i + shift) % cent_total) for i in rang...  9.68 us
    all_to_all x1, waiting for transfers between devices, per_device(): lax.all_to_all(table, shard, split_axis=0, concat_axis=0, tiled=True)  9.53 us
    gather x1, local copies, waits for them, and re-layouts, per_device(): asked = jnp.take(query_block, query_table, axis=0)  8.3 us
    dot_general x1, matrix products, per_device(): jnp.einsum('ntd,npd->ntp', asked, chosen, preferred_element_type=jnp.floa...  8.3 us
  transfers between devices with their start and end apart: 9, of which 7 were waited for; matrix products, arithmetic and copies ran while one was open for 12% of the time, Pallas kernels for 0%

profile of v9, /device:TPU:1, one launch (start us, length us, event | category | flops | bytes accessed | tf_op | source)
XLA Modules:
  0.0 158.8 jit_solution(12887956598735191495)
XLA Ops:
  7.2 3.8 %collective-permute-start.1 = (bf16[16,32,128]{2,1,0:T(8,128)(2,1)}, bf16[16,32,128]{2,1,0:T(8,128)(2,1)S(1)}, u32[]{:S(2)}, u32[]{:S(2)}) collective-permute-start(bf16[16,32,128]{2,1,0:T(8,128)(2,1)} %param.6), channel_id=1, source_target_pairs={{0,128},{64,192},{128,0},{192,64},{1,129},{65,193},{129,1},{193,65... | collective-permute-start | bytes 393224 | tf_op jit(solution)/shard_map/ppermute | solution.py:44
  11.5 2.3 %collective-permute-start.2 = (bf16[16,32,128]{2,1,0:T(8,128)(2,1)}, bf16[16,32,128]{2,1,0:T(8,128)(2,1)S(1)}, u32[]{:S(2)}, u32[]{:S(2)}) collective-permute-start(bf16[16,32,128]{2,1,0:T(8,128)(2,1)} %param.6), channel_id=1, source_target_pairs={{0,192},{64,0},{128,64},{192,128},{1,193},{65,1},{129,65},{193,129... | collective-permute-start | bytes 393224 | tf_op jit(solution)/shard_map/ppermute | solution.py:44
  13.7 4.9 %collective-permute-done = bf16[16,32,128]{2,1,0:T(8,128)(2,1)S(1)} collective-permute-done((bf16[16,32,128]{2,1,0:T(8,128)(2,1)}, bf16[16,32,128]{2,1,0:T(8,128)(2,1)S(1)}, u32[]{:S(2)}, u32[]{:S(2)}) %collective-permute-start) | collective-permute-done | bytes 131104 | tf_op jit(solution)/shard_map/ppermute | solution.py:44
  18.6 1.8 %pad_maximum_fusion = bf16[64,32,128]{2,1,0:T(8,128)(2,1)} fusion(bf16[16,32,128]{2,1,0:T(8,128)(2,1)S(1)} %collective-permute-done.2, bf16[16,32,128]{2,1,0:T(8,128)(2,1)S(1)} %collective-permute-done.1, bf16[16,32,128]{2,1,0:T(8,128)(2,1)S(1)} %collective-permute-done, bf16[16,32,128]{2,1,0:T(8,128)(2,1)} %param.6), kind=kLoop, calls=%fused_computation.15 | loop fusion | flops 786432 | bytes 1048576 | tf_op jit(solution)/shard_map/concatenate | solution.py:48
  20.4 0.8 reshape.584
  21.2 0.8 reshape.585
  22.8 2.1 %gather_fusion.1 = s32[256]{0:T(256)S(1)} fusion(s32[16384]{0:T(1024)} %param.10, s32[1024]{0:T(1024)S(1)} %pad_clamp_fusion.3), kind=kCustom, calls=%fused_computation.1 | custom fusion | bytes 3072 | tf_op jit(solution)/shard_map/jit(_take)/gather | solution.py:24
  26.1 1.2 scatter_custom_fusion
  28.1 11.9 %all-to-all-start = ((s32[64,1,24]{2,1,0:T(1,128)}), s32[64,1,24]{2,1,0:T(1,128)S(1)}, u32[]{:S(2)}, u32[]{:S(2)}) async-start(s32[64,1,24]{2,1,0:T(1,128)} %bitcast.9), calls=%async_computation | async-start | bytes 65536 | tf_op jit(solution)/shard_map/all_to_all | solution.py:50
  40.0 9.5 %all-to-all-done = s32[64,1,24]{2,1,0:T(1,128)S(1)} async-done(((s32[64,1,24]{2,1,0:T(1,128)}), s32[64,1,24]{2,1,0:T(1,128)S(1)}, u32[]{:S(2)}, u32[]{:S(2)}) %all-to-all-start) | async-done | bytes 6176 | tf_op jit(solution)/shard_map/all_to_all | solution.py:50
  51.1 5.0 %gather_fusion.2 = s32[768]{0:T(1024)S(1)} fusion(s32[256]{0:T(256)S(1)} %copy-done.1, s32[1024]{0:T(1024)S(1)} %pad_clamp_fusion.2), kind=kCustom, calls=%fused_computation.2 | custom fusion | bytes 9216 | tf_op jit(solution)/shard_map/jit(_take)/gather | solution.py:74
  56.2 4.5 %gather_fusion.4 = bf16[768,32,128]{2,1,0:T(8,128)(2,1)} fusion(bf16[256,32,128]{2,1,0:T(8,128)(2,1)S(1)} %copy-done, s32[1024]{0:T(1024)S(1)} %pad_clamp_fusion.2), kind=kCustom, calls=%fused_computation.4 | custom fusion | bytes 12585984 | tf_op jit(solution)/shard_map/jit(_take)/gather | solution.py:71
  61.0 19.1 %all-gather.2.cloned.1.call-done = bf16[1024,32,128]{2,1,0:T(8,128)(2,1)} async-done(((bf16[64,32,128]{2,1,0:T(8,128)(2,1)}), bf16[1024,32,128]{2,1,0:T(8,128)(2,1)}) %all-gather.2.cloned.1.call-update) | async-done | bytes 8388624 | tf_op jit(solution)/shard_map/all_gather | solution.py:47
  80.1 17.2 %convolution_reduce_fusion = f32[32768]{0:T(1024)S(1)} fusion(bf16[32768,128]{1,0:T(8,128)(2,1)} %bitcast.57, bf16[768,128]{1,0:T(8,128)(2,1)S(1)} %copy-done.3), kind=kOutput, calls=%fused_computation.7 | convolution fusion | flops 6467584000 | bytes 8716288 | tf_op jit(solution)/shard_map/rd,cd->rc/dot_general | solution.py:55
  98.3 8.3 %gather_fusion.3 = bf16[768,32,128]{2,1,0:T(8,128)(2,1)} fusion(bf16[1024,32,128]{2,1,0:T(8,128)(2,1)} %all-gather.2.cloned.1.call-done, s32[1024]{0:T(1024)S(1)} %pad_clamp_fusion.1), kind=kCustom, calls=%fused_computation.3 | custom fusion | bytes 12585984 | tf_op jit(solution)/shard_map/jit(_take)/gather | solution.py:70
  106.6 8.3 %select_reduce_fusion = f32[768,32]{1,0:T(8,128)S(1)} fusion(pred[768,32]{1,0:T(8,128)(4,1)S(1)} %broadcast_compare_fusion, bf16[768,32,128]{2,1,0:T(8,128)(2,1)} %gather_fusion.4, pred[768]{0:T(1024)(128)(4,1)S(1)} %le.102, bf16[768,32,128]{2,1,0:T(8,128)(2,1)} %gather_fusion.3, pred[768]{0:T(1024)(128)(4,1)S(1)} %compare_and_fusion), kind=kOutput, calls=%fused_computation.8 | convolution fusion | flops 209166336 | bytes 12707328 | tf_op jit(solution)/shard_map/ntd,npd->ntp/dot_general | solution.py:72
  115.1 2.8 %collective-permute-start.4 = (f32[1792,32]{0,1:T(8,128)S(1)}, f32[1792,32]{0,1:T(8,128)S(1)}, u32[]{:S(2)}, u32[]{:S(2)}) collective-permute-start(f32[1792,32]{0,1:T(8,128)S(1)} %pad_maximum_fusion.1), channel_id=1, source_target_pairs={{0,2},{1,3},{2,0},{3,1},{4,6},{5,7},{6,4},{7,5},{8,10},{9,11},{10,... | collective-permute-start | bytes 688136 | tf_op jit(solution)/shard_map/ppermute | solution.py:81
  117.9 0.9 collective-permute-start.5
  119.3 4.2 %collective-permute-done.4 = f32[1792,32]{0,1:T(8,128)S(1)} collective-permute-done((f32[1792,32]{0,1:T(8,128)S(1)}, f32[1792,32]{0,1:T(8,128)S(1)}, u32[]{:S(2)}, u32[]{:S(2)}) %collective-permute-start.4) | collective-permute-done | bytes 229408 | tf_op jit(solution)/shard_map/ppermute | solution.py:81
  123.6 5.0 %collective-permute-done.5 = f32[1792,32]{0,1:T(8,128)S(1)} collective-permute-done((f32[1792,32]{0,1:T(8,128)S(1)}, f32[1792,32]{0,1:T(8,128)S(1)}, u32[]{:S(2)}, u32[]{:S(2)}) %collective-permute-start.5) | collective-permute-done | bytes 229408 | tf_op jit(solution)/shard_map/ppermute | solution.py:81
  129.7 0.8 copy.76
  130.5 7.9 %all-to-all-start.1 = ((f32[64,1,524]{2,1,0:T(1,128)}), f32[64,1,524]{2,1,0:T(1,128)S(1)}, u32[]{:S(2)}, u32[]{:S(2)}) async-start(f32[64,1,524]{2,1,0:T(1,128)} %copy.76), calls=%async_computation.1 | async-start | bytes 327680 | tf_op jit(solution)/shard_map/all_to_all | solution.py:92
  138.6 10.4 %all-to-all-done.1 = f32[64,1,524]{2,1,0:T(1,128)S(1)} async-done(((f32[64,1,524]{2,1,0:T(1,128)}), f32[64,1,524]{2,1,0:T(1,128)S(1)}, u32[]{:S(2)}, u32[]{:S(2)}) %all-to-all-start.1) | async-done | bytes 134176 | tf_op jit(solution)/shard_map/all_to_all | solution.py:92
  149.9 1.4 gather_fusion.5
  (81 shorter events, 9.5 us)
Async XLA Ops:
  7.2 49.0 %copy-start = (bf16[256,32,128]{2,1,0:T(8,128)(2,1)S(1)}, bf16[256,32,128]{2,1,0:T(8,128)(2,1)}, u32[]{:S(2)}) copy-start(bf16[256,32,128]{2,1,0:T(8,128)(2,1)} %param.8) | copy-start | bytes 6291460
  7.2 43.9 %copy-start.1 = (s32[256]{0:T(256)S(1)}, s32[256]{0:T(256)}, u32[]{:S(2)}) copy-start(s32[256]{0:T(256)} %param.9) | copy-start | bytes 3076
  7.2 72.9 %all-gather.2.cloned.1.call-start = ((), (), s32[]{:S(2)}) async-start(), calls=%async_computation.2 | async-start | bytes 8912896 | tf_op jit(solution)/shard_map/all_gather | solution.py:47
  7.2 6.5 %collective-permute-start.1 = (bf16[16,32,128]{2,1,0:T(8,128)(2,1)}, bf16[16,32,128]{2,1,0:T(8,128)(2,1)S(1)}, u32[]{:S(2)}, u32[]{:S(2)}) collective-permute-start(bf16[16,32,128]{2,1,0:T(8,128)(2,1)} %param.6), channel_id=1, source_target_pairs={{0,128},{64,192},{128,0},{192,64},{1,129},{65,193},{129,1},{193,65... | collective-permute-start | bytes 393224 | tf_op jit(solution)/shard_map/ppermute | solution.py:44
  11.1 7.6 %collective-permute-start = (bf16[16,32,128]{2,1,0:T(8,128)(2,1)}, bf16[16,32,128]{2,1,0:T(8,128)(2,1)S(1)}, u32[]{:S(2)}, u32[]{:S(2)}) collective-permute-start(bf16[16,32,128]{2,1,0:T(8,128)(2,1)} %param.6), channel_id=1, source_target_pairs={{0,64},{64,128},{128,192},{192,0},{1,65},{65,129},{129,193},{193,1... | collective-permute-start | bytes 393224 | tf_op jit(solution)/shard_map/ppermute | solution.py:44
  11.5 7.2 %collective-permute-start.2 = (bf16[16,32,128]{2,1,0:T(8,128)(2,1)}, bf16[16,32,128]{2,1,0:T(8,128)(2,1)S(1)}, u32[]{:S(2)}, u32[]{:S(2)}) collective-permute-start(bf16[16,32,128]{2,1,0:T(8,128)(2,1)} %param.6), channel_id=1, source_target_pairs={{0,192},{64,0},{128,64},{192,128},{1,193},{65,1},{129,65},{193,129... | collective-permute-start | bytes 393224 | tf_op jit(solution)/shard_map/ppermute | solution.py:44
  28.1 21.5 %all-to-all-start = ((s32[64,1,24]{2,1,0:T(1,128)}), s32[64,1,24]{2,1,0:T(1,128)S(1)}, u32[]{:S(2)}, u32[]{:S(2)}) async-start(s32[64,1,24]{2,1,0:T(1,128)} %bitcast.9), calls=%async_computation | async-start | bytes 65536 | tf_op jit(solution)/shard_map/all_to_all | solution.py:50
  56.1 23.9 %copy-start.3 = (bf16[768,128]{1,0:T(8,128)(2,1)S(1)}, bf16[768,128]{1,0:T(8,128)(2,1)}, u32[]{:S(2)}) copy-start(bf16[768,128]{1,0:T(8,128)(2,1)} %param.7) | copy-start | bytes 589828
  114.9 36.4 %copy-start.2 = (s32[16,16]{1,0:T(8,128)S(1)}, s32[16,16]{1,0:T(8,128)}, u32[]{:S(2)}) copy-start(s32[16,16]{1,0:T(8,128)} %param.11) | copy-start | bytes 3076
  115.1 8.5 %collective-permute-start.4 = (f32[1792,32]{0,1:T(8,128)S(1)}, f32[1792,32]{0,1:T(8,128)S(1)}, u32[]{:S(2)}, u32[]{:S(2)}) collective-permute-start(f32[1792,32]{0,1:T(8,128)S(1)} %pad_maximum_fusion.1), channel_id=1, source_target_pairs={{0,2},{1,3},{2,0},{3,1},{4,6},{5,7},{6,4},{7,5},{8,10},{9,11},{10,... | collective-permute-start | bytes 688136 | tf_op jit(solution)/shard_map/ppermute | solution.py:81
  117.9 10.7 %collective-permute-start.5 = (f32[1792,32]{0,1:T(8,128)S(1)}, f32[1792,32]{0,1:T(8,128)S(1)}, u32[]{:S(2)}, u32[]{:S(2)}) collective-permute-start(f32[1792,32]{0,1:T(8,128)S(1)} %pad_maximum_fusion.1), channel_id=1, source_target_pairs={{0,3},{1,0},{2,1},{3,2},{4,7},{5,4},{6,5},{7,6},{8,11},{9,8},{10,9... | collective-permute-start | bytes 688136 | tf_op jit(solution)/shard_map/ppermute | solution.py:81
  118.7 10.3 %collective-permute-start.3 = (f32[1792,32]{0,1:T(8,128)S(1)}, f32[1792,32]{0,1:T(8,128)S(1)}, u32[]{:S(2)}, u32[]{:S(2)}) collective-permute-start(f32[1792,32]{0,1:T(8,128)S(1)} %pad_maximum_fusion.1), channel_id=1, source_target_pairs={{0,1},{1,2},{2,3},{3,0},{4,5},{5,6},{6,7},{7,4},{8,9},{9,10},{10,1... | collective-permute-start | bytes 688136 | tf_op jit(solution)/shard_map/ppermute | solution.py:81
  130.5 18.5 %all-to-all-start.1 = ((f32[64,1,524]{2,1,0:T(1,128)}), f32[64,1,524]{2,1,0:T(1,128)S(1)}, u32[]{:S(2)}, u32[]{:S(2)}) async-start(f32[64,1,524]{2,1,0:T(1,128)} %copy.76), calls=%async_computation.1 | async-start | bytes 327680 | tf_op jit(solution)/shard_map/all_to_all | solution.py:92
Sparse Core Ops, SparseCore 0:
  20.5 59.4 all-gather.1

commit v10 on v9

--- a/solution.py
+++ b/solution.py
@@ -1,9 +1,35 @@
 import jax
 import jax.numpy as jnp
 from jax import lax
+from jax.experimental import pallas as pl
 from jax.sharding import Mesh, PartitionSpec as P
 
 masked_score = -1e30
+
+
+def centroid_best(rows, centroids):
+    row_total, width = rows.shape
+    block = 2048 if row_total % 2048 == 0 else row_total
+    steps = row_total // block
+
+    def kernel(row_ref, centroid_ref, out_ref):
+        scored = lax.dot_general(
+            centroid_ref[...], row_ref[...], (((1,), (1,)), ((), ())),
+            preferred_element_type=jnp.float32,
+        )
+        out_ref[...] = jnp.max(scored, axis=0).reshape(1, 1, block)
+
+    best = pl.pallas_call(
+        kernel,
+        grid=(steps,),
+        in_specs=[
+            pl.BlockSpec((block, width), lambda i: (i, 0)),
+            pl.BlockSpec(centroids.shape, lambda i: (0, 0)),
+        ],
+        out_specs=pl.BlockSpec((1, 1, block), lambda i: (i, 0, 0)),
+        out_shape=jax.ShapeDtypeStruct((steps, 1, block), jnp.float32),
+    )(rows, centroids)
+    return best.reshape(row_total)
 
 
 shard = ("y", "rest")
@@ -51,9 +77,9 @@
         shard_total, capacity, 2
     )
 
-    flattened = query_block.reshape(-1, feature_width)
-    scored = jnp.einsum("rd,cd->rc", flattened, centroids, preferred_element_type=jnp.float32)
-    by_shift = jnp.max(scored, axis=1).reshape(rest_total, y_total, query_count, query_tokens)
+    by_shift = centroid_best(query_block.reshape(-1, feature_width), centroids).reshape(
+        rest_total, y_total, query_count, query_tokens
+    )
     shift_of_y = (my_y - jnp.arange(y_total, dtype=jnp.int32)) % y_total
     local_best = (
         jnp.take(by_shift, shift_of_y, axis=1)

time: 159 us -> 162 us (1.019)
  Pallas kernels: 0 us -> 18.1 us
  matrix products: 25.5 us -> 8.3 us
    pallas_call x0 -> x1, Pallas kernels: none -> 18.1 us  [centroid_best(): pl.pallas_call(kernel, grid=(steps,), in_specs=[pl.BlockSpec((block, widt...]
    dot_general x1 -> x0, matrix products: 17.2 us -> none  [per_device(): jnp.einsum('rd,cd->rc', flattened, centroids, preferred_element_type=jnp....]
  transfers between devices with their start and end apart: 9 -> 9, of which waited for: 7 -> 7; matrix products, arithmetic and copies ran while one was open for 12% -> 11% of each run, Pallas kernels for 0% -> 0%
where the time goes in v10:
time: 162 us; the launch traced here: 161 us
  waiting for transfers between devices  53.6 us (33%)
  local copies, waits for them, and re-layouts  30.8 us (19%)
  starting transfers between devices  30.6 us (19%)
  Pallas kernels  18.1 us (11%)
  between operations  14.4 us (9%)
  matrix products  8.3 us (5%)
  other arithmetic  5.11 us (3%)
    all_gather x1, waiting for transfers between devices, per_device(): lax.all_gather(jnp.concatenate(along_y, axis=0), 'rest', axis=0, tiled=True)  19.1 us
    pallas_call x1, Pallas kernels, centroid_best(): pl.pallas_call(kernel, grid=(steps,), in_specs=[pl.BlockSpec((block, widt...  18.1 us
    all_to_all x1, starting transfers between devices, per_device(): lax.all_to_all(table, shard, split_axis=0, concat_axis=0, tiled=True)  11.9 us
    all_to_all x1, waiting for transfers between devices, per_device(): lax.all_to_all(outgoing, shard, split_axis=0, concat_axis=0, tiled=True)  10.4 us
    ppermute x3, waiting for transfers between devices, per_device(): lax.ppermute(merged, 'cent', [(i, (i + shift) % cent_total) for i in rang...  9.68 us
    all_to_all x1, waiting for transfers between devices, per_device(): lax.all_to_all(table, shard, split_axis=0, concat_axis=0, tiled=True)  9.53 us
    gather x1, local copies, waits for them, and re-layouts, per_device(): asked = jnp.take(query_block, query_table, axis=0)  8.3 us
    dot_general x1, matrix products, per_device(): jnp.einsum('ntd,npd->ntp', asked, chosen, preferred_element_type=jnp.floa...  8.3 us
  transfers between devices with their start and end apart: 9, of which 7 were waited for; matrix products, arithmetic and copies ran while one was open for 11% of the time, Pallas kernels for 0%

profile of v10, /device:TPU:1, one launch (start us, length us, event | category | flops | bytes accessed | tf_op | source)
XLA Modules:
  0.0 160.9 jit_solution(9906124531558317253)
XLA Ops:
  7.2 3.8 %collective-permute-start.1 = (bf16[16,32,128]{2,1,0:T(8,128)(2,1)}, bf16[16,32,128]{2,1,0:T(8,128)(2,1)S(1)}, u32[]{:S(2)}, u32[]{:S(2)}) collective-permute-start(bf16[16,32,128]{2,1,0:T(8,128)(2,1)} %param.6), channel_id=1, source_target_pairs={{0,128},{64,192},{128,0},{192,64},{1,129},{65,193},{129,1},{193,65... | collective-permute-start | bytes 393224 | tf_op jit(solution)/shard_map/ppermute | solution.py:70
  11.5 2.3 %collective-permute-start.2 = (bf16[16,32,128]{2,1,0:T(8,128)(2,1)}, bf16[16,32,128]{2,1,0:T(8,128)(2,1)S(1)}, u32[]{:S(2)}, u32[]{:S(2)}) collective-permute-start(bf16[16,32,128]{2,1,0:T(8,128)(2,1)} %param.6), channel_id=1, source_target_pairs={{0,192},{64,0},{128,64},{192,128},{1,193},{65,1},{129,65},{193,129... | collective-permute-start | bytes 393224 | tf_op jit(solution)/shard_map/ppermute | solution.py:70
  13.7 4.9 %collective-permute-done = bf16[16,32,128]{2,1,0:T(8,128)(2,1)S(1)} collective-permute-done((bf16[16,32,128]{2,1,0:T(8,128)(2,1)}, bf16[16,32,128]{2,1,0:T(8,128)(2,1)S(1)}, u32[]{:S(2)}, u32[]{:S(2)}) %collective-permute-start) | collective-permute-done | bytes 131104 | tf_op jit(solution)/shard_map/ppermute | solution.py:70
  18.6 1.8 %pad_maximum_fusion = bf16[64,32,128]{2,1,0:T(8,128)(2,1)} fusion(bf16[16,32,128]{2,1,0:T(8,128)(2,1)S(1)} %collective-permute-done.2, bf16[16,32,128]{2,1,0:T(8,128)(2,1)S(1)} %collective-permute-done.1, bf16[16,32,128]{2,1,0:T(8,128)(2,1)S(1)} %collective-permute-done, bf16[16,32,128]{2,1,0:T(8,128)(2,1)} %param.6), kind=kLoop, calls=%fused_computation.14 | loop fusion | flops 786432 | bytes 1048576 | tf_op jit(solution)/shard_map/concatenate | solution.py:74
  20.4 0.8 reshape.580
  22.8 2.1 %gather_fusion.1 = s32[256]{0:T(256)S(1)} fusion(s32[16384]{0:T(1024)} %param.10, s32[1024]{0:T(1024)S(1)} %pad_clamp_fusion.3), kind=kCustom, calls=%fused_computation.1 | custom fusion | bytes 3072 | tf_op jit(solution)/shard_map/jit(_take)/gather | solution.py:50
  26.1 1.2 scatter_custom_fusion
  28.1 11.9 %all-to-all-start = ((s32[64,1,24]{2,1,0:T(1,128)}), s32[64,1,24]{2,1,0:T(1,128)S(1)}, u32[]{:S(2)}, u32[]{:S(2)}) async-start(s32[64,1,24]{2,1,0:T(1,128)} %bitcast.9), calls=%async_computation | async-start | bytes 65536 | tf_op jit(solution)/shard_map/all_to_all | solution.py:76
  40.0 9.5 %all-to-all-done = s32[64,1,24]{2,1,0:T(1,128)S(1)} async-done(((s32[64,1,24]{2,1,0:T(1,128)}), s32[64,1,24]{2,1,0:T(1,128)S(1)}, u32[]{:S(2)}, u32[]{:S(2)}) %all-to-all-start) | async-done | bytes 6176 | tf_op jit(solution)/shard_map/all_to_all | solution.py:76
  51.1 5.0 %gather_fusion.2 = s32[768]{0:T(1024)S(1)} fusion(s32[256]{0:T(256)S(1)} %copy-done.1, s32[1024]{0:T(1024)S(1)} %pad_clamp_fusion.2), kind=kCustom, calls=%fused_computation.2 | custom fusion | bytes 9216 | tf_op jit(solution)/shard_map/jit(_take)/gather | solution.py:100
  56.1 4.5 %gather_fusion.4 = bf16[768,32,128]{2,1,0:T(8,128)(2,1)} fusion(bf16[256,32,128]{2,1,0:T(8,128)(2,1)S(1)} %copy-done, s32[1024]{0:T(1024)S(1)} %pad_clamp_fusion.2), kind=kCustom, calls=%fused_computation.4 | custom fusion | bytes 12585984 | tf_op jit(solution)/shard_map/jit(_take)/gather | solution.py:97
  61.0 19.1 %all-gather.2.cloned.1.call-done = bf16[1024,32,128]{2,1,0:T(8,128)(2,1)} async-done(((bf16[64,32,128]{2,1,0:T(8,128)(2,1)}), bf16[1024,32,128]{2,1,0:T(8,128)(2,1)}) %all-gather.2.cloned.1.call-update) | async-done | bytes 8388624 | tf_op jit(solution)/shard_map/all_gather | solution.py:73
  80.1 18.1 %shard_map.77 = f32[16,1,2048]{2,1,0:T(1,128)} custom-call(bf16[32768,128]{1,0:T(8,128)(2,1)} %bitcast.55, bf16[768,128]{1,0:T(8,128)(2,1)} %centroid_ref.1), custom_call_target="tpu_custom_call" | custom-call | tf_op jit(solution)/shard_map/pallas_call | solution.py:22
  98.1 1.2 reduce
  100.4 8.3 %gather_fusion.3 = bf16[768,32,128]{2,1,0:T(8,128)(2,1)} fusion(bf16[1024,32,128]{2,1,0:T(8,128)(2,1)} %all-gather.2.cloned.1.call-done, s32[1024]{0:T(1024)S(1)} %pad_clamp_fusion.1), kind=kCustom, calls=%fused_computation.3 | custom fusion | bytes 12585984 | tf_op jit(solution)/shard_map/jit(_take)/gather | solution.py:96
  108.7 8.3 %select_reduce_fusion = f32[768,32]{1,0:T(8,128)S(1)} fusion(pred[768,32]{1,0:T(8,128)(4,1)S(1)} %broadcast_compare_fusion, bf16[768,32,128]{2,1,0:T(8,128)(2,1)} %gather_fusion.4, pred[768]{0:T(1024)(128)(4,1)S(1)} %le.102, bf16[768,32,128]{2,1,0:T(8,128)(2,1)} %gather_fusion.3, pred[768]{0:T(1024)(128)(4,1)S(1)} %compare_and_fusion), kind=kOutput, calls=%fused_computation.7 | convolution fusion | flops 209166336 | bytes 12707328 | tf_op jit(solution)/shard_map/ntd,npd->ntp/dot_general | solution.py:98
  117.2 2.8 %collective-permute-start.4 = (f32[1792,32]{0,1:T(8,128)S(1)}, f32[1792,32]{0,1:T(8,128)S(1)}, u32[]{:S(2)}, u32[]{:S(2)}) collective-permute-start(f32[1792,32]{0,1:T(8,128)S(1)} %pad_maximum_fusion.1), channel_id=1, source_target_pairs={{0,2},{1,3},{2,0},{3,1},{4,6},{5,7},{6,4},{7,5},{8,10},{9,11},{10,... | collective-permute-start | bytes 688136 | tf_op jit(solution)/shard_map/ppermute | solution.py:107
  119.9 0.9 collective-permute-start.5
  121.4 4.2 %collective-permute-done.4 = f32[1792,32]{0,1:T(8,128)S(1)} collective-permute-done((f32[1792,32]{0,1:T(8,128)S(1)}, f32[1792,32]{0,1:T(8,128)S(1)}, u32[]{:S(2)}, u32[]{:S(2)}) %collective-permute-start.4) | collective-permute-done | bytes 229408 | tf_op jit(solution)/shard_map/ppermute | solution.py:107
  125.6 5.0 %collective-permute-done.5 = f32[1792,32]{0,1:T(8,128)S(1)} collective-permute-done((f32[1792,32]{0,1:T(8,128)S(1)}, f32[1792,32]{0,1:T(8,128)S(1)}, u32[]{:S(2)}, u32[]{:S(2)}) %collective-permute-start.5) | collective-permute-done | bytes 229408 | tf_op jit(solution)/shard_map/ppermute | solution.py:107
  131.8 0.8 copy.77
  132.6 7.9 %all-to-all-start.1 = ((f32[64,1,524]{2,1,0:T(1,128)}), f32[64,1,524]{2,1,0:T(1,128)S(1)}, u32[]{:S(2)}, u32[]{:S(2)}) async-start(f32[64,1,524]{2,1,0:T(1,128)} %copy.77), calls=%async_computation.1 | async-start | bytes 327680 | tf_op jit(solution)/shard_map/all_to_all | solution.py:118
  140.7 10.4 %all-to-all-done.1 = f32[64,1,524]{2,1,0:T(1,128)S(1)} async-done(((f32[64,1,524]{2,1,0:T(1,128)}), f32[64,1,524]{2,1,0:T(1,128)S(1)}, u32[]{:S(2)}, u32[]{:S(2)}) %all-to-all-start.1) | async-done | bytes 134176 | tf_op jit(solution)/shard_map/all_to_all | solution.py:118
  151.9 1.4 gather_fusion.5
  (80 shorter events, 10.3 us)
Async XLA Ops:
  7.2 49.0 %copy-start = (bf16[256,32,128]{2,1,0:T(8,128)(2,1)S(1)}, bf16[256,32,128]{2,1,0:T(8,128)(2,1)}, u32[]{:S(2)}) copy-start(bf16[256,32,128]{2,1,0:T(8,128)(2,1)} %param.8) | copy-start | bytes 6291460
  7.2 43.9 %copy-start.1 = (s32[256]{0:T(256)S(1)}, s32[256]{0:T(256)}, u32[]{:S(2)}) copy-start(s32[256]{0:T(256)} %param.9) | copy-start | bytes 3076
  7.2 72.9 %all-gather.2.cloned.1.call-start = ((), (), s32[]{:S(2)}) async-start(), calls=%async_computation.2 | async-start | bytes 8912896 | tf_op jit(solution)/shard_map/all_gather | solution.py:73
  7.2 6.5 %collective-permute-start.1 = (bf16[16,32,128]{2,1,0:T(8,128)(2,1)}, bf16[16,32,128]{2,1,0:T(8,128)(2,1)S(1)}, u32[]{:S(2)}, u32[]{:S(2)}) collective-permute-start(bf16[16,32,128]{2,1,0:T(8,128)(2,1)} %param.6), channel_id=1, source_target_pairs={{0,128},{64,192},{128,0},{192,64},{1,129},{65,193},{129,1},{193,65... | collective-permute-start | bytes 393224 | tf_op jit(solution)/shard_map/ppermute | solution.py:70
  11.1 7.6 %collective-permute-start = (bf16[16,32,128]{2,1,0:T(8,128)(2,1)}, bf16[16,32,128]{2,1,0:T(8,128)(2,1)S(1)}, u32[]{:S(2)}, u32[]{:S(2)}) collective-permute-start(bf16[16,32,128]{2,1,0:T(8,128)(2,1)} %param.6), channel_id=1, source_target_pairs={{0,64},{64,128},{128,192},{192,0},{1,65},{65,129},{129,193},{193,1... | collective-permute-start | bytes 393224 | tf_op jit(solution)/shard_map/ppermute | solution.py:70
  11.5 7.2 %collective-permute-start.2 = (bf16[16,32,128]{2,1,0:T(8,128)(2,1)}, bf16[16,32,128]{2,1,0:T(8,128)(2,1)S(1)}, u32[]{:S(2)}, u32[]{:S(2)}) collective-permute-start(bf16[16,32,128]{2,1,0:T(8,128)(2,1)} %param.6), channel_id=1, source_target_pairs={{0,192},{64,0},{128,64},{192,128},{1,193},{65,1},{129,65},{193,129... | collective-permute-start | bytes 393224 | tf_op jit(solution)/shard_map/ppermute | solution.py:70
  28.1 21.5 %all-to-all-start = ((s32[64,1,24]{2,1,0:T(1,128)}), s32[64,1,24]{2,1,0:T(1,128)S(1)}, u32[]{:S(2)}, u32[]{:S(2)}) async-start(s32[64,1,24]{2,1,0:T(1,128)} %bitcast.9), calls=%async_computation | async-start | bytes 65536 | tf_op jit(solution)/shard_map/all_to_all | solution.py:76
  117.0 36.4 %copy-start.2 = (s32[16,16]{1,0:T(8,128)S(1)}, s32[16,16]{1,0:T(8,128)}, u32[]{:S(2)}) copy-start(s32[16,16]{1,0:T(8,128)} %param.11) | copy-start | bytes 3076
  117.2 8.5 %collective-permute-start.4 = (f32[1792,32]{0,1:T(8,128)S(1)}, f32[1792,32]{0,1:T(8,128)S(1)}, u32[]{:S(2)}, u32[]{:S(2)}) collective-permute-start(f32[1792,32]{0,1:T(8,128)S(1)} %pad_maximum_fusion.1), channel_id=1, source_target_pairs={{0,2},{1,3},{2,0},{3,1},{4,6},{5,7},{6,4},{7,5},{8,10},{9,11},{10,... | collective-permute-start | bytes 688136 | tf_op jit(solution)/shard_map/ppermute | solution.py:107
  119.9 10.7 %collective-permute-start.5 = (f32[1792,32]{0,1:T(8,128)S(1)}, f32[1792,32]{0,1:T(8,128)S(1)}, u32[]{:S(2)}, u32[]{:S(2)}) collective-permute-start(f32[1792,32]{0,1:T(8,128)S(1)} %pad_maximum_fusion.1), channel_id=1, source_target_pairs={{0,3},{1,0},{2,1},{3,2},{4,7},{5,4},{6,5},{7,6},{8,11},{9,8},{10,9... | collective-permute-start | bytes 688136 | tf_op jit(solution)/shard_map/ppermute | solution.py:107
  120.8 10.3 %collective-permute-start.3 = (f32[1792,32]{0,1:T(8,128)S(1)}, f32[1792,32]{0,1:T(8,128)S(1)}, u32[]{:S(2)}, u32[]{:S(2)}) collective-permute-start(f32[1792,32]{0,1:T(8,128)S(1)} %pad_maximum_fusion.1), channel_id=1, source_target_pairs={{0,1},{1,2},{2,3},{3,0},{4,5},{5,6},{6,7},{7,4},{8,9},{9,10},{10,1... | collective-permute-start | bytes 688136 | tf_op jit(solution)/shard_map/ppermute | solution.py:107
  132.6 18.5 %all-to-all-start.1 = ((f32[64,1,524]{2,1,0:T(1,128)}), f32[64,1,524]{2,1,0:T(1,128)S(1)}, u32[]{:S(2)}, u32[]{:S(2)}) async-start(f32[64,1,524]{2,1,0:T(1,128)} %copy.77), calls=%async_computation.1 | async-start | bytes 327680 | tf_op jit(solution)/shard_map/all_to_all | solution.py:118
Sparse Core Ops, SparseCore 0:
  20.5 59.4 all-gather.1

commit v11 on v9

--- a/solution.py
+++ b/solution.py
@@ -75,17 +75,19 @@
     pair_scored = jnp.where(valid_tokens[:, None, :], pair_scored, masked_score)
     partial_value = jnp.max(pair_scored, axis=2)
 
-    merged = jnp.concatenate([local_best.reshape(-1, query_tokens), partial_value], axis=0)
     cent_total = lax.axis_size("cent")
-    arrived = [
-        lax.ppermute(merged, "cent", [(i, (i + shift) % cent_total) for i in range(cent_total)])
-        for shift in range(1, cent_total)
-    ]
-    for other in arrived:
-        merged = jnp.maximum(merged, other)
-    token_rows_out = shard_total * query_count
-    best_all = merged[:token_rows_out].reshape(shard_total, query_count * query_tokens)
-    complete = merged[token_rows_out:]
+
+    def cent_max(values):
+        arrived = [
+            lax.ppermute(values, "cent", [(i, (i + shift) % cent_total) for i in range(cent_total)])
+            for shift in range(1, cent_total)
+        ]
+        for other in arrived:
+            values = jnp.maximum(values, other)
+        return values
+
+    complete = cent_max(partial_value)
+    best_all = cent_max(local_best.reshape(shard_total, query_count * query_tokens))
     pair_scores = (jnp.sum(complete, axis=1) / query_tokens).reshape(shard_total, capacity)
 
     outgoing = jnp.concatenate([best_all, pair_scores], axis=1)

time: 159 us -> 157 us (0.987)
  waiting for transfers between devices: 53.6 us -> 47 us
  starting transfers between devices: 30.6 us -> 34.1 us
  other arithmetic: 3.89 us -> 7.06 us
  matrix products: 25.5 us -> 22.6 us
    ppermute x3 -> x6, waiting for transfers between devices: 9.68 us -> 6.03 us  [cent_max(): lax.ppermute(values, 'cent', [(i, (i + shift) % cent_total) for i in rang...]
    dot_general x1, matrix products: 17.2 us -> 13.7 us  [per_device(): jnp.einsum('rd,cd->rc', flattened, centroids, preferred_element_type=jnp....]
    ppermute x3 -> x6, starting transfers between devices: 4.25 us -> 7 us  [cent_max(): lax.ppermute(values, 'cent', [(i, (i + shift) % cent_total) for i in rang...]
  transfers between devices with their start and end apart: 9 -> 12, of which waited for: 7 -> 7; matrix products, arithmetic and copies ran while one was open for 12% -> 24% of each run, Pallas kernels for 0% -> 0%
where the time goes in v11:
time: 157 us
  waiting for transfers between devices  47 us (30%)
  starting transfers between devices  34.1 us (22%)
  local copies, waits for them, and re-layouts  31.5 us (20%)
  matrix products  22.6 us (14%)
  between operations  14.4 us (9%)
  other arithmetic  7.06 us (4%)
    all_gather x1, waiting for transfers between devices, per_device(): lax.all_gather(jnp.concatenate(along_y, axis=0), 'rest', axis=0, tiled=True)  18.6 us
    dot_general x1, matrix products, per_device(): jnp.einsum('rd,cd->rc', flattened, centroids, preferred_element_type=jnp....  13.7 us
    all_to_all x1, starting transfers between devices, per_device(): lax.all_to_all(table, shard, split_axis=0, concat_axis=0, tiled=True)  11.9 us
    all_to_all x1, waiting for transfers between devices, per_device(): lax.all_to_all(outgoing, shard, split_axis=0, concat_axis=0, tiled=True)  9.11 us
    dot_general x1, matrix products, per_device(): jnp.einsum('ntd,npd->ntp', asked, chosen, preferred_element_type=jnp.floa...  8.89 us
    all_to_all x1, starting transfers between devices, per_device(): lax.all_to_all(outgoing, shard, split_axis=0, concat_axis=0, tiled=True)  8.7 us
    all_to_all x1, waiting for transfers between devices, per_device(): lax.all_to_all(table, shard, split_axis=0, concat_axis=0, tiled=True)  8.44 us
    gather x1, local copies, waits for them, and re-layouts, per_device(): asked = jnp.take(query_block, query_table, axis=0)  8.29 us
  transfers between devices with their start and end apart: 12, of which 7 were waited for; matrix products, arithmetic and copies ran while one was open for 24% of the time, Pallas kernels for 0%

profile of v11, /device:TPU:1, one launch (start us, length us, event | category | flops | bytes accessed | tf_op | source)
XLA Modules:
  0.0 156.7 jit_solution(1981072478561170637)
XLA Ops:
  7.2 3.8 %collective-permute-start.1 = (bf16[16,32,128]{2,1,0:T(8,128)(2,1)}, bf16[16,32,128]{2,1,0:T(8,128)(2,1)S(1)}, u32[]{:S(2)}, u32[]{:S(2)}) collective-permute-start(bf16[16,32,128]{2,1,0:T(8,128)(2,1)} %param.6), channel_id=1, source_target_pairs={{0,128},{64,192},{128,0},{192,64},{1,129},{65,193},{129,1},{193,65... | collective-permute-start | bytes 393224 | tf_op jit(solution)/shard_map/ppermute | solution.py:44
  11.5 2.3 %collective-permute-start.2 = (bf16[16,32,128]{2,1,0:T(8,128)(2,1)}, bf16[16,32,128]{2,1,0:T(8,128)(2,1)S(1)}, u32[]{:S(2)}, u32[]{:S(2)}) collective-permute-start(bf16[16,32,128]{2,1,0:T(8,128)(2,1)} %param.6), channel_id=1, source_target_pairs={{0,192},{64,0},{128,64},{192,128},{1,193},{65,1},{129,65},{193,129... | collective-permute-start | bytes 393224 | tf_op jit(solution)/shard_map/ppermute | solution.py:44
  13.7 4.9 %collective-permute-done = bf16[16,32,128]{2,1,0:T(8,128)(2,1)S(1)} collective-permute-done((bf16[16,32,128]{2,1,0:T(8,128)(2,1)}, bf16[16,32,128]{2,1,0:T(8,128)(2,1)S(1)}, u32[]{:S(2)}, u32[]{:S(2)}) %collective-permute-start) | collective-permute-done | bytes 131104 | tf_op jit(solution)/shard_map/ppermute | solution.py:44
  18.6 1.8 %pad_maximum_fusion = bf16[64,32,128]{2,1,0:T(8,128)(2,1)} fusion(bf16[16,32,128]{2,1,0:T(8,128)(2,1)S(1)} %collective-permute-done.2, bf16[16,32,128]{2,1,0:T(8,128)(2,1)S(1)} %collective-permute-done.1, bf16[16,32,128]{2,1,0:T(8,128)(2,1)S(1)} %collective-permute-done, bf16[16,32,128]{2,1,0:T(8,128)(2,1)} %param.6), kind=kLoop, calls=%fused_computation.15 | loop fusion | flops 786432 | bytes 1048576 | tf_op jit(solution)/shard_map/concatenate | solution.py:48
  22.8 2.1 %gather_fusion.1 = s32[256]{0:T(256)S(1)} fusion(s32[16384]{0:T(1024)} %param.10, s32[1024]{0:T(1024)S(1)} %pad_clamp_fusion.3), kind=kCustom, calls=%fused_computation.1 | custom fusion | bytes 3072 | tf_op jit(solution)/shard_map/jit(_take)/gather | solution.py:24
  26.6 1.2 scatter_custom_fusion
  28.6 11.9 %all-to-all-start = ((s32[64,1,24]{2,1,0:T(1,128)}), s32[64,1,24]{2,1,0:T(1,128)S(1)}, u32[]{:S(2)}, u32[]{:S(2)}) async-start(s32[64,1,24]{2,1,0:T(1,128)} %bitcast.8), calls=%async_computation | async-start | bytes 65536 | tf_op jit(solution)/shard_map/all_to_all | solution.py:50
  41.6 8.4 %all-to-all-done = s32[64,1,24]{2,1,0:T(1,128)S(1)} async-done(((s32[64,1,24]{2,1,0:T(1,128)}), s32[64,1,24]{2,1,0:T(1,128)S(1)}, u32[]{:S(2)}, u32[]{:S(2)}) %all-to-all-start) | async-done | bytes 6176 | tf_op jit(solution)/shard_map/all_to_all | solution.py:50
  51.6 5.0 %gather_fusion.2 = s32[768]{0:T(1024)S(1)} fusion(s32[256]{0:T(256)S(1)} %copy-done.1, s32[1024]{0:T(1024)S(1)} %pad_clamp_fusion.2), kind=kCustom, calls=%fused_computation.2 | custom fusion | bytes 9216 | tf_op jit(solution)/shard_map/jit(_take)/gather | solution.py:74
  56.7 4.5 %gather_fusion.4 = bf16[768,32,128]{2,1,0:T(8,128)(2,1)} fusion(bf16[256,32,128]{2,1,0:T(8,128)(2,1)S(1)} %copy-done, s32[1024]{0:T(1024)S(1)} %pad_clamp_fusion.2), kind=kCustom, calls=%fused_computation.4 | custom fusion | bytes 12585984 | tf_op jit(solution)/shard_map/jit(_take)/gather | solution.py:71
  61.5 18.6 %all-gather.2.cloned.1.call-done = bf16[1024,32,128]{2,1,0:T(8,128)(2,1)} async-done(((bf16[64,32,128]{2,1,0:T(8,128)(2,1)}), bf16[1024,32,128]{2,1,0:T(8,128)(2,1)}) %all-gather.2.cloned.1.call-update) | async-done | bytes 8388624 | tf_op jit(solution)/shard_map/all_gather | solution.py:47
  80.1 8.3 %gather_fusion.3 = bf16[768,32,128]{2,1,0:T(8,128)(2,1)} fusion(bf16[1024,32,128]{2,1,0:T(8,128)(2,1)} %all-gather.2.cloned.1.call-done, s32[1024]{0:T(1024)S(1)} %pad_clamp_fusion.1), kind=kCustom, calls=%fused_computation.3 | custom fusion | bytes 12585984 | tf_op jit(solution)/shard_map/jit(_take)/gather | solution.py:70
  88.3 8.9 %select_reduce_fusion = f32[768,32]{1,0:T(8,128)S(1)} fusion(pred[768,32]{1,0:T(8,128)(4,1)S(1)} %broadcast_compare_fusion, bf16[768,32,128]{2,1,0:T(8,128)(2,1)} %gather_fusion.4, pred[768]{0:T(1024)(128)(4,1)S(1)} %le.102, bf16[768,32,128]{2,1,0:T(8,128)(2,1)} %gather_fusion.3, pred[768]{0:T(1024)(128)(4,1)S(1)} %compare_and_fusion), kind=kOutput, calls=%fused_computation.8 | convolution fusion | flops 209166336 | bytes 12707328 | tf_op jit(solution)/shard_map/ntd,npd->ntp/dot_general | solution.py:72
  97.2 2.5 %collective-permute-start.8 = (f32[768,32]{1,0:T(8,128)S(1)}, f32[768,32]{1,0:T(8,128)}, u32[]{:S(2)}, u32[]{:S(2)}) collective-permute-start(f32[768,32]{1,0:T(8,128)S(1)} %select_reduce_fusion), channel_id=1, source_target_pairs={{0,3},{1,0},{2,1},{3,2},{4,7},{5,4},{6,5},{7,6},{8,11},{9,8},{10,9... | collective-permute-start | bytes 294920 | tf_op jit(solution)/shard_map/ppermute | solution.py:82
  100.9 13.7 %convolution_reduce_fusion = f32[32768]{0:T(1024)S(1)} fusion(bf16[32768,128]{1,0:T(8,128)(2,1)S(1)} %bitcast.56, bf16[768,128]{1,0:T(8,128)(2,1)S(1)} %copy-done.7), kind=kOutput, calls=%fused_computation.7 | convolution fusion | flops 6467584000 | bytes 8716288 | tf_op jit(solution)/shard_map/rd,cd->rc/dot_general | solution.py:55
  115.8 2.2 %collective-permute-start.5 = (f32[64,512]{1,0:T(8,128)S(1)}, f32[64,512]{1,0:T(8,128)S(1)}, u32[]{:S(2)}, u32[]{:S(2)}) collective-permute-start(f32[64,512]{1,0:T(8,128)S(1)} %reshape_reshape.3), channel_id=1, source_target_pairs={{0,3},{1,0},{2,1},{3,2},{4,7},{5,4},{6,5},{7,6},{8,11},{9,8},{10,9... | collective-permute-start | bytes 393224 | tf_op jit(solution)/shard_map/ppermute | solution.py:82
  118.0 1.2 collective-permute-start.4
  119.2 1.6 %collective-permute-done.6 = f32[768,32]{1,0:T(8,128)} collective-permute-done((f32[768,32]{1,0:T(8,128)S(1)}, f32[768,32]{1,0:T(8,128)}, u32[]{:S(2)}, u32[]{:S(2)}) %collective-permute-start.6) | collective-permute-done | bytes 98336 | tf_op jit(solution)/shard_map/ppermute | solution.py:82
  120.8 1.4 maximum_reduce_fusion
  122.4 1.0 collective-permute-done.4
  123.4 3.4 %collective-permute-done.3 = f32[64,512]{1,0:T(8,128)S(1)} collective-permute-done((f32[64,512]{1,0:T(8,128)S(1)}, f32[64,512]{1,0:T(8,128)S(1)}, u32[]{:S(2)}, u32[]{:S(2)}) %collective-permute-start.3) | collective-permute-done | bytes 131104 | tf_op jit(solution)/shard_map/ppermute | solution.py:82
  127.6 8.7 %all-to-all-start.1 = ((f32[64,1,524]{2,1,0:T(1,128)}), f32[64,1,524]{2,1,0:T(1,128)S(1)}, u32[]{:S(2)}, u32[]{:S(2)}) async-start(f32[64,1,524]{2,1,0:T(1,128)} %all_to_all.16), calls=%async_computation.1 | async-start | bytes 327680 | tf_op jit(solution)/shard_map/all_to_all | solution.py:94
  137.8 9.1 %all-to-all-done.1 = f32[64,1,524]{2,1,0:T(1,128)S(1)} async-done(((f32[64,1,524]{2,1,0:T(1,128)}), f32[64,1,524]{2,1,0:T(1,128)S(1)}, u32[]{:S(2)}, u32[]{:S(2)}) %all-to-all-start.1) | async-done | bytes 134176 | tf_op jit(solution)/shard_map/all_to_all | solution.py:94
  147.8 1.4 gather_fusion.5
  (90 shorter events, 14.5 us)
Async XLA Ops:
  7.2 49.5 %copy-start = (bf16[256,32,128]{2,1,0:T(8,128)(2,1)S(1)}, bf16[256,32,128]{2,1,0:T(8,128)(2,1)}, u32[]{:S(2)}) copy-start(bf16[256,32,128]{2,1,0:T(8,128)(2,1)} %param.8) | copy-start | bytes 6291460
  7.2 44.5 %copy-start.1 = (s32[256]{0:T(256)S(1)}, s32[256]{0:T(256)}, u32[]{:S(2)}) copy-start(s32[256]{0:T(256)} %param.9) | copy-start | bytes 3076
  7.2 72.9 %all-gather.2.cloned.1.call-start = ((), (), s32[]{:S(2)}) async-start(), calls=%async_computation.2 | async-start | bytes 8912896 | tf_op jit(solution)/shard_map/all_gather | solution.py:47
  7.2 6.5 %collective-permute-start.1 = (bf16[16,32,128]{2,1,0:T(8,128)(2,1)}, bf16[16,32,128]{2,1,0:T(8,128)(2,1)S(1)}, u32[]{:S(2)}, u32[]{:S(2)}) collective-permute-start(bf16[16,32,128]{2,1,0:T(8,128)(2,1)} %param.6), channel_id=1, source_target_pairs={{0,128},{64,192},{128,0},{192,64},{1,129},{65,193},{129,1},{193,65... | collective-permute-start | bytes 393224 | tf_op jit(solution)/shard_map/ppermute | solution.py:44
  11.1 7.6 %collective-permute-start = (bf16[16,32,128]{2,1,0:T(8,128)(2,1)}, bf16[16,32,128]{2,1,0:T(8,128)(2,1)S(1)}, u32[]{:S(2)}, u32[]{:S(2)}) collective-permute-start(bf16[16,32,128]{2,1,0:T(8,128)(2,1)} %param.6), channel_id=1, source_target_pairs={{0,64},{64,128},{128,192},{192,0},{1,65},{65,129},{129,193},{193,1... | collective-permute-start | bytes 393224 | tf_op jit(solution)/shard_map/ppermute | solution.py:44
  11.5 7.2 %collective-permute-start.2 = (bf16[16,32,128]{2,1,0:T(8,128)(2,1)}, bf16[16,32,128]{2,1,0:T(8,128)(2,1)S(1)}, u32[]{:S(2)}, u32[]{:S(2)}) collective-permute-start(bf16[16,32,128]{2,1,0:T(8,128)(2,1)} %param.6), channel_id=1, source_target_pairs={{0,192},{64,0},{128,64},{192,128},{1,193},{65,1},{129,65},{193,129... | collective-permute-start | bytes 393224 | tf_op jit(solution)/shard_map/ppermute | solution.py:44
  26.0 0.5 copy-start.4
  26.6 34.6 %copy-start.5 = (s32[256,1]{0,1:T(1,128)}, s32[256,1]{0,1:T(1,128)S(1)}, u32[]{:S(2)}) copy-start(s32[256,1]{0,1:T(1,128)S(1)} %compare_select_fusion.9) | copy-start | bytes 3076
  28.6 21.5 %all-to-all-start = ((s32[64,1,24]{2,1,0:T(1,128)}), s32[64,1,24]{2,1,0:T(1,128)S(1)}, u32[]{:S(2)}, u32[]{:S(2)}) async-start(s32[64,1,24]{2,1,0:T(1,128)} %bitcast.8), calls=%async_computation | async-start | bytes 65536 | tf_op jit(solution)/shard_map/all_to_all | solution.py:50
  88.3 12.5 %copy-start.2 = (bf16[1024,32,128]{2,1,0:T(8,128)(2,1)S(1)}, bf16[1024,32,128]{2,1,0:T(8,128)(2,1)}, u32[]{:S(2)}) copy-start(bf16[1024,32,128]{2,1,0:T(8,128)(2,1)} %all-gather.2.cloned.1.call-done) | copy-start | bytes 25165828
  88.3 12.5 %copy-start.7 = (bf16[768,128]{1,0:T(8,128)(2,1)S(1)}, bf16[768,128]{1,0:T(8,128)(2,1)}, u32[]{:S(2)}) copy-start(bf16[768,128]{1,0:T(8,128)(2,1)} %param.7) | copy-start | bytes 589828
  97.2 21.9 %collective-permute-start.8 = (f32[768,32]{1,0:T(8,128)S(1)}, f32[768,32]{1,0:T(8,128)}, u32[]{:S(2)}, u32[]{:S(2)}) collective-permute-start(f32[768,32]{1,0:T(8,128)S(1)} %select_reduce_fusion), channel_id=1, source_target_pairs={{0,3},{1,0},{2,1},{3,2},{4,7},{5,4},{6,5},{7,6},{8,11},{9,8},{10,9... | collective-permute-start | bytes 294920 | tf_op jit(solution)/shard_map/ppermute | solution.py:82
  99.7 19.5 %collective-permute-start.7 = (f32[768,32]{1,0:T(8,128)S(1)}, f32[768,32]{1,0:T(8,128)}, u32[]{:S(2)}, u32[]{:S(2)}) collective-permute-start(f32[768,32]{1,0:T(8,128)S(1)} %select_reduce_fusion), channel_id=1, source_target_pairs={{0,2},{1,3},{2,0},{3,1},{4,6},{5,7},{6,4},{7,5},{8,10},{9,11},{10,... | collective-permute-start | bytes 294920 | tf_op jit(solution)/shard_map/ppermute | solution.py:82
  100.3 20.5 %collective-permute-start.6 = (f32[768,32]{1,0:T(8,128)S(1)}, f32[768,32]{1,0:T(8,128)}, u32[]{:S(2)}, u32[]{:S(2)}) collective-permute-start(f32[768,32]{1,0:T(8,128)S(1)} %select_reduce_fusion), channel_id=1, source_target_pairs={{0,1},{1,2},{2,3},{3,0},{4,5},{5,6},{6,7},{7,4},{8,9},{9,10},{10,1... | collective-permute-start | bytes 294920 | tf_op jit(solution)/shard_map/ppermute | solution.py:82
  100.9 14.6 %copy-start.6 = (pred[4]{0:T(512)(128)(4,1)S(1)}, pred[4]{0:T(512)(128)(4,1)}, u32[]{:S(2)}) copy-start(pred[4]{0:T(512)(128)(4,1)} %compare_and_fusion.1) | copy-start | bytes 16
  114.6 34.6 %copy-start.3 = (s32[16,16]{1,0:T(8,128)S(1)}, s32[16,16]{1,0:T(8,128)}, u32[]{:S(2)}) copy-start(s32[16,16]{1,0:T(8,128)} %param.11) | copy-start | bytes 3076
  115.8 6.5 %collective-permute-start.5 = (f32[64,512]{1,0:T(8,128)S(1)}, f32[64,512]{1,0:T(8,128)S(1)}, u32[]{:S(2)}, u32[]{:S(2)}) collective-permute-start(f32[64,512]{1,0:T(8,128)S(1)} %reshape_reshape.3), channel_id=1, source_target_pairs={{0,3},{1,0},{2,1},{3,2},{4,7},{5,4},{6,5},{7,6},{8,11},{9,8},{10,9... | collective-permute-start | bytes 393224 | tf_op jit(solution)/shard_map/ppermute | solution.py:82
  118.0 5.4 %collective-permute-start.4 = (f32[64,512]{1,0:T(8,128)S(1)}, f32[64,512]{1,0:T(8,128)S(1)}, u32[]{:S(2)}, u32[]{:S(2)}) collective-permute-start(f32[64,512]{1,0:T(8,128)S(1)} %reshape_reshape.3), channel_id=1, source_target_pairs={{0,2},{1,3},{2,0},{3,1},{4,6},{5,7},{6,4},{7,5},{8,10},{9,11},{10,... | collective-permute-start | bytes 393224 | tf_op jit(solution)/shard_map/ppermute | solution.py:82
  119.2 7.6 %collective-permute-start.3 = (f32[64,512]{1,0:T(8,128)S(1)}, f32[64,512]{1,0:T(8,128)S(1)}, u32[]{:S(2)}, u32[]{:S(2)}) collective-permute-start(f32[64,512]{1,0:T(8,128)S(1)} %reshape_reshape.3), channel_id=1, source_target_pairs={{0,1},{1,2},{2,3},{3,0},{4,5},{5,6},{6,7},{7,4},{8,9},{9,10},{10,1... | collective-permute-start | bytes 393224 | tf_op jit(solution)/shard_map/ppermute | solution.py:82
  127.6 19.3 %all-to-all-start.1 = ((f32[64,1,524]{2,1,0:T(1,128)}), f32[64,1,524]{2,1,0:T(1,128)S(1)}, u32[]{:S(2)}, u32[]{:S(2)}) async-start(f32[64,1,524]{2,1,0:T(1,128)} %all_to_all.16), calls=%async_computation.1 | async-start | bytes 327680 | tf_op jit(solution)/shard_map/all_to_all | solution.py:94
Sparse Core Ops, SparseCore 0:
  20.5 59.4 all-gather.1

commit v12 on v11

--- a/solution.py
+++ b/solution.py
@@ -51,15 +51,27 @@
         shard_total, capacity, 2
     )
 
-    flattened = query_block.reshape(-1, feature_width)
-    scored = jnp.einsum("rd,cd->rc", flattened, centroids, preferred_element_type=jnp.float32)
-    by_shift = jnp.max(scored, axis=1).reshape(rest_total, y_total, query_count, query_tokens)
+    cent_total = lax.axis_size("cent")
+
+    def cent_max(values):
+        arrived = [
+            lax.ppermute(values, "cent", [(i, (i + shift) % cent_total) for i in range(cent_total)])
+            for shift in range(1, cent_total)
+        ]
+        for other in arrived:
+            values = jnp.maximum(values, other)
+        return values
+
     shift_of_y = (my_y - jnp.arange(y_total, dtype=jnp.int32)) % y_total
-    local_best = (
-        jnp.take(by_shift, shift_of_y, axis=1)
-        .transpose(1, 0, 2, 3)
-        .reshape(shard_total, query_count, query_tokens)
-    )
+    halves = 2 if rest_total % 2 == 0 else 1
+    rest_part = rest_total // halves
+    rows_per = rest_part * y_total * query_count
+    best_parts = []
+    for half in range(halves):
+        block = query_block[half * rows_per:(half + 1) * rows_per].reshape(-1, feature_width)
+        scored = jnp.einsum("rd,cd->rc", block, centroids, preferred_element_type=jnp.float32)
+        by_shift = jnp.max(scored, axis=1).reshape(rest_part, y_total, query_count * query_tokens)
+        best_parts.append(cent_max(jnp.take(by_shift, shift_of_y, axis=1).transpose(1, 0, 2)))
 
     slot_table = jnp.maximum(mine[..., 0], 0).reshape(-1)
     global_query = jnp.maximum(mine[..., 1], 0).reshape(-1)
@@ -75,19 +87,8 @@
     pair_scored = jnp.where(valid_tokens[:, None, :], pair_scored, masked_score)
     partial_value = jnp.max(pair_scored, axis=2)
 
-    cent_total = lax.axis_size("cent")
-
-    def cent_max(values):
-        arrived = [
-            lax.ppermute(values, "cent", [(i, (i + shift) % cent_total) for i in range(cent_total)])
-            for shift in range(1, cent_total)
-        ]
-        for other in arrived:
-            values = jnp.maximum(values, other)
-        return values
-
     complete = cent_max(partial_value)
-    best_all = cent_max(local_best.reshape(shard_total, query_count * query_tokens))
+    best_all = jnp.concatenate(best_parts, axis=1).reshape(shard_total, query_count * query_tokens)
     pair_scores = (jnp.sum(complete, axis=1) / query_tokens).reshape(shard_total, capacity)
 
     outgoing = jnp.concatenate([best_all, pair_scores], axis=1)

time: 157 us -> 178 us (1.13)
  waiting for transfers between devices: 47 us -> 60.9 us
  local copies, waits for them, and re-layouts: 31.5 us -> 36 us
  starting transfers between devices: 34.1 us -> 37.8 us
  other arithmetic: 7.06 us -> 4.02 us
    ppermute x6 -> x9, waiting for transfers between devices: 6.03 us -> 17 us  [cent_max(): lax.ppermute(values, 'cent', [(i, (i + shift) % cent_total) for i in rang...]
    slice x1 -> x2, local copies, waits for them, and re-layouts: 0.18 us -> 5.72 us  [the longest x1 5.54 us: per_device(): query_block[half * rows_per:(half + 1) * rows_per]]
    ppermute x6 -> x9, starting transfers between devices: 7 us -> 11.5 us  [cent_max(): lax.ppermute(values, 'cent', [(i, (i + shift) % cent_total) for i in rang...]
    dot_general x1 -> x2, matrix products: 13.7 us -> 16.1 us  [per_device(): jnp.einsum('rd,cd->rc', block, centroids, preferred_element_type=jnp.floa...]
  transfers between devices with their start and end apart: 12 -> 15, of which waited for: 7 -> 8; matrix products, arithmetic and copies ran while one was open for 24% -> 20% of each run, Pallas kernels for 0% -> 0%
where the time goes in v12:
time: 178 us; the launch traced here: 177 us
  waiting for transfers between devices  60.9 us (34%)
  starting transfers between devices  37.8 us (21%)
  local copies, waits for them, and re-layouts  36 us (20%)
  matrix products  24.3 us (14%)
  between operations  14.4 us (8%)
  other arithmetic  4.02 us (2%)
    all_gather x1, waiting for transfers between devices, per_device(): lax.all_gather(jnp.concatenate(along_y, axis=0), 'rest', axis=0, tiled=True)  19.1 us
    ppermute x9, waiting for transfers between devices, cent_max(): lax.ppermute(values, 'cent', [(i, (i + shift) % cent_total) for i in rang...  17 us
    dot_general x2, matrix products, per_device(): jnp.einsum('rd,cd->rc', block, centroids, preferred_element_type=jnp.floa...  16.1 us
    all_to_all x1, starting transfers between devices, per_device(): lax.all_to_all(table, shard, split_axis=0, concat_axis=0, tiled=True)  12.6 us
    ppermute x9, starting transfers between devices, cent_max(): lax.ppermute(values, 'cent', [(i, (i + shift) % cent_total) for i in rang...  11.5 us
    all_to_all x1, waiting for transfers between devices, per_device(): lax.all_to_all(outgoing, shard, split_axis=0, concat_axis=0, tiled=True)  10.4 us
    all_to_all x1, waiting for transfers between devices, per_device(): lax.all_to_all(table, shard, split_axis=0, concat_axis=0, tiled=True)  9.52 us
    gather x1, local copies, waits for them, and re-layouts, per_device(): asked = jnp.take(query_block, query_table, axis=0)  8.29 us
  transfers between devices with their start and end apart: 15, of which 8 were waited for; matrix products, arithmetic and copies ran while one was open for 20% of the time, Pallas kernels for 0%

profile of v12, /device:TPU:1, one launch (start us, length us, event | category | flops | bytes accessed | tf_op | source)
XLA Modules:
  0.0 177.5 jit_solution(9649304212564580102)
XLA Ops:
  7.2 2.2 %collective-permute-start = (bf16[16,32,128]{2,1,0:T(8,128)(2,1)}, bf16[16,32,128]{2,1,0:T(8,128)(2,1)S(1)}, u32[]{:S(2)}, u32[]{:S(2)}) collective-permute-start(bf16[16,32,128]{2,1,0:T(8,128)(2,1)} %param.8), channel_id=1, source_target_pairs={{0,64},{64,128},{128,192},{192,0},{1,65},{65,129},{129,193},{193,1... | collective-permute-start | bytes 393224 | tf_op jit(solution)/shard_map/ppermute | solution.py:44
  9.4 2.6 %collective-permute-start.1 = (bf16[16,32,128]{2,1,0:T(8,128)(2,1)}, bf16[16,32,128]{2,1,0:T(8,128)(2,1)S(1)}, u32[]{:S(2)}, u32[]{:S(2)}) collective-permute-start(bf16[16,32,128]{2,1,0:T(8,128)(2,1)} %param.8), channel_id=1, source_target_pairs={{0,128},{64,192},{128,0},{192,64},{1,129},{65,193},{129,1},{193,65... | collective-permute-start | bytes 393224 | tf_op jit(solution)/shard_map/ppermute | solution.py:44
  13.4 4.5 %collective-permute-done.1 = bf16[16,32,128]{2,1,0:T(8,128)(2,1)S(1)} collective-permute-done((bf16[16,32,128]{2,1,0:T(8,128)(2,1)}, bf16[16,32,128]{2,1,0:T(8,128)(2,1)S(1)}, u32[]{:S(2)}, u32[]{:S(2)}) %collective-permute-start.1) | collective-permute-done | bytes 131104 | tf_op jit(solution)/shard_map/ppermute | solution.py:44
  18.0 1.8 %pad_maximum_fusion = bf16[64,32,128]{2,1,0:T(8,128)(2,1)} fusion(bf16[16,32,128]{2,1,0:T(8,128)(2,1)S(1)} %collective-permute-done.2, bf16[16,32,128]{2,1,0:T(8,128)(2,1)S(1)} %collective-permute-done.1, bf16[16,32,128]{2,1,0:T(8,128)(2,1)S(1)} %collective-permute-done, bf16[16,32,128]{2,1,0:T(8,128)(2,1)} %param.8), kind=kLoop, calls=%fused_computation.17 | loop fusion | flops 786432 | bytes 1048576 | tf_op jit(solution)/shard_map/concatenate | solution.py:48
  22.2 2.1 %gather_fusion = s32[256]{0:T(256)S(1)} fusion(s32[16384]{0:T(1024)} %param.12, s32[1024]{0:T(1024)S(1)} %pad_clamp_fusion.3), kind=kCustom, calls=%fused_computation.2 | custom fusion | bytes 3072 | tf_op jit(solution)/shard_map/jit(_take)/gather | solution.py:24
  27.4 12.6 %all-to-all-start = ((s32[64,1,24]{2,1,0:T(1,128)}), s32[64,1,24]{2,1,0:T(1,128)S(1)}, u32[]{:S(2)}, u32[]{:S(2)}) async-start(s32[64,1,24]{2,1,0:T(1,128)} %bitcast.15), calls=%async_computation | async-start | bytes 65536 | tf_op jit(solution)/shard_map/all_to_all | solution.py:50
  40.1 9.5 %all-to-all-done = s32[64,1,24]{2,1,0:T(1,128)S(1)} async-done(((s32[64,1,24]{2,1,0:T(1,128)}), s32[64,1,24]{2,1,0:T(1,128)S(1)}, u32[]{:S(2)}, u32[]{:S(2)}) %all-to-all-start) | async-done | bytes 6176 | tf_op jit(solution)/shard_map/all_to_all | solution.py:50
  51.2 5.0 %gather_fusion.1 = s32[768]{0:T(1024)S(1)} fusion(s32[256]{0:T(256)S(1)} %copy-done.1, s32[1024]{0:T(1024)S(1)} %pad_clamp_fusion.2), kind=kCustom, calls=%fused_computation.3 | custom fusion | bytes 9216 | tf_op jit(solution)/shard_map/jit(_take)/gather | solution.py:86
  56.2 4.5 %gather_fusion.3 = bf16[768,32,128]{2,1,0:T(8,128)(2,1)} fusion(bf16[256,32,128]{2,1,0:T(8,128)(2,1)S(1)} %copy-done, s32[1024]{0:T(1024)S(1)} %pad_clamp_fusion.2), kind=kCustom, calls=%fused_computation.5 | custom fusion | bytes 12585984 | tf_op jit(solution)/shard_map/jit(_take)/gather | solution.py:83
  61.0 19.1 %all-gather.2.cloned.1.call-done = bf16[1024,32,128]{2,1,0:T(8,128)(2,1)} async-done(((bf16[64,32,128]{2,1,0:T(8,128)(2,1)}), bf16[1024,32,128]{2,1,0:T(8,128)(2,1)}) %all-gather.2.cloned.1.call-update) | async-done | bytes 8388624 | tf_op jit(solution)/shard_map/all_gather | solution.py:47
  80.1 5.5 %fusion.36 = (bf16[512,32,128]{2,1,0:T(8,128)(2,1)S(1)}, bf16[512,32,128]{2,1,0:T(8,128)(2,1)}) fusion(bf16[1024,32,128]{2,1,0:T(8,128)(2,1)} %all-gather.2.cloned.1.call-done), kind=kLoop, calls=%fused_computation.135 | loop fusion | bytes 16777216 | tf_op jit(solution)/shard_map/slice | solution.py:71
  85.6 6.9 %convolution_reduce_fusion.1 = f32[16384]{0:T(1024)S(1)} fusion(bf16[16384,128]{1,0:T(8,128)(2,1)S(1)} %bitcast.62, bf16[768,128]{1,0:T(8,128)(2,1)S(1)} %copy-done.3), kind=kOutput, calls=%fused_computation.10 | convolution fusion | flops 3233792000 | bytes 4456448 | tf_op jit(solution)/shard_map/rd,cd->rc/dot_general | solution.py:72
  92.7 9.1 %convolution_reduce_fusion = f32[16384]{0:T(1024)S(1)} fusion(bf16[16384,128]{1,0:T(8,128)(2,1)} %bitcast.61, bf16[768,128]{1,0:T(8,128)(2,1)S(1)} %copy-done.3), kind=kOutput, calls=%fused_computation.9 | convolution fusion | flops 3233792000 | bytes 4456448 | tf_op jit(solution)/shard_map/rd,cd->rc/dot_general | solution.py:72
  104.3 2.4 %collective-permute-start.4 = (f32[4,8,512]{2,1,0:T(8,128)S(1)}, f32[4,8,512]{2,1,0:T(8,128)S(1)}, u32[]{:S(2)}, u32[]{:S(2)}) collective-permute-start(f32[4,8,512]{2,1,0:T(8,128)S(1)} %get-tuple-element.12), channel_id=1, source_target_pairs={{0,2},{1,3},{2,0},{3,1},{4,6},{5,7},{6,4},{7,5},{8,10},{9,11},{10,... | collective-permute-start | bytes 196616 | tf_op jit(solution)/shard_map/ppermute | solution.py:58
  109.1 8.3 %gather_fusion.2 = bf16[768,32,128]{2,1,0:T(8,128)(2,1)} fusion(bf16[1024,32,128]{2,1,0:T(8,128)(2,1)} %all-gather.2.cloned.1.call-done, s32[1024]{0:T(1024)S(1)} %pad_clamp_fusion.1), kind=kCustom, calls=%fused_computation.4 | custom fusion | bytes 12585984 | tf_op jit(solution)/shard_map/jit(_take)/gather | solution.py:82
  117.4 8.3 %select_reduce_fusion = f32[768,32]{1,0:T(8,128)S(1)} fusion(pred[768,32]{1,0:T(8,128)(4,1)S(1)} %broadcast_compare_fusion, bf16[768,32,128]{2,1,0:T(8,128)(2,1)} %gather_fusion.3, pred[768]{0:T(1024)(128)(4,1)S(1)} %le.98, bf16[768,32,128]{2,1,0:T(8,128)(2,1)} %gather_fusion.2, pred[768]{0:T(1024)(128)(4,1)S(1)} %compare_and_fusion), kind=kOutput, calls=%fused_computation.8 | convolution fusion | flops 209166336 | bytes 12707328 | tf_op jit(solution)/shard_map/ntd,npd->ntp/dot_general | solution.py:84
  125.7 1.6 collective-permute-start.8
  127.3 2.4 %collective-permute-start.10 = (f32[768,32]{1,0:T(8,128)S(1)}, f32[768,32]{1,0:T(8,128)S(1)}, u32[]{:S(2)}, u32[]{:S(2)}) collective-permute-start(f32[768,32]{1,0:T(8,128)S(1)} %select_reduce_fusion), channel_id=1, source_target_pairs={{0,2},{1,3},{2,0},{3,1},{4,6},{5,7},{6,4},{7,5},{8,10},{9,11},{10,... | collective-permute-start | bytes 294920 | tf_op jit(solution)/shard_map/ppermute | solution.py:58
  131.3 6.6 %collective-permute-done.10 = f32[768,32]{1,0:T(8,128)S(1)} collective-permute-done((f32[768,32]{1,0:T(8,128)S(1)}, f32[768,32]{1,0:T(8,128)S(1)}, u32[]{:S(2)}, u32[]{:S(2)}) %collective-permute-start.10) | collective-permute-done | bytes 98336 | tf_op jit(solution)/shard_map/ppermute | solution.py:58
  137.8 8.4 %collective-permute-done.11 = f32[768,32]{1,0:T(8,128)S(1)} collective-permute-done((f32[768,32]{1,0:T(8,128)S(1)}, f32[768,32]{1,0:T(8,128)S(1)}, u32[]{:S(2)}, u32[]{:S(2)}) %collective-permute-start.11) | collective-permute-done | bytes 98336 | tf_op jit(solution)/shard_map/ppermute | solution.py:58
  146.2 2.0 %collective-permute-done.9 = f32[768,32]{1,0:T(8,128)S(1)} collective-permute-done((f32[768,32]{1,0:T(8,128)S(1)}, f32[768,32]{1,0:T(8,128)S(1)}, u32[]{:S(2)}, u32[]{:S(2)}) %collective-permute-start.9) | collective-permute-done | bytes 98336 | tf_op jit(solution)/shard_map/ppermute | solution.py:58
  149.3 7.8 %all-to-all-start.1 = ((f32[64,1,524]{2,1,0:T(1,128)}), f32[64,1,524]{2,1,0:T(1,128)S(1)}, u32[]{:S(2)}, u32[]{:S(2)}) async-start(f32[64,1,524]{2,1,0:T(1,128)} %all_to_all.16), calls=%async_computation.1 | async-start | bytes 327680 | tf_op jit(solution)/shard_map/all_to_all | solution.py:95
  157.3 10.4 %all-to-all-done.1 = f32[64,1,524]{2,1,0:T(1,128)S(1)} async-done(((f32[64,1,524]{2,1,0:T(1,128)}), f32[64,1,524]{2,1,0:T(1,128)S(1)}, u32[]{:S(2)}, u32[]{:S(2)}) %all-to-all-start.1) | async-done | bytes 134176 | tf_op jit(solution)/shard_map/all_to_all | solution.py:95
  167.9 1.4 gather_fusion.4
  (95 shorter events, 18.1 us)
Async XLA Ops:
  7.2 49.0 %copy-start = (bf16[256,32,128]{2,1,0:T(8,128)(2,1)S(1)}, bf16[256,32,128]{2,1,0:T(8,128)(2,1)}, u32[]{:S(2)}) copy-start(bf16[256,32,128]{2,1,0:T(8,128)(2,1)} %param.10) | copy-start | bytes 6291460
  7.2 44.0 %copy-start.1 = (s32[256]{0:T(256)S(1)}, s32[256]{0:T(256)}, u32[]{:S(2)}) copy-start(s32[256]{0:T(256)} %param.11) | copy-start | bytes 3076
  7.2 72.9 %all-gather.2.cloned.1.call-start = ((), (), s32[]{:S(2)}) async-start(), calls=%async_computation.2 | async-start | bytes 8912896 | tf_op jit(solution)/shard_map/all_gather | solution.py:47
  7.2 6.2 %collective-permute-start = (bf16[16,32,128]{2,1,0:T(8,128)(2,1)}, bf16[16,32,128]{2,1,0:T(8,128)(2,1)S(1)}, u32[]{:S(2)}, u32[]{:S(2)}) collective-permute-start(bf16[16,32,128]{2,1,0:T(8,128)(2,1)} %param.8), channel_id=1, source_target_pairs={{0,64},{64,128},{128,192},{192,0},{1,65},{65,129},{129,193},{193,1... | collective-permute-start | bytes 393224 | tf_op jit(solution)/shard_map/ppermute | solution.py:44
  9.4 8.6 %collective-permute-start.1 = (bf16[16,32,128]{2,1,0:T(8,128)(2,1)}, bf16[16,32,128]{2,1,0:T(8,128)(2,1)S(1)}, u32[]{:S(2)}, u32[]{:S(2)}) collective-permute-start(bf16[16,32,128]{2,1,0:T(8,128)(2,1)} %param.8), channel_id=1, source_target_pairs={{0,128},{64,192},{128,0},{192,64},{1,129},{65,193},{129,1},{193,65... | collective-permute-start | bytes 393224 | tf_op jit(solution)/shard_map/ppermute | solution.py:44
  12.0 5.9 %collective-permute-start.2 = (bf16[16,32,128]{2,1,0:T(8,128)(2,1)}, bf16[16,32,128]{2,1,0:T(8,128)(2,1)S(1)}, u32[]{:S(2)}, u32[]{:S(2)}) collective-permute-start(bf16[16,32,128]{2,1,0:T(8,128)(2,1)} %param.8), channel_id=1, source_target_pairs={{0,192},{64,0},{128,64},{192,128},{1,193},{65,1},{129,65},{193,129... | collective-permute-start | bytes 393224 | tf_op jit(solution)/shard_map/ppermute | solution.py:44
  27.4 22.2 %all-to-all-start = ((s32[64,1,24]{2,1,0:T(1,128)}), s32[64,1,24]{2,1,0:T(1,128)S(1)}, u32[]{:S(2)}, u32[]{:S(2)}) async-start(s32[64,1,24]{2,1,0:T(1,128)} %bitcast.15), calls=%async_computation | async-start | bytes 65536 | tf_op jit(solution)/shard_map/all_to_all | solution.py:50
  61.0 24.6 %copy-start.3 = (bf16[768,128]{1,0:T(8,128)(2,1)S(1)}, bf16[768,128]{1,0:T(8,128)(2,1)}, u32[]{:S(2)}) copy-start(bf16[768,128]{1,0:T(8,128)(2,1)} %param.9) | copy-start | bytes 589828
  103.1 22.6 %collective-permute-start.3 = (f32[4,8,512]{2,1,0:T(8,128)S(1)}, f32[4,8,512]{2,1,0:T(8,128)S(1)}, u32[]{:S(2)}, u32[]{:S(2)}) collective-permute-start(f32[4,8,512]{2,1,0:T(8,128)S(1)} %get-tuple-element.12), channel_id=1, source_target_pairs={{0,1},{1,2},{2,3},{3,0},{4,5},{5,6},{6,7},{7,4},{8,9},{9,10},{10,1... | collective-permute-start | bytes 196616 | tf_op jit(solution)/shard_map/ppermute | solution.py:58
  104.3 22.9 %collective-permute-start.4 = (f32[4,8,512]{2,1,0:T(8,128)S(1)}, f32[4,8,512]{2,1,0:T(8,128)S(1)}, u32[]{:S(2)}, u32[]{:S(2)}) collective-permute-start(f32[4,8,512]{2,1,0:T(8,128)S(1)} %get-tuple-element.12), channel_id=1, source_target_pairs={{0,2},{1,3},{2,0},{3,1},{4,6},{5,7},{6,4},{7,5},{8,10},{9,11},{10,... | collective-permute-start | bytes 196616 | tf_op jit(solution)/shard_map/ppermute | solution.py:58
  106.7 22.9 %collective-permute-start.5 = (f32[4,8,512]{2,1,0:T(8,128)S(1)}, f32[4,8,512]{2,1,0:T(8,128)S(1)}, u32[]{:S(2)}, u32[]{:S(2)}) collective-permute-start(f32[4,8,512]{2,1,0:T(8,128)S(1)} %get-tuple-element.12), channel_id=1, source_target_pairs={{0,3},{1,0},{2,1},{3,2},{4,7},{5,4},{6,5},{7,6},{8,11},{9,8},{10,9... | collective-permute-start | bytes 196616 | tf_op jit(solution)/shard_map/ppermute | solution.py:58
  107.9 22.5 %collective-permute-start.6 = (f32[4,8,512]{2,1,0:T(8,128)S(1)}, f32[4,8,512]{2,1,0:T(8,128)S(1)}, u32[]{:S(2)}, u32[]{:S(2)}) collective-permute-start(f32[4,8,512]{2,1,0:T(8,128)S(1)} %get-tuple-element.13), channel_id=1, source_target_pairs={{0,1},{1,2},{2,3},{3,0},{4,5},{5,6},{6,7},{7,4},{8,9},{9,10},{10,1... | collective-permute-start | bytes 196616 | tf_op jit(solution)/shard_map/ppermute | solution.py:58
  108.2 23.0 %collective-permute-start.7 = (f32[4,8,512]{2,1,0:T(8,128)S(1)}, f32[4,8,512]{2,1,0:T(8,128)S(1)}, u32[]{:S(2)}, u32[]{:S(2)}) collective-permute-start(f32[4,8,512]{2,1,0:T(8,128)S(1)} %get-tuple-element.13), channel_id=1, source_target_pairs={{0,2},{1,3},{2,0},{3,1},{4,6},{5,7},{6,4},{7,5},{8,10},{9,11},{10,... | collective-permute-start | bytes 196616 | tf_op jit(solution)/shard_map/ppermute | solution.py:58
  117.4 52.6 %copy-start.2 = (s32[16,16]{1,0:T(8,128)S(1)}, s32[16,16]{1,0:T(8,128)}, u32[]{:S(2)}) copy-start(s32[16,16]{1,0:T(8,128)} %param.13) | copy-start | bytes 3076
  125.7 5.5 %collective-permute-start.8 = (f32[4,8,512]{2,1,0:T(8,128)S(1)}, f32[4,8,512]{2,1,0:T(8,128)S(1)}, u32[]{:S(2)}, u32[]{:S(2)}) collective-permute-start(f32[4,8,512]{2,1,0:T(8,128)S(1)} %get-tuple-element.13), channel_id=1, source_target_pairs={{0,3},{1,0},{2,1},{3,2},{4,7},{5,4},{6,5},{7,6},{8,11},{9,8},{10,9... | collective-permute-start | bytes 196616 | tf_op jit(solution)/shard_map/ppermute | solution.py:58
  127.3 10.5 %collective-permute-start.10 = (f32[768,32]{1,0:T(8,128)S(1)}, f32[768,32]{1,0:T(8,128)S(1)}, u32[]{:S(2)}, u32[]{:S(2)}) collective-permute-start(f32[768,32]{1,0:T(8,128)S(1)} %select_reduce_fusion), channel_id=1, source_target_pairs={{0,2},{1,3},{2,0},{3,1},{4,6},{5,7},{6,4},{7,5},{8,10},{9,11},{10,... | collective-permute-start | bytes 294920 | tf_op jit(solution)/shard_map/ppermute | solution.py:58
  129.6 16.6 %collective-permute-start.11 = (f32[768,32]{1,0:T(8,128)S(1)}, f32[768,32]{1,0:T(8,128)S(1)}, u32[]{:S(2)}, u32[]{:S(2)}) collective-permute-start(f32[768,32]{1,0:T(8,128)S(1)} %select_reduce_fusion), channel_id=1, source_target_pairs={{0,3},{1,0},{2,1},{3,2},{4,7},{5,4},{6,5},{7,6},{8,11},{9,8},{10,9... | collective-permute-start | bytes 294920 | tf_op jit(solution)/shard_map/ppermute | solution.py:58
  130.4 17.9 %collective-permute-start.9 = (f32[768,32]{1,0:T(8,128)S(1)}, f32[768,32]{1,0:T(8,128)S(1)}, u32[]{:S(2)}, u32[]{:S(2)}) collective-permute-start(f32[768,32]{1,0:T(8,128)S(1)} %select_reduce_fusion), channel_id=1, source_target_pairs={{0,1},{1,2},{2,3},{3,0},{4,5},{5,6},{6,7},{7,4},{8,9},{9,10},{10,1... | collective-permute-start | bytes 294920 | tf_op jit(solution)/shard_map/ppermute | solution.py:58
  149.3 18.4 %all-to-all-start.1 = ((f32[64,1,524]{2,1,0:T(1,128)}), f32[64,1,524]{2,1,0:T(1,128)S(1)}, u32[]{:S(2)}, u32[]{:S(2)}) async-start(f32[64,1,524]{2,1,0:T(1,128)} %all_to_all.16), calls=%async_computation.1 | async-start | bytes 327680 | tf_op jit(solution)/shard_map/all_to_all | solution.py:95
Sparse Core Ops, SparseCore 0:
  19.9 60.1 all-gather.1

commit v13 on v11

--- a/solution.py
+++ b/solution.py
@@ -87,13 +87,15 @@
         return values
 
     complete = cent_max(partial_value)
-    best_all = cent_max(local_best.reshape(shard_total, query_count * query_tokens))
+    best_all = local_best.reshape(shard_total, query_count * query_tokens)
     pair_scores = (jnp.sum(complete, axis=1) / query_tokens).reshape(shard_total, capacity)
 
     outgoing = jnp.concatenate([best_all, pair_scores], axis=1)
     incoming = lax.all_to_all(outgoing, shard, split_axis=0, concat_axis=0, tiled=True)
-    token_best = jnp.max(incoming[:, : query_count * query_tokens], axis=0).reshape(
-        query_count, query_tokens
+    token_best = cent_max(
+        jnp.max(incoming[:, : query_count * query_tokens], axis=0).reshape(
+            query_count, query_tokens
+        )
     )
     returned = incoming[:, query_count * query_tokens:]
 

time: 157 us -> 155 us (0.987)
  starting transfers between devices: 34.1 us -> 31.3 us
    ppermute x6, starting transfers between devices: 7 us -> 5.12 us  [cent_max(): lax.ppermute(values, 'cent', [(i, (i + shift) % cent_total) for i in rang...]
  transfers between devices with their start and end apart: 12 -> 12, of which waited for: 7 -> 8; matrix products, arithmetic and copies ran while one was open for 24% -> 25% of each run, Pallas kernels for 0% -> 0%
where the time goes in v13:
time: 155 us; the launch traced here: 154 us
  waiting for transfers between devices  47.3 us (31%)
  starting transfers between devices  31.3 us (20%)
  local copies, waits for them, and re-layouts  30.9 us (20%)
  matrix products  22.6 us (15%)
  between operations  14.4 us (9%)
  other arithmetic  7.62 us (5%)
    all_gather x1, waiting for transfers between devices, per_device(): lax.all_gather(jnp.concatenate(along_y, axis=0), 'rest', axis=0, tiled=True)  18.6 us
    dot_general x1, matrix products, per_device(): jnp.einsum('rd,cd->rc', flattened, centroids, preferred_element_type=jnp....  13.7 us
    all_to_all x1, starting transfers between devices, per_device(): lax.all_to_all(table, shard, split_axis=0, concat_axis=0, tiled=True)  11.9 us
    all_to_all x1, waiting for transfers between devices, per_device(): lax.all_to_all(outgoing, shard, split_axis=0, concat_axis=0, tiled=True)  9.11 us
    dot_general x1, matrix products, per_device(): jnp.einsum('ntd,npd->ntp', asked, chosen, preferred_element_type=jnp.floa...  8.89 us
    all_to_all x1, waiting for transfers between devices, per_device(): lax.all_to_all(table, shard, split_axis=0, concat_axis=0, tiled=True)  8.44 us
    gather x1, local copies, waits for them, and re-layouts, per_device(): asked = jnp.take(query_block, query_table, axis=0)  8.29 us
    all_to_all x1, starting transfers between devices, per_device(): lax.all_to_all(outgoing, shard, split_axis=0, concat_axis=0, tiled=True)  7.76 us
  transfers between devices with their start and end apart: 12, of which 8 were waited for; matrix products, arithmetic and copies ran while one was open for 25% of the time, Pallas kernels for 0%

profile of v13, /device:TPU:1, one launch (start us, length us, event | category | flops | bytes accessed | tf_op | source)
XLA Modules:
  0.0 154.0 jit_solution(12811848021422557147)
XLA Ops:
  7.2 3.8 %collective-permute-start.1 = (bf16[16,32,128]{2,1,0:T(8,128)(2,1)}, bf16[16,32,128]{2,1,0:T(8,128)(2,1)S(1)}, u32[]{:S(2)}, u32[]{:S(2)}) collective-permute-start(bf16[16,32,128]{2,1,0:T(8,128)(2,1)} %param.6), channel_id=1, source_target_pairs={{0,128},{64,192},{128,0},{192,64},{1,129},{65,193},{129,1},{193,65... | collective-permute-start | bytes 393224 | tf_op jit(solution)/shard_map/ppermute | solution.py:44
  11.5 2.3 %collective-permute-start.2 = (bf16[16,32,128]{2,1,0:T(8,128)(2,1)}, bf16[16,32,128]{2,1,0:T(8,128)(2,1)S(1)}, u32[]{:S(2)}, u32[]{:S(2)}) collective-permute-start(bf16[16,32,128]{2,1,0:T(8,128)(2,1)} %param.6), channel_id=1, source_target_pairs={{0,192},{64,0},{128,64},{192,128},{1,193},{65,1},{129,65},{193,129... | collective-permute-start | bytes 393224 | tf_op jit(solution)/shard_map/ppermute | solution.py:44
  13.7 4.9 %collective-permute-done = bf16[16,32,128]{2,1,0:T(8,128)(2,1)S(1)} collective-permute-done((bf16[16,32,128]{2,1,0:T(8,128)(2,1)}, bf16[16,32,128]{2,1,0:T(8,128)(2,1)S(1)}, u32[]{:S(2)}, u32[]{:S(2)}) %collective-permute-start) | collective-permute-done | bytes 131104 | tf_op jit(solution)/shard_map/ppermute | solution.py:44
  18.6 1.8 %pad_maximum_fusion = bf16[64,32,128]{2,1,0:T(8,128)(2,1)} fusion(bf16[16,32,128]{2,1,0:T(8,128)(2,1)S(1)} %collective-permute-done.2, bf16[16,32,128]{2,1,0:T(8,128)(2,1)S(1)} %collective-permute-done.1, bf16[16,32,128]{2,1,0:T(8,128)(2,1)S(1)} %collective-permute-done, bf16[16,32,128]{2,1,0:T(8,128)(2,1)} %param.6), kind=kLoop, calls=%fused_computation.15 | loop fusion | flops 786432 | bytes 1048576 | tf_op jit(solution)/shard_map/concatenate | solution.py:48
  20.4 0.8 reshape.581
  21.2 0.8 reshape.582
  22.0 0.8 reshape.583
  22.8 2.1 %gather_fusion.1 = s32[256]{0:T(256)S(1)} fusion(s32[16384]{0:T(1024)} %param.10, s32[1024]{0:T(1024)S(1)} %pad_clamp_fusion.3), kind=kCustom, calls=%fused_computation.1 | custom fusion | bytes 3072 | tf_op jit(solution)/shard_map/jit(_take)/gather | solution.py:24
  26.6 1.2 scatter_custom_fusion
  28.6 11.9 %all-to-all-start = ((s32[64,1,24]{2,1,0:T(1,128)}), s32[64,1,24]{2,1,0:T(1,128)S(1)}, u32[]{:S(2)}, u32[]{:S(2)}) async-start(s32[64,1,24]{2,1,0:T(1,128)} %bitcast.8), calls=%async_computation | async-start | bytes 65536 | tf_op jit(solution)/shard_map/all_to_all | solution.py:50
  41.6 8.4 %all-to-all-done = s32[64,1,24]{2,1,0:T(1,128)S(1)} async-done(((s32[64,1,24]{2,1,0:T(1,128)}), s32[64,1,24]{2,1,0:T(1,128)S(1)}, u32[]{:S(2)}, u32[]{:S(2)}) %all-to-all-start) | async-done | bytes 6176 | tf_op jit(solution)/shard_map/all_to_all | solution.py:50
  51.6 5.0 %gather_fusion.2 = s32[768]{0:T(1024)S(1)} fusion(s32[256]{0:T(256)S(1)} %copy-done.1, s32[1024]{0:T(1024)S(1)} %pad_clamp_fusion.2), kind=kCustom, calls=%fused_computation.2 | custom fusion | bytes 9216 | tf_op jit(solution)/shard_map/jit(_take)/gather | solution.py:74
  56.7 4.5 %gather_fusion.4 = bf16[768,32,128]{2,1,0:T(8,128)(2,1)} fusion(bf16[256,32,128]{2,1,0:T(8,128)(2,1)S(1)} %copy-done, s32[1024]{0:T(1024)S(1)} %pad_clamp_fusion.2), kind=kCustom, calls=%fused_computation.4 | custom fusion | bytes 12585984 | tf_op jit(solution)/shard_map/jit(_take)/gather | solution.py:71
  61.5 18.6 %all-gather.2.cloned.1.call-done = bf16[1024,32,128]{2,1,0:T(8,128)(2,1)} async-done(((bf16[64,32,128]{2,1,0:T(8,128)(2,1)}), bf16[1024,32,128]{2,1,0:T(8,128)(2,1)}) %all-gather.2.cloned.1.call-update) | async-done | bytes 8388624 | tf_op jit(solution)/shard_map/all_gather | solution.py:47
  80.1 8.3 %gather_fusion.3 = bf16[768,32,128]{2,1,0:T(8,128)(2,1)} fusion(bf16[1024,32,128]{2,1,0:T(8,128)(2,1)} %all-gather.2.cloned.1.call-done, s32[1024]{0:T(1024)S(1)} %pad_clamp_fusion.1), kind=kCustom, calls=%fused_computation.3 | custom fusion | bytes 12585984 | tf_op jit(solution)/shard_map/jit(_take)/gather | solution.py:70
  88.3 8.9 %select_reduce_fusion = f32[768,32]{1,0:T(8,128)S(1)} fusion(pred[768,32]{1,0:T(8,128)(4,1)S(1)} %broadcast_compare_fusion, bf16[768,32,128]{2,1,0:T(8,128)(2,1)} %gather_fusion.4, pred[768]{0:T(1024)(128)(4,1)S(1)} %le.102, bf16[768,32,128]{2,1,0:T(8,128)(2,1)} %gather_fusion.3, pred[768]{0:T(1024)(128)(4,1)S(1)} %compare_and_fusion), kind=kOutput, calls=%fused_computation.8 | convolution fusion | flops 209166336 | bytes 12707328 | tf_op jit(solution)/shard_map/ntd,npd->ntp/dot_general | solution.py:72
  97.2 2.5 %collective-permute-start.5 = (f32[768,32]{1,0:T(8,128)S(1)}, f32[768,32]{1,0:T(8,128)}, u32[]{:S(2)}, u32[]{:S(2)}) collective-permute-start(f32[768,32]{1,0:T(8,128)S(1)} %select_reduce_fusion), channel_id=1, source_target_pairs={{0,3},{1,0},{2,1},{3,2},{4,7},{5,4},{6,5},{7,6},{8,11},{9,8},{10,9... | collective-permute-start | bytes 294920 | tf_op jit(solution)/shard_map/ppermute | solution.py:82
  100.9 13.7 %convolution_reduce_fusion = f32[32768]{0:T(1024)S(1)} fusion(bf16[32768,128]{1,0:T(8,128)(2,1)S(1)} %bitcast.56, bf16[768,128]{1,0:T(8,128)(2,1)S(1)} %copy-done.7), kind=kOutput, calls=%fused_computation.7 | convolution fusion | flops 6467584000 | bytes 8716288 | tf_op jit(solution)/shard_map/rd,cd->rc/dot_general | solution.py:55
  116.2 4.6 %collective-permute-done.3 = f32[768,32]{1,0:T(8,128)} collective-permute-done((f32[768,32]{1,0:T(8,128)S(1)}, f32[768,32]{1,0:T(8,128)}, u32[]{:S(2)}, u32[]{:S(2)}) %collective-permute-start.3) | collective-permute-done | bytes 98336 | tf_op jit(solution)/shard_map/ppermute | solution.py:82
  120.8 1.4 maximum_reduce_fusion
  122.4 0.8 all_to_all.16
  123.2 7.8 %all-to-all-start.1 = ((f32[64,1,524]{2,1,0:T(1,128)}), f32[64,1,524]{2,1,0:T(1,128)S(1)}, u32[]{:S(2)}, u32[]{:S(2)}) async-start(f32[64,1,524]{2,1,0:T(1,128)} %all_to_all.16), calls=%async_computation.1 | async-start | bytes 327680 | tf_op jit(solution)/shard_map/all_to_all | solution.py:94
  132.4 9.1 %all-to-all-done.1 = f32[64,1,524]{2,1,0:T(1,128)S(1)} async-done(((f32[64,1,524]{2,1,0:T(1,128)}), f32[64,1,524]{2,1,0:T(1,128)S(1)}, u32[]{:S(2)}, u32[]{:S(2)}) %all-to-all-start.1) | async-done | bytes 134176 | tf_op jit(solution)/shard_map/all_to_all | solution.py:94
  143.2 1.4 gather_fusion.5
  (90 shorter events, 14.5 us)
Async XLA Ops:
  7.2 49.5 %copy-start = (bf16[256,32,128]{2,1,0:T(8,128)(2,1)S(1)}, bf16[256,32,128]{2,1,0:T(8,128)(2,1)}, u32[]{:S(2)}) copy-start(bf16[256,32,128]{2,1,0:T(8,128)(2,1)} %param.8) | copy-start | bytes 6291460
  7.2 44.5 %copy-start.1 = (s32[256]{0:T(256)S(1)}, s32[256]{0:T(256)}, u32[]{:S(2)}) copy-start(s32[256]{0:T(256)} %param.9) | copy-start | bytes 3076
  7.2 72.9 %all-gather.2.cloned.1.call-start = ((), (), s32[]{:S(2)}) async-start(), calls=%async_computation.2 | async-start | bytes 8912896 | tf_op jit(solution)/shard_map/all_gather | solution.py:47
  7.2 6.5 %collective-permute-start.1 = (bf16[16,32,128]{2,1,0:T(8,128)(2,1)}, bf16[16,32,128]{2,1,0:T(8,128)(2,1)S(1)}, u32[]{:S(2)}, u32[]{:S(2)}) collective-permute-start(bf16[16,32,128]{2,1,0:T(8,128)(2,1)} %param.6), channel_id=1, source_target_pairs={{0,128},{64,192},{128,0},{192,64},{1,129},{65,193},{129,1},{193,65... | collective-permute-start | bytes 393224 | tf_op jit(solution)/shard_map/ppermute | solution.py:44
  11.1 7.6 %collective-permute-start = (bf16[16,32,128]{2,1,0:T(8,128)(2,1)}, bf16[16,32,128]{2,1,0:T(8,128)(2,1)S(1)}, u32[]{:S(2)}, u32[]{:S(2)}) collective-permute-start(bf16[16,32,128]{2,1,0:T(8,128)(2,1)} %param.6), channel_id=1, source_target_pairs={{0,64},{64,128},{128,192},{192,0},{1,65},{65,129},{129,193},{193,1... | collective-permute-start | bytes 393224 | tf_op jit(solution)/shard_map/ppermute | solution.py:44
  11.5 7.2 %collective-permute-start.2 = (bf16[16,32,128]{2,1,0:T(8,128)(2,1)}, bf16[16,32,128]{2,1,0:T(8,128)(2,1)S(1)}, u32[]{:S(2)}, u32[]{:S(2)}) collective-permute-start(bf16[16,32,128]{2,1,0:T(8,128)(2,1)} %param.6), channel_id=1, source_target_pairs={{0,192},{64,0},{128,64},{192,128},{1,193},{65,1},{129,65},{193,129... | collective-permute-start | bytes 393224 | tf_op jit(solution)/shard_map/ppermute | solution.py:44
  26.0 0.5 copy-start.4
  26.6 34.6 %copy-start.5 = (s32[256,1]{0,1:T(1,128)}, s32[256,1]{0,1:T(1,128)S(1)}, u32[]{:S(2)}) copy-start(s32[256,1]{0,1:T(1,128)S(1)} %compare_select_fusion.9) | copy-start | bytes 3076
  28.6 21.5 %all-to-all-start = ((s32[64,1,24]{2,1,0:T(1,128)}), s32[64,1,24]{2,1,0:T(1,128)S(1)}, u32[]{:S(2)}, u32[]{:S(2)}) async-start(s32[64,1,24]{2,1,0:T(1,128)} %bitcast.8), calls=%async_computation | async-start | bytes 65536 | tf_op jit(solution)/shard_map/all_to_all | solution.py:50
  88.3 12.5 %copy-start.2 = (bf16[1024,32,128]{2,1,0:T(8,128)(2,1)S(1)}, bf16[1024,32,128]{2,1,0:T(8,128)(2,1)}, u32[]{:S(2)}) copy-start(bf16[1024,32,128]{2,1,0:T(8,128)(2,1)} %all-gather.2.cloned.1.call-done) | copy-start | bytes 25165828
  88.3 12.5 %copy-start.7 = (bf16[768,128]{1,0:T(8,128)(2,1)S(1)}, bf16[768,128]{1,0:T(8,128)(2,1)}, u32[]{:S(2)}) copy-start(bf16[768,128]{1,0:T(8,128)(2,1)} %param.7) | copy-start | bytes 589828
  97.2 19.0 %collective-permute-start.5 = (f32[768,32]{1,0:T(8,128)S(1)}, f32[768,32]{1,0:T(8,128)}, u32[]{:S(2)}, u32[]{:S(2)}) collective-permute-start(f32[768,32]{1,0:T(8,128)S(1)} %select_reduce_fusion), channel_id=1, source_target_pairs={{0,3},{1,0},{2,1},{3,2},{4,7},{5,4},{6,5},{7,6},{8,11},{9,8},{10,9... | collective-permute-start | bytes 294920 | tf_op jit(solution)/shard_map/ppermute | solution.py:82
  99.7 16.5 %collective-permute-start.4 = (f32[768,32]{1,0:T(8,128)S(1)}, f32[768,32]{1,0:T(8,128)}, u32[]{:S(2)}, u32[]{:S(2)}) collective-permute-start(f32[768,32]{1,0:T(8,128)S(1)} %select_reduce_fusion), channel_id=1, source_target_pairs={{0,2},{1,3},{2,0},{3,1},{4,6},{5,7},{6,4},{7,5},{8,10},{9,11},{10,... | collective-permute-start | bytes 294920 | tf_op jit(solution)/shard_map/ppermute | solution.py:82
  100.3 20.5 %collective-permute-start.3 = (f32[768,32]{1,0:T(8,128)S(1)}, f32[768,32]{1,0:T(8,128)}, u32[]{:S(2)}, u32[]{:S(2)}) collective-permute-start(f32[768,32]{1,0:T(8,128)S(1)} %select_reduce_fusion), channel_id=1, source_target_pairs={{0,1},{1,2},{2,3},{3,0},{4,5},{5,6},{6,7},{7,4},{8,9},{9,10},{10,1... | collective-permute-start | bytes 294920 | tf_op jit(solution)/shard_map/ppermute | solution.py:82
  100.9 14.6 %copy-start.6 = (pred[4]{0:T(512)(128)(4,1)S(1)}, pred[4]{0:T(512)(128)(4,1)}, u32[]{:S(2)}) copy-start(pred[4]{0:T(512)(128)(4,1)} %compare_and_fusion.1) | copy-start | bytes 16
  114.6 30.1 %copy-start.3 = (s32[16,16]{1,0:T(8,128)S(1)}, s32[16,16]{1,0:T(8,128)}, u32[]{:S(2)}) copy-start(s32[16,16]{1,0:T(8,128)} %param.11) | copy-start | bytes 3076
  123.2 18.4 %all-to-all-start.1 = ((f32[64,1,524]{2,1,0:T(1,128)}), f32[64,1,524]{2,1,0:T(1,128)S(1)}, u32[]{:S(2)}, u32[]{:S(2)}) async-start(f32[64,1,524]{2,1,0:T(1,128)} %all_to_all.16), calls=%async_computation.1 | async-start | bytes 327680 | tf_op jit(solution)/shard_map/all_to_all | solution.py:94
  141.7 3.7 %collective-permute-start.8 = (f32[16,32]{1,0:T(8,128)S(1)}, f32[16,32]{1,0:T(8,128)S(1)}, u32[]{:S(2)}, u32[]{:S(2)}) collective-permute-start(f32[16,32]{1,0:T(8,128)S(1)} %reshape.586), channel_id=1, source_target_pairs={{0,3},{1,0},{2,1},{3,2},{4,7},{5,4},{6,5},{7,6},{8,11},{9,8},{10,9... | collective-permute-start | bytes 6152 | tf_op jit(solution)/shard_map/ppermute | solution.py:82
  142.0 4.0 %collective-permute-start.7 = (f32[16,32]{1,0:T(8,128)S(1)}, f32[16,32]{1,0:T(8,128)S(1)}, u32[]{:S(2)}, u32[]{:S(2)}) collective-permute-start(f32[16,32]{1,0:T(8,128)S(1)} %reshape.586), channel_id=1, source_target_pairs={{0,2},{1,3},{2,0},{3,1},{4,6},{5,7},{6,4},{7,5},{8,10},{9,11},{10,... | collective-permute-start | bytes 6152 | tf_op jit(solution)/shard_map/ppermute | solution.py:82
  142.6 4.0 %collective-permute-start.6 = (f32[16,32]{1,0:T(8,128)S(1)}, f32[16,32]{1,0:T(8,128)S(1)}, u32[]{:S(2)}, u32[]{:S(2)}) collective-permute-start(f32[16,32]{1,0:T(8,128)S(1)} %reshape.586), channel_id=1, source_target_pairs={{0,1},{1,2},{2,3},{3,0},{4,5},{5,6},{6,7},{7,4},{8,9},{9,10},{10,1... | collective-permute-start | bytes 6152 | tf_op jit(solution)/shard_map/ppermute | solution.py:82
Sparse Core Ops, SparseCore 0:
  20.5 59.4 all-gather.1

commit v14 on v13

--- a/solution.py
+++ b/solution.py
@@ -67,13 +67,15 @@
     query_table = (
         (source_shard % rest_total) * y_total + (my_y - source_shard // rest_total) % y_total
     ) * query_count + global_query % query_count
-    asked = jnp.take(query_block, query_table, axis=0)
-    chosen = jnp.take(passages, slot_table, axis=0)
-    pair_scored = jnp.einsum("ntd,npd->ntp", asked, chosen, preferred_element_type=jnp.float32)
     token_index = lax.axis_index("cent") * token_rows + jnp.arange(token_rows, dtype=jnp.int32)
-    valid_tokens = token_index[None, :] < jnp.take(lengths, slot_table, axis=0)[:, None]
-    pair_scored = jnp.where(valid_tokens[:, None, :], pair_scored, masked_score)
-    partial_value = jnp.max(pair_scored, axis=2)
+
+    def pair_maxima(query_rows, slot_rows):
+        asked = jnp.take(query_block, query_rows, axis=0)
+        chosen = jnp.take(passages, slot_rows, axis=0)
+        pair_scored = jnp.einsum("ntd,npd->ntp", asked, chosen, preferred_element_type=jnp.float32)
+        valid_tokens = token_index[None, :] < jnp.take(lengths, slot_rows, axis=0)[:, None]
+        pair_scored = jnp.where(valid_tokens[:, None, :], pair_scored, masked_score)
+        return jnp.max(pair_scored, axis=2)
 
     cent_total = lax.axis_size("cent")
 
@@ -86,7 +88,21 @@
             values = jnp.maximum(values, other)
         return values
 
-    complete = cent_max(partial_value)
+    pair_total = shard_total * capacity
+    pair_halves = 2 if pair_total % 2 == 0 else 1
+    half_size = pair_total // pair_halves
+    complete = jnp.concatenate(
+        [
+            cent_max(
+                pair_maxima(
+                    query_table[h * half_size:(h + 1) * half_size],
+                    slot_table[h * half_size:(h + 1) * half_size],
+                )
+            )
+            for h in range(pair_halves)
+        ],
+        axis=0,
+    )
     best_all = local_best.reshape(shard_total, query_count * query_tokens)
     pair_scores = (jnp.sum(complete, axis=1) / query_tokens).reshape(shard_total, capacity)
 

time: 155 us -> 171 us (1.10)
  starting transfers between devices: 31.3 us -> 37.1 us
  local copies, waits for them, and re-layouts: 30.9 us -> 36.1 us
  matrix products: 22.6 us -> 27.7 us
    gather x3 -> x6, local copies, waits for them, and re-layouts: 17.8 us -> 24.3 us  [the longest x2 12.2 us: pair_maxima(): asked = jnp.take(query_block, query_rows, axis=0)]
    ppermute x6 -> x9, starting transfers between devices: 5.12 us -> 8.56 us  [cent_max(): lax.ppermute(values, 'cent', [(i, (i + shift) % cent_total) for i in rang...]
    dot_general x1, matrix products: 13.7 us -> 17 us  [per_device(): jnp.einsum('rd,cd->rc', flattened, centroids, preferred_element_type=jnp....]
    all_to_all x1, starting transfers between devices: 7.76 us -> 10.1 us  [per_device(): lax.all_to_all(outgoing, shard, split_axis=0, concat_axis=0, tiled=True)]
    max x1 -> x3, other arithmetic: 0.6 us -> 2.82 us  [cent_max(): values = jnp.maximum(values, other)]
    dot_general x1 -> x2, matrix products: 8.89 us -> 10.7 us  [pair_maxima(): jnp.einsum('ntd,npd->ntp', asked, chosen, preferred_element_type=jnp.floa...]
    all_gather x1, waiting for transfers between devices: 18.6 us -> 16.8 us  [per_device(): lax.all_gather(jnp.concatenate(along_y, axis=0), 'rest', axis=0, tiled=True)]
    ppermute x6 -> x9, waiting for transfers between devices: 6.24 us -> 6 us  [cent_max(): lax.ppermute(values, 'cent', [(i, (i + shift) % cent_total) for i in rang...]
  transfers between devices with their start and end apart: 12 -> 15, of which waited for: 8 -> 7; matrix products, arithmetic and copies ran while one was open for 25% -> 32% of each run, Pallas kernels for 0% -> 0%
where the time goes in v14:
time: 171 us; the launch traced here: 170 us
  waiting for transfers between devices  47.1 us (28%)
  starting transfers between devices  37.1 us (22%)
  local copies, waits for them, and re-layouts  36.1 us (21%)
  matrix products  27.7 us (16%)
  between operations  14.5 us (8%)
  other arithmetic  7.77 us (5%)
    dot_general x1, matrix products, per_device(): jnp.einsum('rd,cd->rc', flattened, centroids, preferred_element_type=jnp....  17 us
    all_gather x1, waiting for transfers between devices, per_device(): lax.all_gather(jnp.concatenate(along_y, axis=0), 'rest', axis=0, tiled=True)  16.8 us
    gather x2, local copies, waits for them, and re-layouts, pair_maxima(): asked = jnp.take(query_block, query_rows, axis=0)  12.2 us
    all_to_all x1, starting transfers between devices, per_device(): lax.all_to_all(table, shard, split_axis=0, concat_axis=0, tiled=True)  11.9 us
    dot_general x2, matrix products, pair_maxima(): jnp.einsum('ntd,npd->ntp', asked, chosen, preferred_element_type=jnp.floa...  10.7 us
    all_to_all x1, waiting for transfers between devices, per_device(): lax.all_to_all(outgoing, shard, split_axis=0, concat_axis=0, tiled=True)  10.4 us
    all_to_all x1, starting transfers between devices, per_device(): lax.all_to_all(outgoing, shard, split_axis=0, concat_axis=0, tiled=True)  10.1 us
    all_to_all x1, waiting for transfers between devices, per_device(): lax.all_to_all(table, shard, split_axis=0, concat_axis=0, tiled=True)  8.95 us
  transfers between devices with their start and end apart: 15, of which 7 were waited for; matrix products, arithmetic and copies ran while one was open for 32% of the time, Pallas kernels for 0%

profile of v14, /device:TPU:1, one launch (start us, length us, event | category | flops | bytes accessed | tf_op | source)
XLA Modules:
  0.0 170.2 jit_solution(10548040042128501639)
XLA Ops:
  7.2 3.8 %collective-permute-start.1 = (bf16[16,32,128]{2,1,0:T(8,128)(2,1)}, bf16[16,32,128]{2,1,0:T(8,128)(2,1)S(1)}, u32[]{:S(2)}, u32[]{:S(2)}) collective-permute-start(bf16[16,32,128]{2,1,0:T(8,128)(2,1)} %param.12), channel_id=1, source_target_pairs={{0,128},{64,192},{128,0},{192,64},{1,129},{65,193},{129,1},{193,65... | collective-permute-start | bytes 393224 | tf_op jit(solution)/shard_map/ppermute | solution.py:44
  11.5 2.3 %collective-permute-start.2 = (bf16[16,32,128]{2,1,0:T(8,128)(2,1)}, bf16[16,32,128]{2,1,0:T(8,128)(2,1)S(1)}, u32[]{:S(2)}, u32[]{:S(2)}) collective-permute-start(bf16[16,32,128]{2,1,0:T(8,128)(2,1)} %param.12), channel_id=1, source_target_pairs={{0,192},{64,0},{128,64},{192,128},{1,193},{65,1},{129,65},{193,129... | collective-permute-start | bytes 393224 | tf_op jit(solution)/shard_map/ppermute | solution.py:44
  13.7 4.9 %collective-permute-done = bf16[16,32,128]{2,1,0:T(8,128)(2,1)S(1)} collective-permute-done((bf16[16,32,128]{2,1,0:T(8,128)(2,1)}, bf16[16,32,128]{2,1,0:T(8,128)(2,1)S(1)}, u32[]{:S(2)}, u32[]{:S(2)}) %collective-permute-start) | collective-permute-done | bytes 131104 | tf_op jit(solution)/shard_map/ppermute | solution.py:44
  18.6 1.8 %pad_maximum_fusion = bf16[64,32,128]{2,1,0:T(8,128)(2,1)} fusion(bf16[16,32,128]{2,1,0:T(8,128)(2,1)S(1)} %collective-permute-done.2, bf16[16,32,128]{2,1,0:T(8,128)(2,1)S(1)} %collective-permute-done.1, bf16[16,32,128]{2,1,0:T(8,128)(2,1)S(1)} %collective-permute-done, bf16[16,32,128]{2,1,0:T(8,128)(2,1)} %param.12), kind=kLoop, calls=%fused_computation.25 | loop fusion | flops 786432 | bytes 1048576 | tf_op jit(solution)/shard_map/concatenate | solution.py:48
  22.8 2.1 %gather_fusion.1 = s32[256]{0:T(256)S(1)} fusion(s32[16384]{0:T(1024)} %param.16, s32[1024]{0:T(1024)S(1)} %pad_clamp_fusion.5), kind=kCustom, calls=%fused_computation.7 | custom fusion | bytes 3072 | tf_op jit(solution)/shard_map/jit(_take)/gather | solution.py:24
  26.1 1.2 scatter_custom_fusion
  28.1 11.9 %all-to-all-start = ((s32[64,1,24]{2,1,0:T(1,128)}), s32[64,1,24]{2,1,0:T(1,128)S(1)}, u32[]{:S(2)}, u32[]{:S(2)}) async-start(s32[64,1,24]{2,1,0:T(1,128)} %bitcast.8), calls=%async_computation | async-start | bytes 65536 | tf_op jit(solution)/shard_map/all_to_all | solution.py:50
  40.5 8.9 %all-to-all-done = s32[64,1,24]{2,1,0:T(1,128)S(1)} async-done(((s32[64,1,24]{2,1,0:T(1,128)}), s32[64,1,24]{2,1,0:T(1,128)S(1)}, u32[]{:S(2)}, u32[]{:S(2)}) %all-to-all-start) | async-done | bytes 6176 | tf_op jit(solution)/shard_map/all_to_all | solution.py:50
  50.1 2.8 %gather_fusion.3 = s32[384]{0:T(512)S(1)} fusion(s32[256]{0:T(256)S(1)} %copy-done.1, s32[1024]{0:T(1024)S(1)} %pad_clamp_fusion.4), kind=kCustom, calls=%fused_computation.clone | custom fusion | bytes 4608 | tf_op jit(solution)/shard_map/jit(_take)/gather | solution.py:76
  52.9 2.8 %gather_fusion.6 = s32[384]{0:T(512)S(1)} fusion(s32[256]{0:T(256)S(1)} %copy-done.1, s32[1024]{0:T(1024)S(1)} %pad_clamp_fusion.2), kind=kCustom, calls=%fused_computation.3.clone | custom fusion | bytes 4608 | tf_op jit(solution)/shard_map/jit(_take)/gather | solution.py:76
  55.8 3.2 %gather_fusion.8 = bf16[384,32,128]{2,1,0:T(8,128)(2,1)} fusion(bf16[256,32,128]{2,1,0:T(8,128)(2,1)S(1)} %copy-done, s32[1024]{0:T(1024)S(1)} %pad_clamp_fusion.2), kind=kCustom, calls=%fused_computation.5.clone | custom fusion | bytes 6292992 | tf_op jit(solution)/shard_map/jit(_take)/gather | solution.py:74
  59.0 3.3 %gather_fusion.5 = bf16[384,32,128]{2,1,0:T(8,128)(2,1)} fusion(bf16[256,32,128]{2,1,0:T(8,128)(2,1)S(1)} %copy-done, s32[1024]{0:T(1024)S(1)} %pad_clamp_fusion.4), kind=kCustom, calls=%fused_computation.2.clone | custom fusion | bytes 6292992 | tf_op jit(solution)/shard_map/jit(_take)/gather | solution.py:74
  63.2 16.8 %all-gather.2.cloned.1.call-done = bf16[1024,32,128]{2,1,0:T(8,128)(2,1)} async-done(((bf16[64,32,128]{2,1,0:T(8,128)(2,1)}), bf16[1024,32,128]{2,1,0:T(8,128)(2,1)}) %all-gather.2.cloned.1.call-update) | async-done | bytes 8388624 | tf_op jit(solution)/shard_map/all_gather | solution.py:47
  80.1 6.0 %gather_fusion.7 = bf16[384,32,128]{2,1,0:T(8,128)(2,1)} fusion(bf16[1024,32,128]{2,1,0:T(8,128)(2,1)} %all-gather.2.cloned.1.call-done, s32[1024]{0:T(1024)S(1)} %pad_clamp_fusion.1), kind=kCustom, calls=%fused_computation.4.clone | custom fusion | bytes 6292992 | tf_op jit(solution)/shard_map/jit(_take)/gather | solution.py:73
  86.1 5.3 %select_reduce_fusion = f32[384,32]{1,0:T(8,128)S(1)} fusion(pred[384,32]{1,0:T(8,128)(4,1)S(1)} %get-tuple-element.21, bf16[384,32,128]{2,1,0:T(8,128)(2,1)} %gather_fusion.8, pred[384]{0:T(512)(128)(4,1)S(1)} %get-tuple-element.8, bf16[384,32,128]{2,1,0:T(8,128)(2,1)} %gather_fusion.7, pred[384]{0:T(512)(128)(4,1)S(1)} %get-tuple-element.17), kind=kOutput, calls=%fused_computation.11 | convolution fusion | flops 104583168 | bytes 6353664 | tf_op jit(solution)/shard_map/ntd,npd->ntp/dot_general | solution.py:75
  91.4 2.5 %collective-permute-start.8 = (f32[384,32]{1,0:T(8,128)S(1)}, f32[384,32]{1,0:T(8,128)}, u32[]{:S(2)}, u32[]{:S(2)}) collective-permute-start(f32[384,32]{1,0:T(8,128)S(1)} %select_reduce_fusion), channel_id=1, source_target_pairs={{0,3},{1,0},{2,1},{3,2},{4,7},{5,4},{6,5},{7,6},{8,11},{9,8},{10,9... | collective-permute-start | bytes 147464 | tf_op jit(solution)/shard_map/ppermute | solution.py:84
  95.1 6.2 %gather_fusion.4 = bf16[384,32,128]{2,1,0:T(8,128)(2,1)} fusion(bf16[1024,32,128]{2,1,0:T(8,128)(2,1)} %all-gather.2.cloned.1.call-done, s32[1024]{0:T(1024)S(1)} %pad_clamp_fusion.3), kind=kCustom, calls=%fused_computation.1.clone | custom fusion | bytes 6292992 | tf_op jit(solution)/shard_map/jit(_take)/gather | solution.py:73
  101.2 5.4 %select_reduce_fusion.1 = f32[384,32]{1,0:T(8,128)S(1)} fusion(pred[384,32]{1,0:T(8,128)(4,1)S(1)} %get-tuple-element.20, bf16[384,32,128]{2,1,0:T(8,128)(2,1)} %gather_fusion.5, pred[384]{0:T(512)(128)(4,1)S(1)} %get-tuple-element.6, bf16[384,32,128]{2,1,0:T(8,128)(2,1)} %gather_fusion.4, pred[384]{0:T(512)(128)(4,1)S(1)} %get-tuple-element.16), kind=kOutput, calls=%fused_computation.12 | convolution fusion | flops 104583168 | bytes 6353664 | tf_op jit(solution)/shard_map/ntd,npd->ntp/dot_general | solution.py:75
  106.6 2.2 %collective-permute-start.5 = (f32[384,32]{1,0:T(8,128)S(1)}, f32[384,32]{1,0:T(8,128)}, u32[]{:S(2)}, u32[]{:S(2)}) collective-permute-start(f32[384,32]{1,0:T(8,128)S(1)} %select_reduce_fusion.1), channel_id=1, source_target_pairs={{0,3},{1,0},{2,1},{3,2},{4,7},{5,4},{6,5},{7,6},{8,11},{9,8},{10,9... | collective-permute-start | bytes 147464 | tf_op jit(solution)/shard_map/ppermute | solution.py:84
  110.0 17.0 %convolution_reduce_fusion = f32[32768]{0:T(1024)S(1)} fusion(bf16[32768,128]{1,0:T(8,128)(2,1)} %bitcast.50, bf16[768,128]{1,0:T(8,128)(2,1)S(1)} %copy-done.3), kind=kOutput, calls=%fused_computation.10 | convolution fusion | flops 6467584000 | bytes 8716288 | tf_op jit(solution)/shard_map/rd,cd->rc/dot_general | solution.py:55
  130.2 4.4 %collective-permute-done.3 = f32[384,32]{1,0:T(8,128)S(1)} collective-permute-done((f32[384,32]{1,0:T(8,128)S(1)}, f32[384,32]{1,0:T(8,128)S(1)}, u32[]{:S(2)}, u32[]{:S(2)}) %collective-permute-start.3) | collective-permute-done | bytes 49184 | tf_op jit(solution)/shard_map/ppermute | solution.py:84
  136.7 10.1 %all-to-all-start.1 = ((f32[64,1,524]{2,1,0:T(1,128)}), f32[64,1,524]{2,1,0:T(1,128)S(1)}, u32[]{:S(2)}, u32[]{:S(2)}) async-start(f32[64,1,524]{2,1,0:T(1,128)} %all_to_all.16), calls=%async_computation.1 | async-start | bytes 327680 | tf_op jit(solution)/shard_map/all_to_all | solution.py:110
  147.0 10.4 %all-to-all-done.1 = f32[64,1,524]{2,1,0:T(1,128)S(1)} async-done(((f32[64,1,524]{2,1,0:T(1,128)}), f32[64,1,524]{2,1,0:T(1,128)S(1)}, u32[]{:S(2)}, u32[]{:S(2)}) %all-to-all-start.1) | async-done | bytes 134176 | tf_op jit(solution)/shard_map/all_to_all | solution.py:110
  159.1 1.4 gather_fusion.2
  (100 shorter events, 19.0 us)
Async XLA Ops:
  7.2 48.6 %copy-start = (bf16[256,32,128]{2,1,0:T(8,128)(2,1)S(1)}, bf16[256,32,128]{2,1,0:T(8,128)(2,1)}, u32[]{:S(2)}) copy-start(bf16[256,32,128]{2,1,0:T(8,128)(2,1)} %param.14) | copy-start | bytes 6291460
  7.2 42.9 %copy-start.1 = (s32[256]{0:T(256)S(1)}, s32[256]{0:T(256)}, u32[]{:S(2)}) copy-start(s32[256]{0:T(256)} %param.15) | copy-start | bytes 3076
  7.2 72.9 %all-gather.2.cloned.1.call-start = ((), (), s32[]{:S(2)}) async-start(), calls=%async_computation.2 | async-start | bytes 8912896 | tf_op jit(solution)/shard_map/all_gather | solution.py:47
  7.2 6.5 %collective-permute-start.1 = (bf16[16,32,128]{2,1,0:T(8,128)(2,1)}, bf16[16,32,128]{2,1,0:T(8,128)(2,1)S(1)}, u32[]{:S(2)}, u32[]{:S(2)}) collective-permute-start(bf16[16,32,128]{2,1,0:T(8,128)(2,1)} %param.12), channel_id=1, source_target_pairs={{0,128},{64,192},{128,0},{192,64},{1,129},{65,193},{129,1},{193,65... | collective-permute-start | bytes 393224 | tf_op jit(solution)/shard_map/ppermute | solution.py:44
  11.1 7.6 %collective-permute-start = (bf16[16,32,128]{2,1,0:T(8,128)(2,1)}, bf16[16,32,128]{2,1,0:T(8,128)(2,1)S(1)}, u32[]{:S(2)}, u32[]{:S(2)}) collective-permute-start(bf16[16,32,128]{2,1,0:T(8,128)(2,1)} %param.12), channel_id=1, source_target_pairs={{0,64},{64,128},{128,192},{192,0},{1,65},{65,129},{129,193},{193,1... | collective-permute-start | bytes 393224 | tf_op jit(solution)/shard_map/ppermute | solution.py:44
  11.5 7.2 %collective-permute-start.2 = (bf16[16,32,128]{2,1,0:T(8,128)(2,1)}, bf16[16,32,128]{2,1,0:T(8,128)(2,1)S(1)}, u32[]{:S(2)}, u32[]{:S(2)}) collective-permute-start(bf16[16,32,128]{2,1,0:T(8,128)(2,1)} %param.12), channel_id=1, source_target_pairs={{0,192},{64,0},{128,64},{192,128},{1,193},{65,1},{129,65},{193,129... | collective-permute-start | bytes 393224 | tf_op jit(solution)/shard_map/ppermute | solution.py:44
  28.1 21.4 %all-to-all-start = ((s32[64,1,24]{2,1,0:T(1,128)}), s32[64,1,24]{2,1,0:T(1,128)S(1)}, u32[]{:S(2)}, u32[]{:S(2)}) async-start(s32[64,1,24]{2,1,0:T(1,128)} %bitcast.8), calls=%async_computation | async-start | bytes 65536 | tf_op jit(solution)/shard_map/all_to_all | solution.py:50
  91.4 37.4 %collective-permute-start.8 = (f32[384,32]{1,0:T(8,128)S(1)}, f32[384,32]{1,0:T(8,128)}, u32[]{:S(2)}, u32[]{:S(2)}) collective-permute-start(f32[384,32]{1,0:T(8,128)S(1)} %select_reduce_fusion), channel_id=1, source_target_pairs={{0,3},{1,0},{2,1},{3,2},{4,7},{5,4},{6,5},{7,6},{8,11},{9,8},{10,9... | collective-permute-start | bytes 147464 | tf_op jit(solution)/shard_map/ppermute | solution.py:84
  93.9 35.0 %collective-permute-start.7 = (f32[384,32]{1,0:T(8,128)S(1)}, f32[384,32]{1,0:T(8,128)}, u32[]{:S(2)}, u32[]{:S(2)}) collective-permute-start(f32[384,32]{1,0:T(8,128)S(1)} %select_reduce_fusion), channel_id=1, source_target_pairs={{0,2},{1,3},{2,0},{3,1},{4,6},{5,7},{6,4},{7,5},{8,10},{9,11},{10,... | collective-permute-start | bytes 147464 | tf_op jit(solution)/shard_map/ppermute | solution.py:84
  94.5 34.4 %collective-permute-start.6 = (f32[384,32]{1,0:T(8,128)S(1)}, f32[384,32]{1,0:T(8,128)}, u32[]{:S(2)}, u32[]{:S(2)}) collective-permute-start(f32[384,32]{1,0:T(8,128)S(1)} %select_reduce_fusion), channel_id=1, source_target_pairs={{0,1},{1,2},{2,3},{3,0},{4,5},{5,6},{6,7},{7,4},{8,9},{9,10},{10,1... | collective-permute-start | bytes 147464 | tf_op jit(solution)/shard_map/ppermute | solution.py:84
  101.2 8.7 %copy-start.3 = (bf16[768,128]{1,0:T(8,128)(2,1)S(1)}, bf16[768,128]{1,0:T(8,128)(2,1)}, u32[]{:S(2)}) copy-start(bf16[768,128]{1,0:T(8,128)(2,1)} %param.13) | copy-start | bytes 589828
  106.6 23.6 %collective-permute-start.5 = (f32[384,32]{1,0:T(8,128)S(1)}, f32[384,32]{1,0:T(8,128)}, u32[]{:S(2)}, u32[]{:S(2)}) collective-permute-start(f32[384,32]{1,0:T(8,128)S(1)} %select_reduce_fusion.1), channel_id=1, source_target_pairs={{0,3},{1,0},{2,1},{3,2},{4,7},{5,4},{6,5},{7,6},{8,11},{9,8},{10,9... | collective-permute-start | bytes 147464 | tf_op jit(solution)/shard_map/ppermute | solution.py:84
  108.8 21.4 %collective-permute-start.4 = (f32[384,32]{1,0:T(8,128)S(1)}, f32[384,32]{1,0:T(8,128)}, u32[]{:S(2)}, u32[]{:S(2)}) collective-permute-start(f32[384,32]{1,0:T(8,128)S(1)} %select_reduce_fusion.1), channel_id=1, source_target_pairs={{0,2},{1,3},{2,0},{3,1},{4,6},{5,7},{6,4},{7,5},{8,10},{9,11},{10,... | collective-permute-start | bytes 147464 | tf_op jit(solution)/shard_map/ppermute | solution.py:84
  128.6 32.0 %copy-start.2 = (s32[16,16]{1,0:T(8,128)S(1)}, s32[16,16]{1,0:T(8,128)}, u32[]{:S(2)}) copy-start(s32[16,16]{1,0:T(8,128)} %param.17) | copy-start | bytes 3076
  128.8 5.8 %collective-permute-start.3 = (f32[384,32]{1,0:T(8,128)S(1)}, f32[384,32]{1,0:T(8,128)S(1)}, u32[]{:S(2)}, u32[]{:S(2)}) collective-permute-start(f32[384,32]{1,0:T(8,128)S(1)} %select_reduce_fusion.1), channel_id=1, source_target_pairs={{0,1},{1,2},{2,3},{3,0},{4,5},{5,6},{6,7},{7,4},{8,9},{9,10},{10,1... | collective-permute-start | bytes 147464 | tf_op jit(solution)/shard_map/ppermute | solution.py:84
  136.7 20.7 %all-to-all-start.1 = ((f32[64,1,524]{2,1,0:T(1,128)}), f32[64,1,524]{2,1,0:T(1,128)S(1)}, u32[]{:S(2)}, u32[]{:S(2)}) async-start(f32[64,1,524]{2,1,0:T(1,128)} %all_to_all.16), calls=%async_computation.1 | async-start | bytes 327680 | tf_op jit(solution)/shard_map/all_to_all | solution.py:110
  157.6 3.7 %collective-permute-start.11 = (f32[16,32]{1,0:T(8,128)S(1)}, f32[16,32]{1,0:T(8,128)S(1)}, u32[]{:S(2)}, u32[]{:S(2)}) collective-permute-start(f32[16,32]{1,0:T(8,128)S(1)} %reshape.418), channel_id=1, source_target_pairs={{0,3},{1,0},{2,1},{3,2},{4,7},{5,4},{6,5},{7,6},{8,11},{9,8},{10,9... | collective-permute-start | bytes 6152 | tf_op jit(solution)/shard_map/ppermute | solution.py:84
  157.6 4.1 %collective-permute-start.10 = (f32[16,32]{1,0:T(8,128)S(1)}, f32[16,32]{1,0:T(8,128)S(1)}, u32[]{:S(2)}, u32[]{:S(2)}) collective-permute-start(f32[16,32]{1,0:T(8,128)S(1)} %reshape.418), channel_id=1, source_target_pairs={{0,2},{1,3},{2,0},{3,1},{4,6},{5,7},{6,4},{7,5},{8,10},{9,11},{10,... | collective-permute-start | bytes 6152 | tf_op jit(solution)/shard_map/ppermute | solution.py:84
  158.2 4.5 %collective-permute-start.9 = (f32[16,32]{1,0:T(8,128)S(1)}, f32[16,32]{1,0:T(8,128)S(1)}, u32[]{:S(2)}, u32[]{:S(2)}) collective-permute-start(f32[16,32]{1,0:T(8,128)S(1)} %reshape.418), channel_id=1, source_target_pairs={{0,1},{1,2},{2,3},{3,0},{4,5},{5,6},{6,7},{7,4},{8,9},{9,10},{10,1... | collective-permute-start | bytes 6152 | tf_op jit(solution)/shard_map/ppermute | solution.py:84
Sparse Core Ops, SparseCore 0:
  20.6 59.4 all-gather.1

commit v15 on v11

--- a/solution.py
+++ b/solution.py
@@ -86,18 +86,20 @@
             values = jnp.maximum(values, other)
         return values
 
-    complete = cent_max(partial_value)
-    best_all = cent_max(local_best.reshape(shard_total, query_count * query_tokens))
-    pair_scores = (jnp.sum(complete, axis=1) / query_tokens).reshape(shard_total, capacity)
+    best_all = local_best.reshape(shard_total, query_count * query_tokens)
+    pair_partials = partial_value.reshape(shard_total, capacity * query_tokens)
 
-    outgoing = jnp.concatenate([best_all, pair_scores], axis=1)
+    outgoing = jnp.concatenate([best_all, pair_partials], axis=1)
     incoming = lax.all_to_all(outgoing, shard, split_axis=0, concat_axis=0, tiled=True)
-    token_best = jnp.max(incoming[:, : query_count * query_tokens], axis=0).reshape(
+    token_part = jnp.max(incoming[:, : query_count * query_tokens], axis=0).reshape(
         query_count, query_tokens
     )
-    returned = incoming[:, query_count * query_tokens:]
-
-    scores = jnp.take(returned.reshape(-1), my_places, axis=0).reshape(query_count, per_query)
+    pair_part = jnp.take(
+        incoming[:, query_count * query_tokens:].reshape(-1, query_tokens), my_places, axis=0
+    )
+    merged = cent_max(jnp.concatenate([token_part, pair_part], axis=0))
+    token_best = merged[:query_count]
+    scores = (jnp.sum(merged[query_count:], axis=1) / query_tokens).reshape(query_count, per_query)
     return (token_best, scores)
 
 

time: 157 us -> 153 us (0.975)
  starting transfers between devices: 34.1 us -> 30.2 us
  other arithmetic: 7.06 us -> 3.53 us
  matrix products: 22.6 us -> 25.5 us
    dot_general x1, matrix products: 13.7 us -> 17.2 us  [per_device(): jnp.einsum('rd,cd->rc', flattened, centroids, preferred_element_type=jnp....]
    ppermute x6 -> x3, starting transfers between devices: 7 us -> 4.2 us  [cent_max(): lax.ppermute(values, 'cent', [(i, (i + shift) % cent_total) for i in rang...]
    ppermute x6 -> x3, waiting for transfers between devices: 6.03 us -> 3.57 us  [cent_max(): lax.ppermute(values, 'cent', [(i, (i + shift) % cent_total) for i in rang...]
    all_to_all x1, waiting for transfers between devices: 9.11 us -> 11.1 us  [per_device(): lax.all_to_all(outgoing, shard, split_axis=0, concat_axis=0, tiled=True)]
  transfers between devices with their start and end apart: 12 -> 9, of which waited for: 7 -> 7; matrix products, arithmetic and copies ran while one was open for 24% -> 12% of each run, Pallas kernels for 0% -> 0%
where the time goes in v15:
time: 153 us; the launch traced here: 152 us
  waiting for transfers between devices  48.1 us (31%)
  local copies, waits for them, and re-layouts  30.5 us (20%)
  starting transfers between devices  30.2 us (20%)
  matrix products  25.5 us (17%)
  between operations  14.4 us (9%)
  other arithmetic  3.53 us (2%)
    all_gather x1, waiting for transfers between devices, per_device(): lax.all_gather(jnp.concatenate(along_y, axis=0), 'rest', axis=0, tiled=True)  19.1 us
    dot_general x1, matrix products, per_device(): jnp.einsum('rd,cd->rc', flattened, centroids, preferred_element_type=jnp....  17.2 us
    all_to_all x1, starting transfers between devices, per_device(): lax.all_to_all(table, shard, split_axis=0, concat_axis=0, tiled=True)  11.9 us
    all_to_all x1, waiting for transfers between devices, per_device(): lax.all_to_all(outgoing, shard, split_axis=0, concat_axis=0, tiled=True)  11.1 us
    all_to_all x1, waiting for transfers between devices, per_device(): lax.all_to_all(table, shard, split_axis=0, concat_axis=0, tiled=True)  9.53 us
    dot_general x1, matrix products, per_device(): jnp.einsum('ntd,npd->ntp', asked, chosen, preferred_element_type=jnp.floa...  8.3 us
    gather x1, local copies, waits for them, and re-layouts, per_device(): asked = jnp.take(query_block, query_table, axis=0)  8.29 us
    all_to_all x1, starting transfers between devices, per_device(): lax.all_to_all(outgoing, shard, split_axis=0, concat_axis=0, tiled=True)  7.55 us
  transfers between devices with their start and end apart: 9, of which 7 were waited for; matrix products, arithmetic and copies ran while one was open for 12% of the time, Pallas kernels for 0%

profile of v15, /device:TPU:1, one launch (start us, length us, event | category | flops | bytes accessed | tf_op | source)
XLA Modules:
  0.0 152.2 jit_solution(8732849371078208326)
XLA Ops:
  7.2 3.8 %collective-permute-start.1 = (bf16[16,32,128]{2,1,0:T(8,128)(2,1)}, bf16[16,32,128]{2,1,0:T(8,128)(2,1)S(1)}, u32[]{:S(2)}, u32[]{:S(2)}) collective-permute-start(bf16[16,32,128]{2,1,0:T(8,128)(2,1)} %param.6), channel_id=1, source_target_pairs={{0,128},{64,192},{128,0},{192,64},{1,129},{65,193},{129,1},{193,65... | collective-permute-start | bytes 393224 | tf_op jit(solution)/shard_map/ppermute | solution.py:44
  11.5 2.3 %collective-permute-start.2 = (bf16[16,32,128]{2,1,0:T(8,128)(2,1)}, bf16[16,32,128]{2,1,0:T(8,128)(2,1)S(1)}, u32[]{:S(2)}, u32[]{:S(2)}) collective-permute-start(bf16[16,32,128]{2,1,0:T(8,128)(2,1)} %param.6), channel_id=1, source_target_pairs={{0,192},{64,0},{128,64},{192,128},{1,193},{65,1},{129,65},{193,129... | collective-permute-start | bytes 393224 | tf_op jit(solution)/shard_map/ppermute | solution.py:44
  13.7 4.9 %collective-permute-done = bf16[16,32,128]{2,1,0:T(8,128)(2,1)S(1)} collective-permute-done((bf16[16,32,128]{2,1,0:T(8,128)(2,1)}, bf16[16,32,128]{2,1,0:T(8,128)(2,1)S(1)}, u32[]{:S(2)}, u32[]{:S(2)}) %collective-permute-start) | collective-permute-done | bytes 131104 | tf_op jit(solution)/shard_map/ppermute | solution.py:44
  18.6 1.8 %pad_maximum_fusion = bf16[64,32,128]{2,1,0:T(8,128)(2,1)} fusion(bf16[16,32,128]{2,1,0:T(8,128)(2,1)S(1)} %collective-permute-done.2, bf16[16,32,128]{2,1,0:T(8,128)(2,1)S(1)} %collective-permute-done.1, bf16[16,32,128]{2,1,0:T(8,128)(2,1)S(1)} %collective-permute-done, bf16[16,32,128]{2,1,0:T(8,128)(2,1)} %param.6), kind=kLoop, calls=%fused_computation.15 | loop fusion | flops 786432 | bytes 1048576 | tf_op jit(solution)/shard_map/concatenate | solution.py:48
  20.4 0.8 reshape.580
  21.2 0.8 reshape.582
  22.0 0.8 reshape.581
  22.8 2.1 %gather_fusion.1 = s32[256]{0:T(256)S(1)} fusion(s32[16384]{0:T(1024)} %param.10, s32[1024]{0:T(1024)S(1)} %pad_clamp_fusion.3), kind=kCustom, calls=%fused_computation.1 | custom fusion | bytes 3072 | tf_op jit(solution)/shard_map/jit(_take)/gather | solution.py:24
  26.1 1.2 scatter_custom_fusion
  28.1 11.9 %all-to-all-start = ((s32[64,1,24]{2,1,0:T(1,128)}), s32[64,1,24]{2,1,0:T(1,128)S(1)}, u32[]{:S(2)}, u32[]{:S(2)}) async-start(s32[64,1,24]{2,1,0:T(1,128)} %bitcast.8), calls=%async_computation | async-start | bytes 65536 | tf_op jit(solution)/shard_map/all_to_all | solution.py:50
  40.0 9.5 %all-to-all-done = s32[64,1,24]{2,1,0:T(1,128)S(1)} async-done(((s32[64,1,24]{2,1,0:T(1,128)}), s32[64,1,24]{2,1,0:T(1,128)S(1)}, u32[]{:S(2)}, u32[]{:S(2)}) %all-to-all-start) | async-done | bytes 6176 | tf_op jit(solution)/shard_map/all_to_all | solution.py:50
  51.1 5.0 %gather_fusion.2 = s32[768]{0:T(1024)S(1)} fusion(s32[256]{0:T(256)S(1)} %copy-done.1, s32[1024]{0:T(1024)S(1)} %pad_clamp_fusion.2), kind=kCustom, calls=%fused_computation.2 | custom fusion | bytes 9216 | tf_op jit(solution)/shard_map/jit(_take)/gather | solution.py:74
  56.2 4.5 %gather_fusion.4 = bf16[768,32,128]{2,1,0:T(8,128)(2,1)} fusion(bf16[256,32,128]{2,1,0:T(8,128)(2,1)S(1)} %copy-done, s32[1024]{0:T(1024)S(1)} %pad_clamp_fusion.2), kind=kCustom, calls=%fused_computation.4 | custom fusion | bytes 12585984 | tf_op jit(solution)/shard_map/jit(_take)/gather | solution.py:71
  61.0 19.1 %all-gather.2.cloned.1.call-done = bf16[1024,32,128]{2,1,0:T(8,128)(2,1)} async-done(((bf16[64,32,128]{2,1,0:T(8,128)(2,1)}), bf16[1024,32,128]{2,1,0:T(8,128)(2,1)}) %all-gather.2.cloned.1.call-update) | async-done | bytes 8388624 | tf_op jit(solution)/shard_map/all_gather | solution.py:47
  80.1 17.2 %convolution_reduce_fusion = f32[32768]{0:T(1024)S(1)} fusion(bf16[32768,128]{1,0:T(8,128)(2,1)} %bitcast.56, bf16[768,128]{1,0:T(8,128)(2,1)S(1)} %copy-done.2), kind=kOutput, calls=%fused_computation.7 | convolution fusion | flops 6467584000 | bytes 8716288 | tf_op jit(solution)/shard_map/rd,cd->rc/dot_general | solution.py:55
  98.4 8.3 %gather_fusion.3 = bf16[768,32,128]{2,1,0:T(8,128)(2,1)} fusion(bf16[1024,32,128]{2,1,0:T(8,128)(2,1)} %all-gather.2.cloned.1.call-done, s32[1024]{0:T(1024)S(1)} %pad_clamp_fusion.1), kind=kCustom, calls=%fused_computation.3 | custom fusion | bytes 12585984 | tf_op jit(solution)/shard_map/jit(_take)/gather | solution.py:70
  106.7 8.3 %select_reduce_fusion = f32[768,32]{1,0:T(8,128)S(1)} fusion(pred[768,32]{1,0:T(8,128)(4,1)S(1)} %broadcast_compare_fusion, bf16[768,32,128]{2,1,0:T(8,128)(2,1)} %gather_fusion.4, pred[768]{0:T(1024)(128)(4,1)S(1)} %le.96, bf16[768,32,128]{2,1,0:T(8,128)(2,1)} %gather_fusion.3, pred[768]{0:T(1024)(128)(4,1)S(1)} %compare_and_fusion), kind=kOutput, calls=%fused_computation.8 | convolution fusion | flops 209166336 | bytes 12707328 | tf_op jit(solution)/shard_map/ntd,npd->ntp/dot_general | solution.py:72
  115.1 0.8 all_to_all.16
  116.0 7.6 %all-to-all-start.1 = ((f32[64,1,896]{2,1,0:T(1,128)}), f32[64,1,896]{2,1,0:T(1,128)S(1)}, u32[]{:S(2)}, u32[]{:S(2)}) async-start(f32[64,1,896]{2,1,0:T(1,128)} %all_to_all.16), calls=%async_computation.1 | async-start | bytes 458752 | tf_op jit(solution)/shard_map/all_to_all | solution.py:93
  123.6 11.1 %all-to-all-done.1 = f32[64,1,896]{2,1,0:T(1,128)S(1)} async-done(((f32[64,1,896]{2,1,0:T(1,128)}), f32[64,1,896]{2,1,0:T(1,128)S(1)}, u32[]{:S(2)}, u32[]{:S(2)}) %all-to-all-start.1) | async-done | bytes 229408 | tf_op jit(solution)/shard_map/all_to_all | solution.py:93
  136.0 2.7 %collective-permute-start.4 = (f32[272,32]{0,1:T(8,128)S(1)}, f32[272,32]{0,1:T(8,128)S(1)}, u32[]{:S(2)}, u32[]{:S(2)}) collective-permute-start(f32[272,32]{0,1:T(8,128)S(1)} %pad_maximum_fusion.2), channel_id=1, source_target_pairs={{0,2},{1,3},{2,0},{3,1},{4,6},{5,7},{6,4},{7,5},{8,10},{9,11},{10,... | collective-permute-start | bytes 104456 | tf_op jit(solution)/shard_map/ppermute | solution.py:82
  138.7 0.9 collective-permute-start.5
  140.5 1.4 collective-permute-done.5
  141.9 1.9 %collective-permute-done.3 = f32[272,32]{0,1:T(8,128)S(1)} collective-permute-done((f32[272,32]{0,1:T(8,128)S(1)}, f32[272,32]{0,1:T(8,128)S(1)}, u32[]{:S(2)}, u32[]{:S(2)}) %collective-permute-start.3) | collective-permute-done | bytes 34848 | tf_op jit(solution)/shard_map/ppermute | solution.py:82
  (78 shorter events, 9.2 us)
Async XLA Ops:
  7.2 49.0 %copy-start = (bf16[256,32,128]{2,1,0:T(8,128)(2,1)S(1)}, bf16[256,32,128]{2,1,0:T(8,128)(2,1)}, u32[]{:S(2)}) copy-start(bf16[256,32,128]{2,1,0:T(8,128)(2,1)} %param.8) | copy-start | bytes 6291460
  7.2 43.9 %copy-start.1 = (s32[256]{0:T(256)S(1)}, s32[256]{0:T(256)}, u32[]{:S(2)}) copy-start(s32[256]{0:T(256)} %param.9) | copy-start | bytes 3076
  7.2 72.9 %all-gather.2.cloned.1.call-start = ((), (), s32[]{:S(2)}) async-start(), calls=%async_computation.2 | async-start | bytes 8912896 | tf_op jit(solution)/shard_map/all_gather | solution.py:47
  7.2 6.5 %collective-permute-start.1 = (bf16[16,32,128]{2,1,0:T(8,128)(2,1)}, bf16[16,32,128]{2,1,0:T(8,128)(2,1)S(1)}, u32[]{:S(2)}, u32[]{:S(2)}) collective-permute-start(bf16[16,32,128]{2,1,0:T(8,128)(2,1)} %param.6), channel_id=1, source_target_pairs={{0,128},{64,192},{128,0},{192,64},{1,129},{65,193},{129,1},{193,65... | collective-permute-start | bytes 393224 | tf_op jit(solution)/shard_map/ppermute | solution.py:44
  11.1 7.6 %collective-permute-start = (bf16[16,32,128]{2,1,0:T(8,128)(2,1)}, bf16[16,32,128]{2,1,0:T(8,128)(2,1)S(1)}, u32[]{:S(2)}, u32[]{:S(2)}) collective-permute-start(bf16[16,32,128]{2,1,0:T(8,128)(2,1)} %param.6), channel_id=1, source_target_pairs={{0,64},{64,128},{128,192},{192,0},{1,65},{65,129},{129,193},{193,1... | collective-permute-start | bytes 393224 | tf_op jit(solution)/shard_map/ppermute | solution.py:44
  11.5 7.2 %collective-permute-start.2 = (bf16[16,32,128]{2,1,0:T(8,128)(2,1)}, bf16[16,32,128]{2,1,0:T(8,128)(2,1)S(1)}, u32[]{:S(2)}, u32[]{:S(2)}) collective-permute-start(bf16[16,32,128]{2,1,0:T(8,128)(2,1)} %param.6), channel_id=1, source_target_pairs={{0,192},{64,0},{128,64},{192,128},{1,193},{65,1},{129,65},{193,129... | collective-permute-start | bytes 393224 | tf_op jit(solution)/shard_map/ppermute | solution.py:44
  28.1 21.5 %all-to-all-start = ((s32[64,1,24]{2,1,0:T(1,128)}), s32[64,1,24]{2,1,0:T(1,128)S(1)}, u32[]{:S(2)}, u32[]{:S(2)}) async-start(s32[64,1,24]{2,1,0:T(1,128)} %bitcast.8), calls=%async_computation | async-start | bytes 65536 | tf_op jit(solution)/shard_map/all_to_all | solution.py:50
  56.1 23.9 %copy-start.2 = (bf16[768,128]{1,0:T(8,128)(2,1)S(1)}, bf16[768,128]{1,0:T(8,128)(2,1)}, u32[]{:S(2)}) copy-start(bf16[768,128]{1,0:T(8,128)(2,1)} %param.7) | copy-start | bytes 589828
  116.0 18.7 %all-to-all-start.1 = ((f32[64,1,896]{2,1,0:T(1,128)}), f32[64,1,896]{2,1,0:T(1,128)S(1)}, u32[]{:S(2)}, u32[]{:S(2)}) async-start(f32[64,1,896]{2,1,0:T(1,128)} %all_to_all.16), calls=%async_computation.1 | async-start | bytes 458752 | tf_op jit(solution)/shard_map/all_to_all | solution.py:93
  136.0 4.5 %collective-permute-start.4 = (f32[272,32]{0,1:T(8,128)S(1)}, f32[272,32]{0,1:T(8,128)S(1)}, u32[]{:S(2)}, u32[]{:S(2)}) collective-permute-start(f32[272,32]{0,1:T(8,128)S(1)} %pad_maximum_fusion.2), channel_id=1, source_target_pairs={{0,2},{1,3},{2,0},{3,1},{4,6},{5,7},{6,4},{7,5},{8,10},{9,11},{10,... | collective-permute-start | bytes 104456 | tf_op jit(solution)/shard_map/ppermute | solution.py:82
  138.7 3.1 %collective-permute-start.5 = (f32[272,32]{0,1:T(8,128)S(1)}, f32[272,32]{0,1:T(8,128)S(1)}, u32[]{:S(2)}, u32[]{:S(2)}) collective-permute-start(f32[272,32]{0,1:T(8,128)S(1)} %pad_maximum_fusion.2), channel_id=1, source_target_pairs={{0,3},{1,0},{2,1},{3,2},{4,7},{5,4},{6,5},{7,6},{8,11},{9,8},{10,9... | collective-permute-start | bytes 104456 | tf_op jit(solution)/shard_map/ppermute | solution.py:82
  139.6 4.2 %collective-permute-start.3 = (f32[272,32]{0,1:T(8,128)S(1)}, f32[272,32]{0,1:T(8,128)S(1)}, u32[]{:S(2)}, u32[]{:S(2)}) collective-permute-start(f32[272,32]{0,1:T(8,128)S(1)} %pad_maximum_fusion.2), channel_id=1, source_target_pairs={{0,1},{1,2},{2,3},{3,0},{4,5},{5,6},{6,7},{7,4},{8,9},{9,10},{10,1... | collective-permute-start | bytes 104456 | tf_op jit(solution)/shard_map/ppermute | solution.py:82
Sparse Core Ops, SparseCore 0:
  20.5 59.4 all-gather.1

commit v16 on v15

--- a/solution.py
+++ b/solution.py
@@ -51,16 +51,6 @@
         shard_total, capacity, 2
     )
 
-    flattened = query_block.reshape(-1, feature_width)
-    scored = jnp.einsum("rd,cd->rc", flattened, centroids, preferred_element_type=jnp.float32)
-    by_shift = jnp.max(scored, axis=1).reshape(rest_total, y_total, query_count, query_tokens)
-    shift_of_y = (my_y - jnp.arange(y_total, dtype=jnp.int32)) % y_total
-    local_best = (
-        jnp.take(by_shift, shift_of_y, axis=1)
-        .transpose(1, 0, 2, 3)
-        .reshape(shard_total, query_count, query_tokens)
-    )
-
     slot_table = jnp.maximum(mine[..., 0], 0).reshape(-1)
     global_query = jnp.maximum(mine[..., 1], 0).reshape(-1)
     source_shard = global_query // query_count
@@ -74,6 +64,17 @@
     valid_tokens = token_index[None, :] < jnp.take(lengths, slot_table, axis=0)[:, None]
     pair_scored = jnp.where(valid_tokens[:, None, :], pair_scored, masked_score)
     partial_value = jnp.max(pair_scored, axis=2)
+
+    ordered_block, partial_value = lax.optimization_barrier((query_block, partial_value))
+    flattened = ordered_block.reshape(-1, feature_width)
+    scored = jnp.einsum("rd,cd->rc", flattened, centroids, preferred_element_type=jnp.float32)
+    by_shift = jnp.max(scored, axis=1).reshape(rest_total, y_total, query_count, query_tokens)
+    shift_of_y = (my_y - jnp.arange(y_total, dtype=jnp.int32)) % y_total
+    local_best = (
+        jnp.take(by_shift, shift_of_y, axis=1)
+        .transpose(1, 0, 2, 3)
+        .reshape(shard_total, query_count, query_tokens)
+    )
 
     cent_total = lax.axis_size("cent")
 

time: 153 us -> 150 us (0.980)
  matrix products: 25.5 us -> 22.6 us
  waiting for transfers between devices: 48.1 us -> 46.1 us
    dot_general x1, matrix products: 17.2 us -> 13.7 us  [per_device(): jnp.einsum('rd,cd->rc', flattened, centroids, preferred_element_type=jnp....]
  transfers between devices with their start and end apart: 9 -> 9, of which waited for: 7 -> 7; matrix products, arithmetic and copies ran while one was open for 12% -> 13% of each run, Pallas kernels for 0% -> 0%
where the time goes in v16:
time: 150 us; the launch traced here: 149 us
  waiting for transfers between devices  46.1 us (31%)
  starting transfers between devices  30.8 us (21%)
  local copies, waits for them, and re-layouts  30.5 us (20%)
  matrix products  22.6 us (15%)
  between operations  14.4 us (10%)
  other arithmetic  4.7 us (3%)
    all_gather x1, waiting for transfers between devices, per_device(): lax.all_gather(jnp.concatenate(along_y, axis=0), 'rest', axis=0, tiled=True)  19.1 us
    dot_general x1, matrix products, per_device(): jnp.einsum('rd,cd->rc', flattened, centroids, preferred_element_type=jnp....  13.7 us
    all_to_all x1, starting transfers between devices, per_device(): lax.all_to_all(table, shard, split_axis=0, concat_axis=0, tiled=True)  12.6 us
    all_to_all x1, waiting for transfers between devices, per_device(): lax.all_to_all(outgoing, shard, split_axis=0, concat_axis=0, tiled=True)  11.1 us
    all_to_all x1, waiting for transfers between devices, per_device(): lax.all_to_all(table, shard, split_axis=0, concat_axis=0, tiled=True)  9.02 us
    dot_general x1, matrix products, per_device(): jnp.einsum('ntd,npd->ntp', asked, chosen, preferred_element_type=jnp.floa...  8.89 us
    gather x1, local copies, waits for them, and re-layouts, per_device(): asked = jnp.take(query_block, query_table, axis=0)  8.29 us
    all_to_all x1, starting transfers between devices, per_device(): lax.all_to_all(outgoing, shard, split_axis=0, concat_axis=0, tiled=True)  7.55 us
  transfers between devices with their start and end apart: 9, of which 7 were waited for; matrix products, arithmetic and copies ran while one was open for 13% of the time, Pallas kernels for 0%

profile of v16, /device:TPU:1, one launch (start us, length us, event | category | flops | bytes accessed | tf_op | source)
XLA Modules:
  0.0 149.1 jit_solution(15738734603783913013)
XLA Ops:
  7.2 2.2 %collective-permute-start = (bf16[16,32,128]{2,1,0:T(8,128)(2,1)}, bf16[16,32,128]{2,1,0:T(8,128)(2,1)S(1)}, u32[]{:S(2)}, u32[]{:S(2)}) collective-permute-start(bf16[16,32,128]{2,1,0:T(8,128)(2,1)} %param.6), channel_id=1, source_target_pairs={{0,64},{64,128},{128,192},{192,0},{1,65},{65,129},{129,193},{193,1... | collective-permute-start | bytes 393224 | tf_op jit(solution)/shard_map/ppermute | solution.py:44
  9.4 2.6 %collective-permute-start.1 = (bf16[16,32,128]{2,1,0:T(8,128)(2,1)}, bf16[16,32,128]{2,1,0:T(8,128)(2,1)S(1)}, u32[]{:S(2)}, u32[]{:S(2)}) collective-permute-start(bf16[16,32,128]{2,1,0:T(8,128)(2,1)} %param.6), channel_id=1, source_target_pairs={{0,128},{64,192},{128,0},{192,64},{1,129},{65,193},{129,1},{193,65... | collective-permute-start | bytes 393224 | tf_op jit(solution)/shard_map/ppermute | solution.py:44
  12.0 1.1 collective-permute-start.2
  13.4 4.5 %collective-permute-done.1 = bf16[16,32,128]{2,1,0:T(8,128)(2,1)S(1)} collective-permute-done((bf16[16,32,128]{2,1,0:T(8,128)(2,1)}, bf16[16,32,128]{2,1,0:T(8,128)(2,1)S(1)}, u32[]{:S(2)}, u32[]{:S(2)}) %collective-permute-start.1) | collective-permute-done | bytes 131104 | tf_op jit(solution)/shard_map/ppermute | solution.py:44
  18.0 1.8 %pad_maximum_fusion = bf16[64,32,128]{2,1,0:T(8,128)(2,1)} fusion(bf16[16,32,128]{2,1,0:T(8,128)(2,1)S(1)} %collective-permute-done.2, bf16[16,32,128]{2,1,0:T(8,128)(2,1)S(1)} %collective-permute-done.1, bf16[16,32,128]{2,1,0:T(8,128)(2,1)S(1)} %collective-permute-done, bf16[16,32,128]{2,1,0:T(8,128)(2,1)} %param.6), kind=kLoop, calls=%fused_computation.15 | loop fusion | flops 786432 | bytes 1048576 | tf_op jit(solution)/shard_map/concatenate | solution.py:48
  19.8 0.8 reshape.578
  22.2 2.1 %gather_fusion = s32[256]{0:T(256)S(1)} fusion(s32[16384]{0:T(1024)} %param.10, s32[1024]{0:T(1024)S(1)} %pad_clamp_fusion.4), kind=kCustom, calls=%fused_computation | custom fusion | bytes 3072 | tf_op jit(solution)/shard_map/jit(_take)/gather | solution.py:24
  25.4 1.2 scatter_custom_fusion
  27.5 12.6 %all-to-all-start = ((s32[64,1,24]{2,1,0:T(1,128)}), s32[64,1,24]{2,1,0:T(1,128)S(1)}, u32[]{:S(2)}, u32[]{:S(2)}) async-start(s32[64,1,24]{2,1,0:T(1,128)} %bitcast.6), calls=%async_computation | async-start | bytes 65536 | tf_op jit(solution)/shard_map/all_to_all | solution.py:50
  40.6 9.0 %all-to-all-done = s32[64,1,24]{2,1,0:T(1,128)S(1)} async-done(((s32[64,1,24]{2,1,0:T(1,128)}), s32[64,1,24]{2,1,0:T(1,128)S(1)}, u32[]{:S(2)}, u32[]{:S(2)}) %all-to-all-start) | async-done | bytes 6176 | tf_op jit(solution)/shard_map/all_to_all | solution.py:50
  51.2 5.0 %gather_fusion.1 = s32[768]{0:T(1024)S(1)} fusion(s32[256]{0:T(256)S(1)} %copy-done.1, s32[1024]{0:T(1024)S(1)} %pad_clamp_fusion.3), kind=kCustom, calls=%fused_computation.1 | custom fusion | bytes 9216 | tf_op jit(solution)/shard_map/jit(_take)/gather | solution.py:64
  56.2 4.5 %gather_fusion.3 = bf16[768,32,128]{2,1,0:T(8,128)(2,1)} fusion(bf16[256,32,128]{2,1,0:T(8,128)(2,1)S(1)} %copy-done, s32[1024]{0:T(1024)S(1)} %pad_clamp_fusion.3), kind=kCustom, calls=%fused_computation.3 | custom fusion | bytes 12585984 | tf_op jit(solution)/shard_map/jit(_take)/gather | solution.py:61
  61.0 19.1 %all-gather.2.cloned.1.call-done = bf16[1024,32,128]{2,1,0:T(8,128)(2,1)} async-done(((bf16[64,32,128]{2,1,0:T(8,128)(2,1)}), bf16[1024,32,128]{2,1,0:T(8,128)(2,1)}) %all-gather.2.cloned.1.call-update) | async-done | bytes 8388624 | tf_op jit(solution)/shard_map/all_gather | solution.py:47
  80.1 8.3 %gather_fusion.2 = bf16[768,32,128]{2,1,0:T(8,128)(2,1)} fusion(bf16[1024,32,128]{2,1,0:T(8,128)(2,1)} %all-gather.2.cloned.1.call-done, s32[1024]{0:T(1024)S(1)} %pad_clamp_fusion.2), kind=kCustom, calls=%fused_computation.2 | custom fusion | bytes 12585984 | tf_op jit(solution)/shard_map/jit(_take)/gather | solution.py:60
  88.4 8.9 %select_reduce_fusion = f32[768,32]{1,0:T(8,128)S(1)} fusion(pred[768,32]{1,0:T(8,128)(4,1)S(1)} %broadcast_compare_fusion, bf16[768,32,128]{2,1,0:T(8,128)(2,1)} %gather_fusion.3, pred[768]{0:T(1024)(128)(4,1)S(1)} %le.96, bf16[768,32,128]{2,1,0:T(8,128)(2,1)} %gather_fusion.2, pred[768]{0:T(1024)(128)(4,1)S(1)} %compare_and_fusion), kind=kOutput, calls=%fused_computation.8 | convolution fusion | flops 209166336 | bytes 12707328 | tf_op jit(solution)/shard_map/ntd,npd->ntp/dot_general | solution.py:62
  97.3 13.7 %convolution_reduce_fusion = f32[32768]{0:T(1024)S(1)} fusion(bf16[32768,128]{1,0:T(8,128)(2,1)S(1)} %bitcast.55, bf16[768,128]{1,0:T(8,128)(2,1)S(1)} %copy-done.5), kind=kOutput, calls=%fused_computation.7 | convolution fusion | flops 6467584000 | bytes 8716288 | tf_op jit(solution)/shard_map/rd,cd->rc/dot_general | solution.py:70
  113.0 0.8 all_to_all.16
  113.8 7.5 %all-to-all-start.1 = ((f32[64,1,896]{2,1,0:T(1,128)}), f32[64,1,896]{2,1,0:T(1,128)S(1)}, u32[]{:S(2)}, u32[]{:S(2)}) async-start(f32[64,1,896]{2,1,0:T(1,128)} %all_to_all.16), calls=%async_computation.1 | async-start | bytes 458752 | tf_op jit(solution)/shard_map/all_to_all | solution.py:94
  121.4 11.1 %all-to-all-done.1 = f32[64,1,896]{2,1,0:T(1,128)S(1)} async-done(((f32[64,1,896]{2,1,0:T(1,128)}), f32[64,1,896]{2,1,0:T(1,128)S(1)}, u32[]{:S(2)}, u32[]{:S(2)}) %all-to-all-start.1) | async-done | bytes 229408 | tf_op jit(solution)/shard_map/all_to_all | solution.py:94
  133.8 1.2 collective-permute-start.3
  135.0 2.4 %collective-permute-start.4 = (f32[272,32]{0,1:T(8,128)S(1)}, f32[272,32]{0,1:T(8,128)S(1)}, u32[]{:S(2)}, u32[]{:S(2)}) collective-permute-start(f32[272,32]{0,1:T(8,128)S(1)} %pad_maximum_fusion.2), channel_id=1, source_target_pairs={{0,2},{1,3},{2,0},{3,1},{4,6},{5,7},{6,4},{7,5},{8,10},{9,11},{10,... | collective-permute-start | bytes 104456 | tf_op jit(solution)/shard_map/ppermute | solution.py:83
  137.4 1.2 collective-permute-start.5
  138.6 1.1 collective-permute-done.4
  139.7 1.0 collective-permute-done.5
  (84 shorter events, 11.0 us)
Async XLA Ops:
  7.2 49.0 %copy-start = (bf16[256,32,128]{2,1,0:T(8,128)(2,1)S(1)}, bf16[256,32,128]{2,1,0:T(8,128)(2,1)}, u32[]{:S(2)}) copy-start(bf16[256,32,128]{2,1,0:T(8,128)(2,1)} %param.8) | copy-start | bytes 6291460
  7.2 44.0 %copy-start.1 = (s32[256]{0:T(256)S(1)}, s32[256]{0:T(256)}, u32[]{:S(2)}) copy-start(s32[256]{0:T(256)} %param.9) | copy-start | bytes 3076
  7.2 72.9 %all-gather.2.cloned.1.call-start = ((), (), s32[]{:S(2)}) async-start(), calls=%async_computation.2 | async-start | bytes 8912896 | tf_op jit(solution)/shard_map/all_gather | solution.py:47
  7.2 6.2 %collective-permute-start = (bf16[16,32,128]{2,1,0:T(8,128)(2,1)}, bf16[16,32,128]{2,1,0:T(8,128)(2,1)S(1)}, u32[]{:S(2)}, u32[]{:S(2)}) collective-permute-start(bf16[16,32,128]{2,1,0:T(8,128)(2,1)} %param.6), channel_id=1, source_target_pairs={{0,64},{64,128},{128,192},{192,0},{1,65},{65,129},{129,193},{193,1... | collective-permute-start | bytes 393224 | tf_op jit(solution)/shard_map/ppermute | solution.py:44
  9.4 8.6 %collective-permute-start.1 = (bf16[16,32,128]{2,1,0:T(8,128)(2,1)}, bf16[16,32,128]{2,1,0:T(8,128)(2,1)S(1)}, u32[]{:S(2)}, u32[]{:S(2)}) collective-permute-start(bf16[16,32,128]{2,1,0:T(8,128)(2,1)} %param.6), channel_id=1, source_target_pairs={{0,128},{64,192},{128,0},{192,64},{1,129},{65,193},{129,1},{193,65... | collective-permute-start | bytes 393224 | tf_op jit(solution)/shard_map/ppermute | solution.py:44
  12.0 5.9 %collective-permute-start.2 = (bf16[16,32,128]{2,1,0:T(8,128)(2,1)}, bf16[16,32,128]{2,1,0:T(8,128)(2,1)S(1)}, u32[]{:S(2)}, u32[]{:S(2)}) collective-permute-start(bf16[16,32,128]{2,1,0:T(8,128)(2,1)} %param.6), channel_id=1, source_target_pairs={{0,192},{64,0},{128,64},{192,128},{1,193},{65,1},{129,65},{193,129... | collective-permute-start | bytes 393224 | tf_op jit(solution)/shard_map/ppermute | solution.py:44
  25.4 35.3 %copy-start.3 = (s32[256,1]{0,1:T(1,128)}, s32[256,1]{0,1:T(1,128)S(1)}, u32[]{:S(2)}) copy-start(s32[256,1]{0,1:T(1,128)S(1)} %compare_select_fusion.7) | copy-start | bytes 3076
  27.5 22.2 %all-to-all-start = ((s32[64,1,24]{2,1,0:T(1,128)}), s32[64,1,24]{2,1,0:T(1,128)S(1)}, u32[]{:S(2)}, u32[]{:S(2)}) async-start(s32[64,1,24]{2,1,0:T(1,128)} %bitcast.6), calls=%async_computation | async-start | bytes 65536 | tf_op jit(solution)/shard_map/all_to_all | solution.py:50
  88.4 8.9 %copy-start.2 = (bf16[1024,32,128]{2,1,0:T(8,128)(2,1)S(1)}, bf16[1024,32,128]{2,1,0:T(8,128)(2,1)}, u32[]{:S(2)}) copy-start(bf16[1024,32,128]{2,1,0:T(8,128)(2,1)} %all-gather.2.cloned.1.call-done) | copy-start | bytes 25165828
  88.4 8.9 %copy-start.5 = (bf16[768,128]{1,0:T(8,128)(2,1)S(1)}, bf16[768,128]{1,0:T(8,128)(2,1)}, u32[]{:S(2)}) copy-start(bf16[768,128]{1,0:T(8,128)(2,1)} %param.7) | copy-start | bytes 589828
  97.3 24.0 %copy-start.4 = (s32[256,1]{0,1:T(1,128)S(1)}, s32[256,1]{0,1:T(1,128)}, u32[]{:S(2)}) copy-start(s32[256,1]{0,1:T(1,128)} %copy-done.3) | copy-start | bytes 3076
  113.8 18.7 %all-to-all-start.1 = ((f32[64,1,896]{2,1,0:T(1,128)}), f32[64,1,896]{2,1,0:T(1,128)S(1)}, u32[]{:S(2)}, u32[]{:S(2)}) async-start(f32[64,1,896]{2,1,0:T(1,128)} %all_to_all.16), calls=%async_computation.1 | async-start | bytes 458752 | tf_op jit(solution)/shard_map/all_to_all | solution.py:94
  133.8 4.8 %collective-permute-start.3 = (f32[272,32]{0,1:T(8,128)S(1)}, f32[272,32]{0,1:T(8,128)S(1)}, u32[]{:S(2)}, u32[]{:S(2)}) collective-permute-start(f32[272,32]{0,1:T(8,128)S(1)} %pad_maximum_fusion.2), channel_id=1, source_target_pairs={{0,1},{1,2},{2,3},{3,0},{4,5},{5,6},{6,7},{7,4},{8,9},{9,10},{10,1... | collective-permute-start | bytes 104456 | tf_op jit(solution)/shard_map/ppermute | solution.py:83
  135.0 4.7 %collective-permute-start.4 = (f32[272,32]{0,1:T(8,128)S(1)}, f32[272,32]{0,1:T(8,128)S(1)}, u32[]{:S(2)}, u32[]{:S(2)}) collective-permute-start(f32[272,32]{0,1:T(8,128)S(1)} %pad_maximum_fusion.2), channel_id=1, source_target_pairs={{0,2},{1,3},{2,0},{3,1},{4,6},{5,7},{6,4},{7,5},{8,10},{9,11},{10,... | collective-permute-start | bytes 104456 | tf_op jit(solution)/shard_map/ppermute | solution.py:83
  137.4 3.2 %collective-permute-start.5 = (f32[272,32]{0,1:T(8,128)S(1)}, f32[272,32]{0,1:T(8,128)S(1)}, u32[]{:S(2)}, u32[]{:S(2)}) collective-permute-start(f32[272,32]{0,1:T(8,128)S(1)} %pad_maximum_fusion.2), channel_id=1, source_target_pairs={{0,3},{1,0},{2,1},{3,2},{4,7},{5,4},{6,5},{7,6},{8,11},{9,8},{10,9... | collective-permute-start | bytes 104456 | tf_op jit(solution)/shard_map/ppermute | solution.py:83
Sparse Core Ops, SparseCore 0:
  19.9 60.1 all-gather.1
